TPU v7x, 256 devices: a whole 4x4x8 slice. The times are simulated.
256 devices in a mesh: row: 8 (over x, core), col: 32 (over y, z).
Axes of the slice: x: 4, y: 4, z: 8, core: 2. Of those that a mesh axis runs over, the one named last changes fastest.
Arguments:
- tokens: bfloat16 [1024, 6144], P('col', 'row'), may hold values from -6 to 6
- w_up: bfloat16 [6144, 24576], P('row', 'col'), may hold values from -0.078125 to 0.078125
- w_down: bfloat16 [24576, 6144], P('col', 'row'), may hold values from -0.0390625 to 0.0390625
- expert_in: bfloat16 [6144, 8192], P(None, 'col'), may hold values from -0.078125 to 0.078125
- expert_out: bfloat16 [8192, 6144], P('col'), may hold values from -0.125 to 0.125
- expert_ids: int32 [1024, 2], P('col'), may hold values from 0 to 3, as said below
- route_weights: bfloat16 [1024, 2], P('col'), may hold values from 0.25 to 1
- out_grad: bfloat16 [1024, 6144], P('col', 'row'), may hold values from -6 to 6
Outputs:
- layer_out: bfloat16 [1024, 6144], P('col', 'row')
- tokens_grad: bfloat16 [1024, 6144], P('col', 'row')
- up_grad: bfloat16 [6144, 24576], P('row', 'col')
- down_grad: bfloat16 [24576, 6144], P('col', 'row')
- expert_in_grad: bfloat16 [6144, 8192], P('row', 'col')
- expert_out_grad: bfloat16 [8192, 6144], P('col', 'row')
Inputs may be any that keep to these rules, and one draw needn't show every extreme that they name: `expert_ids`: the two experts of a token differ. In every aligned block of 4 tokens no expert is named by more than 3 of the block's pairs; one expert is named by exactly 3 pairs, the same expert in all blocks whose index leaves the same remainder modulo 32 // 4; the other experts' counts in a block differ by at most one. Every expert is named somewhere.
All inputs are finite; a program needn't handle non-finite values.
Results may differ from a plain program's by a relative error of at most 0.025.
Values may be sent and summed in bfloat16 or wider, within the bound.
No kernel may reach another device: no remote copies, remote signals or barrier semaphores. Data moves between devices by JAX's collectives and lax.ppermute only.
A program may use at most 128 MiB of HBM per device.

v0:
```python
import jax
import jax.numpy as jnp
from jax import lax
from jax.sharding import PartitionSpec as P

EXPERTS = 4


gelu_scale = 0.7978845608028654
gelu_cubic = 0.044715


def gelu_tanh(value):
    return 0.5 * value * (1.0 + jnp.tanh(gelu_scale * (value + gelu_cubic * value * value * value)))


def gelu_slope(value):
    inner = jnp.tanh(gelu_scale * (value + gelu_cubic * value * value * value))
    return 0.5 * (1.0 + inner) + 0.5 * value * (1.0 - inner * inner) * gelu_scale * (
        1.0 + 3.0 * gelu_cubic * value * value
    )


def slot_ranks(pairs):
    count = pairs.shape[-1]
    positions = jnp.arange(count, dtype=jnp.int32)
    earlier = positions[:, None] > positions[None, :]
    matching = pairs[..., :, None] == pairs[..., None, :]
    return jnp.sum((matching & earlier).astype(jnp.int32), axis=-1)


def on_device(tokens, w_up, w_down, expert_in, expert_out, expert_ids, route_weights, out_grad):
    row_count = lax.axis_size("row")
    col_count = lax.axis_size("col")
    tok_col = tokens.shape[0]
    block_len = tok_col // row_count
    group_len = col_count // EXPERTS
    slot_cap = max(2, 3 * block_len // 4)
    model_width = expert_out.shape[1]
    my_row = lax.axis_index("row")
    tok_panel = lax.all_gather(tokens, "col", axis=0, tiled=True)
    up_terms = jnp.dot(tok_panel, w_up, preferred_element_type=jnp.float32)
    preact = lax.psum_scatter(
        up_terms.astype(jnp.bfloat16), "row", scatter_dimension=0, tiled=True
    ).astype(jnp.float32)
    hidden_full = lax.all_gather(gelu_tanh(preact).astype(jnp.bfloat16), "row", axis=0, tiled=True)
    rows_in = hidden_full
    dense_term = lax.psum_scatter(
        jnp.dot(rows_in, w_down, preferred_element_type=jnp.float32).astype(jnp.bfloat16),
        "col",
        scatter_dimension=0,
        tiled=True,
    ).astype(jnp.float32)
    mixed_act = (tokens.astype(jnp.float32) + dense_term).astype(jnp.bfloat16)
    own_rows, own_grad = (
        lax.all_to_all(mixed_act, "row", split_axis=0, concat_axis=1, tiled=True),
        lax.all_to_all(out_grad, "row", split_axis=0, concat_axis=1, tiled=True),
    )
    chosen = lax.dynamic_slice_in_dim(expert_ids, my_row * block_len, block_len, 0).reshape(-1)
    weights_own = lax.dynamic_slice_in_dim(route_weights, my_row * block_len, block_len, 0)
    weights_flat = weights_own.reshape(-1).astype(jnp.float32)
    rows_x = jnp.repeat(own_rows, 2, axis=0)
    scaled = (weights_flat[:, None] * jnp.repeat(own_grad, 2, axis=0).astype(jnp.float32)).astype(
        jnp.bfloat16
    )
    slot_range = jnp.arange(slot_cap, dtype=jnp.int32)
    placed = slot_ranks(chosen)
    expert_range = jnp.arange(EXPERTS, dtype=jnp.int32)
    onehot = (
        (chosen[None, None, :] == expert_range[:, None, None])
        & (placed[None, None, :] == slot_range[None, :, None])
    ).astype(jnp.bfloat16)
    send_x = jnp.einsum("eca,ad->ecd", onehot, rows_x, preferred_element_type=jnp.float32).astype(
        jnp.bfloat16
    )
    send_g = jnp.einsum("eca,ad->ecd", onehot, scaled, preferred_element_type=jnp.float32).astype(
        jnp.bfloat16
    )
    send_x = jnp.repeat(send_x, group_len, axis=0)
    send_g = jnp.repeat(send_g, group_len, axis=0)
    got_x, got_g = (
        lax.all_to_all(send_x, "col", split_axis=0, concat_axis=0, tiled=True),
        lax.all_to_all(send_g, "col", split_axis=0, concat_axis=0, tiled=True),
    )
    inputs = got_x.reshape(-1, model_width)
    grads = got_g.reshape(-1, model_width)
    e_pre = jnp.dot(inputs, expert_in, preferred_element_type=jnp.float32)
    e_hidden = gelu_tanh(e_pre).astype(jnp.bfloat16)
    values = jnp.dot(e_hidden, expert_out, preferred_element_type=jnp.float32)
    e_dpre = (
        jnp.dot(grads, expert_out.T, preferred_element_type=jnp.float32) * gelu_slope(e_pre)
    ).astype(jnp.bfloat16)
    returns = jnp.dot(e_dpre, expert_in.T, preferred_element_type=jnp.float32)
    grad_in = jnp.dot(inputs.T, e_dpre, preferred_element_type=jnp.float32)
    grad_out = jnp.dot(e_hidden.T, grads, preferred_element_type=jnp.float32)
    values, returns, grad_in, grad_out = (values, returns, grad_in, grad_out)
    back_v, back_d = (
        lax.all_to_all(
            values.reshape(col_count, slot_cap, model_width).astype(jnp.bfloat16),
            "col",
            split_axis=0,
            concat_axis=0,
            tiled=True,
        ).astype(jnp.float32),
        lax.all_to_all(
            returns.reshape(col_count, slot_cap, model_width).astype(jnp.bfloat16),
            "col",
            split_axis=0,
            concat_axis=0,
            tiled=True,
        ).astype(jnp.float32),
    )
    flat_v = (
        back_v.reshape(EXPERTS, group_len, slot_cap, model_width)
        .sum(axis=1)
        .reshape(EXPERTS * slot_cap, model_width)
    )
    flat_d = (
        back_d.reshape(EXPERTS, group_len, slot_cap, model_width)
        .sum(axis=1)
        .reshape(EXPERTS * slot_cap, model_width)
    )
    lookup = chosen * slot_cap + placed
    moe_sum = (
        (weights_flat[:, None] * jnp.take(flat_v, lookup, axis=0))
        .reshape(block_len, 2, model_width)
        .sum(axis=1)
    )
    grad_sum = jnp.take(flat_d, lookup, axis=0).reshape(block_len, 2, model_width).sum(axis=1)
    layer_rows = (own_rows.astype(jnp.float32) + moe_sum).astype(jnp.bfloat16)
    grad_rows = (own_grad.astype(jnp.float32) + grad_sum).astype(jnp.bfloat16)
    layer_out, mixed_grad = (
        lax.all_to_all(layer_rows, "row", split_axis=1, concat_axis=0, tiled=True),
        lax.all_to_all(grad_rows, "row", split_axis=1, concat_axis=0, tiled=True),
    )
    expert_in_grad = lax.psum_scatter(
        grad_in.astype(jnp.bfloat16), "row", scatter_dimension=0, tiled=True
    )
    expert_out_grad = lax.psum_scatter(
        grad_out.astype(jnp.bfloat16), "row", scatter_dimension=1, tiled=True
    )
    cot_panel = lax.all_gather(mixed_grad, "col", axis=0, tiled=True)
    hgrad_terms = jnp.dot(cot_panel, w_down.T, preferred_element_type=jnp.float32)
    down_grad = jnp.dot(hidden_full.T, cot_panel, preferred_element_type=jnp.float32).astype(
        jnp.bfloat16
    )
    hidden_grad = lax.psum_scatter(
        hgrad_terms.astype(jnp.bfloat16), "row", scatter_dimension=0, tiled=True
    ).astype(jnp.float32)
    dpre_full = lax.all_gather(
        (hidden_grad * gelu_slope(preact)).astype(jnp.bfloat16), "row", axis=0, tiled=True
    )
    up_grad = jnp.dot(tok_panel.T, dpre_full, preferred_element_type=jnp.float32).astype(
        jnp.bfloat16
    )
    rows_in = dpre_full
    input_term = lax.psum_scatter(
        jnp.dot(rows_in, w_up.T, preferred_element_type=jnp.float32).astype(jnp.bfloat16),
        "col",
        scatter_dimension=0,
        tiled=True,
    ).astype(jnp.float32)
    tokens_grad = (mixed_grad.astype(jnp.float32) + input_term).astype(jnp.bfloat16)
    return (layer_out, tokens_grad, up_grad, down_grad, expert_in_grad, expert_out_grad)


def solution(mesh):
    in_specs = (
        P("col", "row"),
        P("row", "col"),
        P("col", "row"),
        P(None, "col"),
        P("col", None),
        P("col", None),
        P("col", None),
        P("col", "row"),
    )
    out_specs = (
        P("col", "row"),
        P("col", "row"),
        P("row", "col"),
        P("col", "row"),
        P("row", "col"),
        P("col", "row"),
    )
    return jax.shard_map(
        on_device, mesh=mesh, in_specs=in_specs, out_specs=out_specs, check_vma=False
    )
```

profile of v0, /device:TPU:32, one launch (start us, length us, event | category | flops | bytes accessed | tf_op | source)
XLA Modules:
  0.0 1058.4 jit_solution(8834172341026235586)
XLA Ops:
  8.0 81.4 %all-gather.5.cloned.1.call-done = bf16[1024,768]{1,0:T(8,128)(2,1)} async-done(((bf16[32,768]{1,0:T(8,128)(2,1)}), bf16[1024,768]{1,0:T(8,128)(2,1)}) %all-gather.5.cloned.1.call-update) | async-done | bytes 1572880 | tf_op jit(solution)/shard_map/all_gather | solution.py:41
  89.3 4.3 convolution_convert_fusion.9
  93.7 33.9 %reduce-scatter.7.cloned.1.call-done = bf16[128,768]{1,0:T(8,128)(2,1)} async-done(((bf16[1024,768]{1,0:T(8,128)(2,1)}), bf16[128,768]{1,0:T(8,128)(2,1)}) %reduce-scatter.7.cloned.1.call-update) | async-done | bytes 196624 | tf_op jit(solution)/shard_map/reduce_scatter | solution.py:43
  127.6 1.7 fusion.4
  129.5 26.2 %all-gather.7.cloned.1.call-done = bf16[1024,768]{1,0:T(8,128)(2,1)} async-done(((bf16[128,768]{1,0:T(8,128)(2,1)}), bf16[1024,768]{1,0:T(8,128)(2,1)}) %all-gather.7.cloned.1.call-update) | async-done | bytes 1572880 | tf_op jit(solution)/shard_map/all_gather | solution.py:46
  155.7 4.3 convolution_convert_fusion.8
  161.5 3.3 all-to-all-start.4
  166.0 4.2 all-to-all-done.4
  171.1 207.2 %reduce-scatter.9.cloned.1.call-done = bf16[32,768]{1,0:T(8,128)(2,1)} async-done(((bf16[1024,768]{1,0:T(8,128)(2,1)}), bf16[32,768]{1,0:T(8,128)(2,1)}) %reduce-scatter.9.cloned.1.call-update) | async-done | bytes 49168 | tf_op jit(solution)/shard_map/reduce_scatter | solution.py:48
  379.8 4.3 all-to-all-start
  384.5 5.2 all-to-all-done
  389.7 1.9 broadcast_in_dim.31
  391.6 8.0 all-to-all-start.5
  400.8 37.9 %all-to-all-done.5 = bf16[32,3,6144]{2,1,0:T(4,128)(2,1)} async-done(((bf16[32,3,6144]{2,1,0:T(4,128)(2,1)}), bf16[32,3,6144]{2,1,0:T(4,128)(2,1)}, u32[]{:S(2)}, u32[]{:S(2)}) %all-to-all-start.5) | async-done | bytes 1179680 | tf_op jit(solution)/shard_map/all_to_all | solution.py:83
  438.7 1.9 broadcast_in_dim.29
  440.6 5.8 all-to-all-start.1
  446.4 4.0 reshape.146
  450.3 35.1 %all-to-all-done.1 = bf16[32,3,6144]{2,1,0:T(4,128)(2,1)} async-done(((bf16[32,3,6144]{2,1,0:T(4,128)(2,1)}), bf16[32,3,6144]{2,1,0:T(4,128)(2,1)}, u32[]{:S(2)}, u32[]{:S(2)}) %all-to-all-start.1) | async-done | bytes 1179680 | tf_op jit(solution)/shard_map/all_to_all | solution.py:82
  485.5 3.9 reshape.140
  489.4 2.1 fusion.29
  493.7 2.1 convolution_convert_fusion.2
  495.8 3.8 convert_element_type.155
  499.6 5.5 all-to-all-start.6
  505.1 3.6 convolution_convert_fusion.3
  508.7 3.8 convert_element_type.144
  512.5 31.7 %all-to-all-done.6 = bf16[32,3,6144]{2,1,0:T(4,128)(2,1)} async-done(((bf16[32,3,6144]{2,1,0:T(4,128)(2,1)}), bf16[32,3,6144]{2,1,0:T(4,128)(2,1)}, u32[]{:S(2)}, u32[]{:S(2)}) %all-to-all-start.6) | async-done | bytes 1179680 | tf_op jit(solution)/shard_map/all_to_all | solution.py:105
  544.2 5.5 all-to-all-start.2
  549.9 2.9 convert_reduce_fusion
  554.0 34.7 %all-to-all-done.2 = bf16[32,3,6144]{2,1,0:T(4,128)(2,1)} async-done(((bf16[32,3,6144]{2,1,0:T(4,128)(2,1)}), bf16[32,3,6144]{2,1,0:T(4,128)(2,1)}, u32[]{:S(2)}, u32[]{:S(2)}) %all-to-all-start.2) | async-done | bytes 1179680 | tf_op jit(solution)/shard_map/all_to_all | solution.py:98
  588.8 2.9 convert_reduce_fusion.1
  591.7 1.9 reshape.143
  594.9 2.4 gather_fusion
  601.8 7.9 all_to_all.84
  610.5 71.0 %all-gather.9.cloned.1.call-done = bf16[1024,768]{1,0:T(8,128)(2,1)} async-done(((bf16[32,768]{1,0:T(8,128)(2,1)}), bf16[1024,768]{1,0:T(8,128)(2,1)}) %all-gather.9.cloned.1.call-update) | async-done | bytes 1572880 | tf_op jit(solution)/shard_map/all_gather | solution.py:142
  681.5 4.3 convolution_convert_fusion.7
  685.9 33.9 %reduce-scatter.11.cloned.1.call-done = bf16[128,768]{1,0:T(8,128)(2,1)} async-done(((bf16[1024,768]{1,0:T(8,128)(2,1)}), bf16[128,768]{1,0:T(8,128)(2,1)}) %reduce-scatter.11.cloned.1.call-update) | async-done | bytes 196624 | tf_op jit(solution)/shard_map/reduce_scatter | solution.py:147
  719.8 1.9 fusion.9
  721.8 26.1 %all-gather.11.cloned.1.call-done = bf16[1024,768]{1,0:T(8,128)(2,1)} async-done(((bf16[128,768]{1,0:T(8,128)(2,1)}), bf16[1024,768]{1,0:T(8,128)(2,1)}) %all-gather.11.cloned.1.call-update) | async-done | bytes 1572880 | tf_op jit(solution)/shard_map/all_gather | solution.py:150
  747.9 4.3 convolution_convert_fusion.6
  753.1 3.9 convolution_convert_fusion
  757.8 4.0 convolution_convert_fusion.1
  763.0 8.5 all_to_all.85
  772.2 4.5 convolution_convert_fusion.10
  776.7 2.5 fusion
  779.2 2.4 copy.28
  781.5 188.9 %reduce-scatter.13.cloned.1.call-done = bf16[32,768]{1,0:T(8,128)(2,1)} async-done(((bf16[1024,768]{1,0:T(8,128)(2,1)}), bf16[32,768]{1,0:T(8,128)(2,1)}) %reduce-scatter.13.cloned.1.call-update) | async-done | bytes 49168 | tf_op jit(solution)/shard_map/reduce_scatter | solution.py:157
  971.9 39.4 %reduce-scatter.17.cloned.1.call-done = bf16[256,768]{1,0:T(8,128)(2,1)} async-done(((bf16[256,6144]{1,0:T(8,128)(2,1)}), bf16[256,768]{1,0:T(8,128)(2,1)}) %reduce-scatter.17.cloned.1.call-update) | async-done | bytes 393232 | tf_op jit(solution)/shard_map/reduce_scatter | solution.py:139
  1011.3 40.3 %reduce-scatter.15.cloned.1.call-done = bf16[768,256]{1,0:T(8,128)(2,1)} async-done(((bf16[6144,256]{1,0:T(8,128)(2,1)}), bf16[768,256]{1,0:T(8,128)(2,1)}) %reduce-scatter.15.cloned.1.call-update) | async-done | bytes 393232 | tf_op jit(solution)/shard_map/reduce_scatter | solution.py:136
  (92 shorter events, 22.6 us)
Async XLA Ops:
  7.2 482.3 %copy-start = (bf16[6144,256]{1,0:T(8,128)(2,1)S(1)}, bf16[6144,256]{1,0:T(8,128)(2,1)}, u32[]{:S(2)}) copy-start(bf16[6144,256]{1,0:T(8,128)(2,1)} %param.13) | copy-start | bytes 9437188
  7.2 82.2 %all-gather.5.cloned.1.call-start = ((), (), s32[]{:S(2)}) async-start(), calls=%async_computation.14 | async-start | bytes 1622016 | tf_op jit(solution)/shard_map/all_gather | solution.py:41
  7.9 119.7 %reduce-scatter.7.cloned.1.call-start = ((), (), s32[]{:S(2)}) async-start(), calls=%async_computation.15 | async-start | bytes 1769472 | tf_op jit(solution)/shard_map/reduce_scatter | solution.py:43
  93.7 62.0 %all-gather.7.cloned.1.call-start = ((), (), s32[]{:S(2)}) async-start(), calls=%async_computation.16 | async-start | bytes 1769472 | tf_op jit(solution)/shard_map/all_gather | solution.py:46
  129.4 248.9 %reduce-scatter.9.cloned.1.call-start = ((), (), s32[]{:S(2)}) async-start(), calls=%async_computation.17 | async-start | bytes 1622016 | tf_op jit(solution)/shard_map/reduce_scatter | solution.py:48
  160.0 0.8 copy-start.11
  160.0 4.8 copy-start.12
  160.0 5.8 copy-start.13
  161.5 8.8 all-to-all-start.4
  165.3 0.5 copy-start.14
  170.3 0.6 copy-start.10
  379.8 9.9 all-to-all-start
  391.6 47.1 %all-to-all-start.5 = ((bf16[32,3,6144]{2,1,0:T(4,128)(2,1)}), bf16[32,3,6144]{2,1,0:T(4,128)(2,1)}, u32[]{:S(2)}, u32[]{:S(2)}) async-start(bf16[32,3,6144]{2,1,0:T(4,128)(2,1)} %bitcast.50), calls=%async_computation.7 | async-start | bytes 3145728 | tf_op jit(solution)/shard_map/all_to_all | solution.py:83
  440.6 44.9 %all-to-all-start.1 = ((bf16[32,3,6144]{2,1,0:T(4,128)(2,1)}), bf16[32,3,6144]{2,1,0:T(4,128)(2,1)}, u32[]{:S(2)}, u32[]{:S(2)}) async-start(bf16[32,3,6144]{2,1,0:T(4,128)(2,1)} %bitcast.51), calls=%async_computation.3 | async-start | bytes 3145728 | tf_op jit(solution)/shard_map/all_to_all | solution.py:82
  489.4 2.2 copy-start.1
  489.4 2.6 copy-start.2
  492.0 13.1 %copy-start.3 = (f32[96,256]{1,0:T(8,128)}, f32[96,256]{1,0:T(8,128)S(1)}, u32[]{:S(2)}) copy-start(f32[96,256]{1,0:T(8,128)S(1)} %fusion.29) | copy-start | bytes 294916
  493.1 0.6 copy-start.7
  499.6 44.5 %all-to-all-start.6 = ((bf16[32,3,6144]{2,1,0:T(4,128)(2,1)}), bf16[32,3,6144]{2,1,0:T(4,128)(2,1)}, u32[]{:S(2)}, u32[]{:S(2)}) async-start(bf16[32,3,6144]{2,1,0:T(4,128)(2,1)} %convert_element_type.155), calls=%async_computation.8 | async-start | bytes 3145728 | tf_op jit(solution)/shard_map/all_to_all | solution.py:105
  512.5 37.4 %copy-start.15 = (s32[8]{0:T(128)S(1)}, s32[8]{0:T(128)}, u32[]{:S(2)}) copy-start(s32[8]{0:T(128)} %copy-done.14) | copy-start | bytes 100
  544.2 44.6 %all-to-all-start.2 = ((bf16[32,3,6144]{2,1,0:T(4,128)(2,1)}), bf16[32,3,6144]{2,1,0:T(4,128)(2,1)}, u32[]{:S(2)}, u32[]{:S(2)}) async-start(bf16[32,3,6144]{2,1,0:T(4,128)(2,1)} %convert_element_type.144), calls=%async_computation.4 | async-start | bytes 3145728 | tf_op jit(solution)/shard_map/all_to_all | solution.py:98
  549.7 131.8 %all-gather.9.cloned.1.call-start = ((), (), s32[]{:S(2)}) async-start(), calls=%async_computation.18 | async-start | bytes 1622016 | tf_op jit(solution)/shard_map/all_gather | solution.py:142
  594.9 2.4 copy-start.6
  610.4 109.4 %reduce-scatter.11.cloned.1.call-start = ((), (), s32[]{:S(2)}) async-start(), calls=%async_computation.19 | async-start | bytes 1769472 | tf_op jit(solution)/shard_map/reduce_scatter | solution.py:147
  685.8 34.0 %copy-start.5 = (bf16[128,768]{1,0:T(8,128)(2,1)S(1)}, bf16[128,768]{1,0:T(8,128)(2,1)}, u32[]{:S(2)}) copy-start(bf16[128,768]{1,0:T(8,128)(2,1)} %reduce-scatter.7.cloned.1.call-done) | copy-start | bytes 589828
  685.9 62.0 %all-gather.11.cloned.1.call-start = ((), (), s32[]{:S(2)}) async-start(), calls=%async_computation.20 | async-start | bytes 1769472 | tf_op jit(solution)/shard_map/all_gather | solution.py:150
  721.7 248.7 %reduce-scatter.13.cloned.1.call-start = ((), (), s32[]{:S(2)}) async-start(), calls=%async_computation.21 | async-start | bytes 1622016 | tf_op jit(solution)/shard_map/reduce_scatter | solution.py:157
  752.2 0.9 copy-start.4
  752.2 259.0 %reduce-scatter.17.cloned.1.call-start = ((), (), s32[]{:S(2)}) async-start(), calls=%async_computation.23 | async-start | bytes 3538944 | tf_op jit(solution)/shard_map/reduce_scatter | solution.py:139
  757.0 0.8 copy-start.8
  757.0 294.6 %reduce-scatter.15.cloned.1.call-start = ((), (), s32[]{:S(2)}) async-start(), calls=%async_computation.22 | async-start | bytes 3538944 | tf_op jit(solution)/shard_map/reduce_scatter | solution.py:136
  772.2 4.5 copy-start.16
  772.2 4.5 copy-start.17
  779.2 191.3 %copy-start.9 = (bf16[32,768]{1,0:T(8,128)(2,1)S(1)}, bf16[32,768]{1,0:T(8,128)(2,1)}, u32[]{:S(2)}) copy-start(bf16[32,768]{1,0:T(8,128)(2,1)} %all_to_all.75) | copy-start | bytes 147460
Sparse Core Ops, SparseCore 0:
  10.6 78.7 all-gather.4
  93.8 33.7 reduce-scatter.6
  130.1 25.5 all-gather.6
  160.2 218.0 reduce-scatter.8
  610.5 70.9 all-gather.8
  686.0 33.7 reduce-scatter.10
  722.2 25.5 all-gather.10
  752.4 218.0 reduce-scatter.12
  973.6 37.6 reduce-scatter.16
  1014.3 37.3 reduce-scatter.14
where the time goes:
time: 1060 us
  waiting for transfers between devices  898 us (85%)
  matrix products  41.5 us (4%)
  local copies, waits for them, and re-layouts  38.4 us (4%)
  starting transfers between devices  32.9 us (3%)
  other arithmetic  16.7 us (2%)
  blocking collectives  16.4 us (2%)
  between operations  14.4 us (1%)
    reduce_scatter x1, waiting for transfers between devices, on_device(): lax.psum_scatter(jnp.dot(rows_in, w_down, preferred_element_type=jnp.floa...  207 us
    reduce_scatter x1, waiting for transfers between devices, on_device(): lax.psum_scatter(jnp.dot(rows_in, w_up.T, preferred_element_type=jnp.floa...  189 us
    all_gather x1, waiting for transfers between devices, on_device(): tok_panel = lax.all_gather(tokens, 'col', axis=0, tiled=True)  81.4 us
    all_gather x1, waiting for transfers between devices, on_device(): cot_panel = lax.all_gather(mixed_grad, 'col', axis=0, tiled=True)  71 us
    reduce_scatter x1, waiting for transfers between devices, on_device(): lax.psum_scatter(grad_in.astype(jnp.bfloat16), 'row', scatter_dimension=0...  40.3 us
    reduce_scatter x1, waiting for transfers between devices, on_device(): lax.psum_scatter(grad_out.astype(jnp.bfloat16), 'row', scatter_dimension=...  39.4 us
    all_to_all x1, waiting for transfers between devices, on_device(): lax.all_to_all(send_g, 'col', split_axis=0, concat_axis=0, tiled=True)  37.9 us
    all_to_all x1, waiting for transfers between devices, on_device(): lax.all_to_all(send_x, 'col', split_axis=0, concat_axis=0, tiled=True)  35.1 us
  transfers between devices with their start and end apart: 16, of which 16 were waited for; matrix products, arithmetic and copies ran while one was open for 4% of the time, Pallas kernels for 0%

commit v1 on v0

--- a/solution.py
+++ b/solution.py
@@ -29,6 +29,26 @@
     return jnp.sum((matching & earlier).astype(jnp.int32), axis=-1)
 
 
+def gather_rows(part, axis_name):
+    count = lax.axis_size(axis_name)
+    spread = jnp.broadcast_to(part[None], (count,) + part.shape)
+    got = lax.all_to_all(spread, axis_name, 0, 0, tiled=True)
+    return got.reshape((count * part.shape[0],) + part.shape[1:])
+
+
+def scatter_sum(terms, axis_name):
+    count = lax.axis_size(axis_name)
+    blocks = terms.astype(jnp.bfloat16).reshape((count, terms.shape[0] // count) + terms.shape[1:])
+    got = lax.all_to_all(blocks, axis_name, 0, 0, tiled=True)
+    return got.astype(jnp.float32).sum(axis=0)
+
+
+def scatter_sum_cols(terms, axis_name):
+    count = lax.axis_size(axis_name)
+    got = lax.all_to_all(terms.astype(jnp.bfloat16), axis_name, 1, 0, tiled=True)
+    return got.reshape((count, terms.shape[0], terms.shape[1] // count)).astype(jnp.float32).sum(axis=0)
+
+
 def on_device(tokens, w_up, w_down, expert_in, expert_out, expert_ids, route_weights, out_grad):
     row_count = lax.axis_size("row")
     col_count = lax.axis_size("col")
@@ -38,19 +58,12 @@
     slot_cap = max(2, 3 * block_len // 4)
     model_width = expert_out.shape[1]
     my_row = lax.axis_index("row")
-    tok_panel = lax.all_gather(tokens, "col", axis=0, tiled=True)
+    tok_panel = gather_rows(tokens, "col")
     up_terms = jnp.dot(tok_panel, w_up, preferred_element_type=jnp.float32)
-    preact = lax.psum_scatter(
-        up_terms.astype(jnp.bfloat16), "row", scatter_dimension=0, tiled=True
-    ).astype(jnp.float32)
-    hidden_full = lax.all_gather(gelu_tanh(preact).astype(jnp.bfloat16), "row", axis=0, tiled=True)
+    preact = scatter_sum(up_terms, "row")
+    hidden_full = gather_rows(gelu_tanh(preact).astype(jnp.bfloat16), "row")
     rows_in = hidden_full
-    dense_term = lax.psum_scatter(
-        jnp.dot(rows_in, w_down, preferred_element_type=jnp.float32).astype(jnp.bfloat16),
-        "col",
-        scatter_dimension=0,
-        tiled=True,
-    ).astype(jnp.float32)
+    dense_term = scatter_sum(jnp.dot(rows_in, w_down, preferred_element_type=jnp.float32), "col")
     mixed_act = (tokens.astype(jnp.float32) + dense_term).astype(jnp.bfloat16)
     own_rows, own_grad = (
         lax.all_to_all(mixed_act, "row", split_axis=0, concat_axis=1, tiled=True),
@@ -133,33 +146,20 @@
         lax.all_to_all(layer_rows, "row", split_axis=1, concat_axis=0, tiled=True),
         lax.all_to_all(grad_rows, "row", split_axis=1, concat_axis=0, tiled=True),
     )
-    expert_in_grad = lax.psum_scatter(
-        grad_in.astype(jnp.bfloat16), "row", scatter_dimension=0, tiled=True
-    )
-    expert_out_grad = lax.psum_scatter(
-        grad_out.astype(jnp.bfloat16), "row", scatter_dimension=1, tiled=True
-    )
-    cot_panel = lax.all_gather(mixed_grad, "col", axis=0, tiled=True)
+    expert_in_grad = scatter_sum(grad_in, "row").astype(jnp.bfloat16)
+    expert_out_grad = scatter_sum_cols(grad_out, "row").astype(jnp.bfloat16)
+    cot_panel = gather_rows(mixed_grad, "col")
     hgrad_terms = jnp.dot(cot_panel, w_down.T, preferred_element_type=jnp.float32)
     down_grad = jnp.dot(hidden_full.T, cot_panel, preferred_element_type=jnp.float32).astype(
         jnp.bfloat16
     )
-    hidden_grad = lax.psum_scatter(
-        hgrad_terms.astype(jnp.bfloat16), "row", scatter_dimension=0, tiled=True
-    ).astype(jnp.float32)
-    dpre_full = lax.all_gather(
-        (hidden_grad * gelu_slope(preact)).astype(jnp.bfloat16), "row", axis=0, tiled=True
-    )
+    hidden_grad = scatter_sum(hgrad_terms, "row")
+    dpre_full = gather_rows((hidden_grad * gelu_slope(preact)).astype(jnp.bfloat16), "row")
     up_grad = jnp.dot(tok_panel.T, dpre_full, preferred_element_type=jnp.float32).astype(
         jnp.bfloat16
     )
     rows_in = dpre_full
-    input_term = lax.psum_scatter(
-        jnp.dot(rows_in, w_up.T, preferred_element_type=jnp.float32).astype(jnp.bfloat16),
-        "col",
-        scatter_dimension=0,
-        tiled=True,
-    ).astype(jnp.float32)
+    input_term = scatter_sum(jnp.dot(rows_in, w_up.T, preferred_element_type=jnp.float32), "col")
     tokens_grad = (mixed_grad.astype(jnp.float32) + input_term).astype(jnp.bfloat16)
     return (layer_out, tokens_grad, up_grad, down_grad, expert_in_grad, expert_out_grad)
 

time: 1060 us -> 632 us (0.60)
  waiting for transfers between devices: 898 us -> 368 us
  blocking collectives: 16.4 us -> 85 us
  starting transfers between devices: 32.9 us -> 70.1 us
  between operations: 14.4 us -> 1.07 us
  local copies, waits for them, and re-layouts: 38.4 us -> 51.1 us
    reduce_scatter x6 -> x0, waiting for transfers between devices: 544 us -> none  [the longest x1 207 us: on_device(): lax.psum_scatter(jnp.dot(rows_in, w_down, preferred_element_type=jnp.floa...]
    all_to_all x0 -> x9, waiting for transfers between devices: none -> 224 us  [the longest x4 111 us: scatter_sum(): got = lax.all_to_all(blocks, axis_name, 0, 0, tiled=True)]
    all_gather x4 -> x0, waiting for transfers between devices: 205 us -> none  [the longest x1 81.4 us: on_device(): tok_panel = lax.all_gather(tokens, 'col', axis=0, tiled=True)]
    all_to_all x1 -> x2, blocking collectives: 8.54 us -> 77.1 us  [the longest x1 51.4 us: gather_rows(): got = lax.all_to_all(spread, axis_name, 0, 0, tiled=True)]
    all_to_all x0 -> x9, starting transfers between devices: none -> 39.5 us  [the longest x4 19 us: scatter_sum(): got = lax.all_to_all(blocks, axis_name, 0, 0, tiled=True)]
  transfers between devices with their start and end apart: 16 -> 15, of which waited for: 16 -> 15; matrix products, arithmetic and copies ran while one was open for 4% -> 10% of each run, Pallas kernels for 0% -> 0%
where the time goes in v1:
time: 632 us; the launch traced here: 630 us
  waiting for transfers between devices  368 us (58%)
  blocking collectives  85 us (13%)
  starting transfers between devices  70.1 us (11%)
  local copies, waits for them, and re-layouts  51.1 us (8%)
  matrix products  35.6 us (6%)
  other arithmetic  19 us (3%)
    all_to_all x4, waiting for transfers between devices, scatter_sum(): got = lax.all_to_all(blocks, axis_name, 0, 0, tiled=True)  111 us
    all_to_all x3, waiting for transfers between devices, gather_rows(): got = lax.all_to_all(spread, axis_name, 0, 0, tiled=True)  76.2 us
    all_to_all x1, blocking collectives, gather_rows(): got = lax.all_to_all(spread, axis_name, 0, 0, tiled=True)  51.4 us
    all_to_all x1, waiting for transfers between devices, on_device(): lax.all_to_all(values.reshape(col_count, slot_cap, model_width).astype(jn...  36.6 us
    all_to_all x1, waiting for transfers between devices, scatter_sum_cols(): lax.all_to_all(terms.astype(jnp.bfloat16), axis_name, 1, 0, tiled=True)  35.7 us
    all_to_all x1, waiting for transfers between devices, on_device(): lax.all_to_all(send_x, 'col', split_axis=0, concat_axis=0, tiled=True)  35.1 us
    all_to_all x1, waiting for transfers between devices, on_device(): lax.all_to_all(send_g, 'col', split_axis=0, concat_axis=0, tiled=True)  34.2 us
    all_to_all x1, waiting for transfers between devices, on_device(): lax.all_to_all(returns.reshape(col_count, slot_cap, model_width).astype(j...  32.7 us
  transfers between devices with their start and end apart: 15, of which 15 were waited for; matrix products, arithmetic and copies ran while one was open for 10% of the time, Pallas kernels for 0%

profile of v1, /device:TPU:32, one launch (start us, length us, event | category | flops | bytes accessed | tf_op | source)
XLA Modules:
  0.0 629.8 jit_solution(5777029545172550772)
XLA Ops:
  1.8 51.4 %all_to_all.142 = bf16[32,32,768]{2,1,0:T(8,128)(2,1)S(1)} all-to-all(bf16[32,32,768]{2,1,0:T(8,128)(2,1)S(1)} %broadcast_in_dim.25), channel_id=1, replica_groups=mesh['row'=8,'col'=32] {'col'}, dimensions={0} | all-to-all | bytes 3145728 | tf_op jit(solution)/shard_map/all_to_all | solution.py:35
  54.6 25.7 %all_to_all.143 = bf16[8,128,768]{2,1,0:T(8,128)(2,1)S(1)} all-to-all(bf16[8,128,768]{2,1,0:T(8,128)(2,1)S(1)} %bitcast.74), channel_id=1, replica_groups=mesh['row'=8,'col'=32] {'row'}, dimensions={0} | all-to-all | bytes 3145728 | tf_op jit(solution)/shard_map/all_to_all | solution.py:42
  81.9 4.3 all-to-all-start.2
  87.7 20.1 %all-to-all-done.2 = bf16[8,128,768]{2,1,0:T(8,128)(2,1)} async-done(((bf16[8,128,768]{2,1,0:T(8,128)(2,1)}), bf16[8,128,768]{2,1,0:T(8,128)(2,1)}, u32[]{:S(2)}, u32[]{:S(2)}) %all-to-all-start.2) | async-done | bytes 1572896 | tf_op jit(solution)/shard_map/all_to_all | solution.py:35
  107.8 4.0 all-to-all-start.8
  111.8 4.3 convolution_convert_fusion.8
  117.3 5.0 all-to-all-start.3
  126.9 34.6 %all-to-all-done.3 = bf16[32,32,768]{2,1,0:T(8,128)(2,1)} async-done(((bf16[32,32,768]{2,1,0:T(8,128)(2,1)}), bf16[32,32,768]{2,1,0:T(8,128)(2,1)}, u32[]{:S(2)}, u32[]{:S(2)}) %all-to-all-start.3) | async-done | bytes 1572896 | tf_op jit(solution)/shard_map/all_to_all | solution.py:42
  165.2 3.9 all-to-all-start.4
  171.2 3.5 all-to-all-done.4
  174.7 2.8 broadcast_in_dim.30
  177.5 5.8 all-to-all-start.9
  188.3 34.2 %all-to-all-done.9 = bf16[32,3,6144]{2,1,0:T(4,128)(2,1)} async-done(((bf16[32,3,6144]{2,1,0:T(4,128)(2,1)}), bf16[32,3,6144]{2,1,0:T(4,128)(2,1)}, u32[]{:S(2)}, u32[]{:S(2)}) %all-to-all-start.9) | async-done | bytes 1179680 | tf_op jit(solution)/shard_map/all_to_all | solution.py:96
  222.5 2.8 broadcast_in_dim.28
  225.4 5.8 all-to-all-start.5
  231.2 4.0 reshape.213
  235.1 35.1 %all-to-all-done.5 = bf16[32,3,6144]{2,1,0:T(4,128)(2,1)} async-done(((bf16[32,3,6144]{2,1,0:T(4,128)(2,1)}), bf16[32,3,6144]{2,1,0:T(4,128)(2,1)}, u32[]{:S(2)}, u32[]{:S(2)}) %all-to-all-start.5) | async-done | bytes 1179680 | tf_op jit(solution)/shard_map/all_to_all | solution.py:95
  270.2 3.9 reshape.207
  280.6 3.8 convert_element_type.167
  284.5 5.7 all-to-all-start.10
  290.2 2.6 convolution_convert_fusion.3
  292.8 3.8 convert_element_type.156
  296.6 32.7 %all-to-all-done.10 = bf16[32,3,6144]{2,1,0:T(4,128)(2,1)} async-done(((bf16[32,3,6144]{2,1,0:T(4,128)(2,1)}), bf16[32,3,6144]{2,1,0:T(4,128)(2,1)}, u32[]{:S(2)}, u32[]{:S(2)}) %all-to-all-start.10) | async-done | bytes 1179680 | tf_op jit(solution)/shard_map/all_to_all | solution.py:118
  329.3 5.4 all-to-all-start.6
  334.8 2.2 convert_reduce_fusion
  337.1 36.6 %all-to-all-done.6 = bf16[32,3,6144]{2,1,0:T(4,128)(2,1)S(1)} async-done(((bf16[32,3,6144]{2,1,0:T(4,128)(2,1)}), bf16[32,3,6144]{2,1,0:T(4,128)(2,1)S(1)}, u32[]{:S(2)}, u32[]{:S(2)}) %all-to-all-start.6) | async-done | bytes 1179680 | tf_op jit(solution)/shard_map/all_to_all | solution.py:111
  377.3 7.9 %all_to_all.144 = bf16[4,8,768]{2,0,1:T(4,128)(2,1)S(1)} all-to-all(bf16[4,8,768]{2,0,1:T(4,128)(2,1)S(1)} %fusion.16), channel_id=1, replica_groups=mesh['row'=8,'col'=32] {'row'}, dimensions={1} | all-to-all | bytes 98304 | tf_op jit(solution)/shard_map/all_to_all | solution.py:147
  386.6 5.4 all-to-all-start.12
  393.8 37.3 %all-to-all-done.12 = bf16[32,32,768]{2,1,0:T(8,128)(2,1)S(1)} async-done(((bf16[32,32,768]{2,1,0:T(8,128)(2,1)}), bf16[32,32,768]{2,1,0:T(8,128)(2,1)S(1)}, u32[]{:S(2)}, u32[]{:S(2)}) %all-to-all-start.12) | async-done | bytes 1572896 | tf_op jit(solution)/shard_map/all_to_all | solution.py:35
  431.1 3.3 all-to-all-start.7
  434.5 3.9 convolution_convert_fusion.7
  440.5 4.3 all-to-all-start.13
  444.8 2.3 convolution_convert_fusion
  449.0 17.4 %all-to-all-done.13 = bf16[8,128,768]{2,1,0:T(8,128)(2,1)} async-done(((bf16[8,128,768]{2,1,0:T(8,128)(2,1)}), bf16[8,128,768]{2,1,0:T(8,128)(2,1)}, u32[]{:S(2)}, u32[]{:S(2)}) %all-to-all-start.13) | async-done | bytes 1572896 | tf_op jit(solution)/shard_map/all_to_all | solution.py:42
  466.4 3.6 all-to-all-start.17
  472.7 35.7 %all-to-all-done.17 = bf16[256,8,768]{2,0,1:T(8,128)(2,1)S(1)} async-done(((bf16[256,8,768]{2,0,1:T(8,128)(2,1)}), bf16[256,8,768]{2,0,1:T(8,128)(2,1)S(1)}, u32[]{:S(2)}, u32[]{:S(2)}) %all-to-all-start.17) | async-done | bytes 3145760 | tf_op jit(solution)/shard_map/all_to_all | solution.py:48
  512.2 3.7 all-to-all-start.14
  516.0 2.7 convolution_convert_fusion.1
  518.7 18.8 %all-to-all-done.14 = bf16[8,128,768]{2,1,0:T(8,128)(2,1)S(1)} async-done(((bf16[8,128,768]{2,1,0:T(8,128)(2,1)}), bf16[8,128,768]{2,1,0:T(8,128)(2,1)S(1)}, u32[]{:S(2)}, u32[]{:S(2)}) %all-to-all-start.14) | async-done | bytes 1572896 | tf_op jit(solution)/shard_map/all_to_all | solution.py:35
  538.6 3.6 all-to-all-start.16
  542.3 4.3 convolution_convert_fusion.6
  546.6 34.0 %all-to-all-done.16 = bf16[8,768,256]{2,1,0:T(8,128)(2,1)S(1)} async-done(((bf16[8,768,256]{2,1,0:T(8,128)(2,1)}), bf16[8,768,256]{2,1,0:T(8,128)(2,1)S(1)}, u32[]{:S(2)}, u32[]{:S(2)}) %all-to-all-start.16) | async-done | bytes 3145760 | tf_op jit(solution)/shard_map/all_to_all | solution.py:42
  582.2 6.1 all-to-all-start.15
  590.3 3.3 reduce_sum.120
  593.6 4.0 convolution_convert_fusion.10
  597.6 2.5 fusion
  600.1 2.4 copy.35
  602.5 25.0 %all-to-all-done.15 = bf16[32,32,768]{2,1,0:T(8,128)(2,1)} async-done(((bf16[32,32,768]{2,1,0:T(8,128)(2,1)}), bf16[32,32,768]{2,1,0:T(8,128)(2,1)}, u32[]{:S(2)}, u32[]{:S(2)}) %all-to-all-start.15) | async-done | bytes 1572896 | tf_op jit(solution)/shard_map/all_to_all | solution.py:42
  (112 shorter events, 52.8 us)
Async XLA Ops:
  0.6 273.6 %copy-start = (bf16[6144,256]{1,0:T(8,128)(2,1)S(1)}, bf16[6144,256]{1,0:T(8,128)(2,1)}, u32[]{:S(2)}) copy-start(bf16[6144,256]{1,0:T(8,128)(2,1)} %param.13) | copy-start | bytes 9437188
  1.8 51.4 %copy-start.27 = (bf16[768,768]{1,0:T(8,128)(2,1)S(1)}, bf16[768,768]{1,0:T(8,128)(2,1)}, u32[]{:S(2)}) copy-start(bf16[768,768]{1,0:T(8,128)(2,1)} %param.11) | copy-start | bytes 3538948
  53.2 1.4 copy-start.9
  81.9 25.9 %all-to-all-start.2 = ((bf16[8,128,768]{2,1,0:T(8,128)(2,1)}), bf16[8,128,768]{2,1,0:T(8,128)(2,1)}, u32[]{:S(2)}, u32[]{:S(2)}) async-start(bf16[8,128,768]{2,1,0:T(8,128)(2,1)} %broadcast_in_dim.26), calls=%async_computation.2 | async-start | bytes 3145728 | tf_op jit(solution)/shard_map/all_to_all | solution.py:35
  107.8 9.5 %all-to-all-start.8 = ((bf16[8,4,768]{2,1,0:T(4,128)(2,1)}), bf16[8,4,768]{2,1,0:T(4,128)(2,1)}, u32[]{:S(2)}, u32[]{:S(2)}) async-start(bf16[8,4,768]{2,1,0:T(4,128)(2,1)} %all_to_all.110), calls=%async_computation.8 | async-start | bytes 98304 | tf_op jit(solution)/shard_map/all_to_all | solution.py:70
  117.3 5.0 copy-start.24
  117.3 5.3 copy-start.23
  117.3 44.2 %all-to-all-start.3 = ((bf16[32,32,768]{2,1,0:T(8,128)(2,1)}), bf16[32,32,768]{2,1,0:T(8,128)(2,1)}, u32[]{:S(2)}, u32[]{:S(2)}) async-start(bf16[32,32,768]{2,1,0:T(8,128)(2,1)} %bitcast.70), calls=%async_computation.3 | async-start | bytes 3145728 | tf_op jit(solution)/shard_map/all_to_all | solution.py:42
  123.1 0.5 copy-start.25
  161.5 1.7 copy-start.20
  165.2 9.5 %all-to-all-start.4 = ((bf16[8,4,768]{2,1,0:T(4,128)(2,1)}), bf16[8,4,768]{2,1,0:T(4,128)(2,1)}, u32[]{:S(2)}, u32[]{:S(2)}) async-start(bf16[8,4,768]{2,1,0:T(4,128)(2,1)} %all_to_all.101), calls=%async_computation.4 | async-start | bytes 98304 | tf_op jit(solution)/shard_map/all_to_all | solution.py:69
  177.5 45.0 %all-to-all-start.9 = ((bf16[32,3,6144]{2,1,0:T(4,128)(2,1)}), bf16[32,3,6144]{2,1,0:T(4,128)(2,1)}, u32[]{:S(2)}, u32[]{:S(2)}) async-start(bf16[32,3,6144]{2,1,0:T(4,128)(2,1)} %bitcast.64), calls=%async_computation.9 | async-start | bytes 3145728 | tf_op jit(solution)/shard_map/all_to_all | solution.py:96
  225.4 44.9 %all-to-all-start.5 = ((bf16[32,3,6144]{2,1,0:T(4,128)(2,1)}), bf16[32,3,6144]{2,1,0:T(4,128)(2,1)}, u32[]{:S(2)}, u32[]{:S(2)}) async-start(bf16[32,3,6144]{2,1,0:T(4,128)(2,1)} %bitcast.65), calls=%async_computation.5 | async-start | bytes 3145728 | tf_op jit(solution)/shard_map/all_to_all | solution.py:95
  274.2 2.2 copy-start.3
  274.2 2.6 copy-start.8
  276.8 1.1 copy-start.15
  277.9 0.6 copy-start.16
  284.5 5.7 copy-start.4
  284.5 44.8 %all-to-all-start.10 = ((bf16[32,3,6144]{2,1,0:T(4,128)(2,1)}), bf16[32,3,6144]{2,1,0:T(4,128)(2,1)}, u32[]{:S(2)}, u32[]{:S(2)}) async-start(bf16[32,3,6144]{2,1,0:T(4,128)(2,1)} %convert_element_type.167), calls=%async_computation.10 | async-start | bytes 3145728 | tf_op jit(solution)/shard_map/all_to_all | solution.py:118
  296.6 38.1 %copy-start.26 = (s32[8]{0:T(128)S(1)}, s32[8]{0:T(128)}, u32[]{:S(2)}) copy-start(s32[8]{0:T(128)} %copy-done.25) | copy-start | bytes 100
  329.3 44.5 %all-to-all-start.6 = ((bf16[32,3,6144]{2,1,0:T(4,128)(2,1)}), bf16[32,3,6144]{2,1,0:T(4,128)(2,1)S(1)}, u32[]{:S(2)}, u32[]{:S(2)}) async-start(bf16[32,3,6144]{2,1,0:T(4,128)(2,1)} %convert_element_type.156), calls=%async_computation.6 | async-start | bytes 3145728 | tf_op jit(solution)/shard_map/all_to_all | solution.py:111
  385.2 1.4 copy-start.18
  386.6 44.5 %all-to-all-start.12 = ((bf16[32,32,768]{2,1,0:T(8,128)(2,1)}), bf16[32,32,768]{2,1,0:T(8,128)(2,1)S(1)}, u32[]{:S(2)}, u32[]{:S(2)}) async-start(bf16[32,32,768]{2,1,0:T(8,128)(2,1)} %broadcast_in_dim.31), calls=%async_computation.12 | async-start | bytes 3145728 | tf_op jit(solution)/shard_map/all_to_all | solution.py:35
  431.1 7.3 %copy-start.11 = (bf16[32,32,768]{2,1,0:T(8,128)(2,1)}, bf16[32,32,768]{2,1,0:T(8,128)(2,1)S(1)}, u32[]{:S(2)}) copy-start(bf16[32,32,768]{2,1,0:T(8,128)(2,1)S(1)} %all-to-all-done.12) | copy-start | bytes 4718596
  431.1 8.8 %all-to-all-start.7 = ((bf16[4,8,768]{2,0,1:T(4,128)(2,1)}), bf16[4,8,768]{2,0,1:T(4,128)(2,1)S(1)}, u32[]{:S(2)}, u32[]{:S(2)}) async-start(bf16[4,8,768]{2,0,1:T(4,128)(2,1)} %add_convert_fusion.1), calls=%async_computation.7 | async-start | bytes 98304 | tf_op jit(solution)/shard_map/all_to_all | solution.py:146
  439.9 0.6 copy-start.21
  440.5 25.8 %all-to-all-start.13 = ((bf16[8,128,768]{2,1,0:T(8,128)(2,1)}), bf16[8,128,768]{2,1,0:T(8,128)(2,1)}, u32[]{:S(2)}, u32[]{:S(2)}) async-start(bf16[8,128,768]{2,1,0:T(8,128)(2,1)} %bitcast.18), calls=%async_computation.13 | async-start | bytes 3145728 | tf_op jit(solution)/shard_map/all_to_all | solution.py:42
  466.4 42.0 %all-to-all-start.17 = ((bf16[256,8,768]{2,0,1:T(8,128)(2,1)}), bf16[256,8,768]{2,0,1:T(8,128)(2,1)S(1)}, u32[]{:S(2)}, u32[]{:S(2)}) async-start(bf16[256,8,768]{2,0,1:T(8,128)(2,1)} %bitcast.62), calls=%async_computation.17 | async-start | bytes 6291456 | tf_op jit(solution)/shard_map/all_to_all | solution.py:48
  508.4 1.6 copy-start.5
  512.2 3.7 copy-start.2
  512.2 3.7 copy-start.17
  512.2 25.2 %all-to-all-start.14 = ((bf16[8,128,768]{2,1,0:T(8,128)(2,1)}), bf16[8,128,768]{2,1,0:T(8,128)(2,1)S(1)}, u32[]{:S(2)}, u32[]{:S(2)}) async-start(bf16[8,128,768]{2,1,0:T(8,128)(2,1)} %broadcast_in_dim.32), calls=%async_computation.14 | async-start | bytes 3145728 | tf_op jit(solution)/shard_map/all_to_all | solution.py:35
  537.4 1.2 copy-start.13
  538.6 42.0 %all-to-all-start.16 = ((bf16[8,768,256]{2,1,0:T(8,128)(2,1)}), bf16[8,768,256]{2,1,0:T(8,128)(2,1)S(1)}, u32[]{:S(2)}, u32[]{:S(2)}) async-start(bf16[8,768,256]{2,1,0:T(8,128)(2,1)} %bitcast.22), calls=%async_computation.16 | async-start | bytes 6291456 | tf_op jit(solution)/shard_map/all_to_all | solution.py:42
  542.2 46.1 %copy-start.22 = (bf16[4,8,768]{2,0,1:T(4,128)(2,1)S(1)}, bf16[4,8,768]{2,0,1:T(4,128)(2,1)}, u32[]{:S(2)}) copy-start(bf16[4,8,768]{2,0,1:T(4,128)(2,1)} %copy-done.21) | copy-start | bytes 147460
  580.6 1.7 copy-start.7
  582.2 6.7 %copy-start.6 = (bf16[256,8,768]{2,0,1:T(8,128)(2,1)S(1)}, bf16[256,8,768]{2,0,1:T(8,128)(2,1)}, u32[]{:S(2)}) copy-start(bf16[256,8,768]{2,0,1:T(8,128)(2,1)} %copy-done.5) | copy-start | bytes 9437188
  582.2 45.2 %all-to-all-start.15 = ((bf16[32,32,768]{2,1,0:T(8,128)(2,1)}), bf16[32,32,768]{2,1,0:T(8,128)(2,1)}, u32[]{:S(2)}, u32[]{:S(2)}) async-start(bf16[32,32,768]{2,1,0:T(8,128)(2,1)} %bitcast.73), calls=%async_computation.15 | async-start | bytes 3145728 | tf_op jit(solution)/shard_map/all_to_all | solution.py:42
  590.3 3.3 copy-start.12
  593.5 4.0 copy-start.10
  593.6 4.0 copy-start.14
  597.6 32.2 %copy-start.1 = (bf16[6144,256]{1,0:T(8,128)(2,1)S(1)}, bf16[6144,256]{1,0:T(8,128)(2,1)}, u32[]{:S(2)}) copy-start(bf16[6144,256]{1,0:T(8,128)(2,1)} %param.13) | copy-start | bytes 9437188
  600.1 29.0 %copy-start.19 = (bf16[32,768]{1,0:T(8,128)(2,1)S(1)}, bf16[32,768]{1,0:T(8,128)(2,1)}, u32[]{:S(2)}) copy-start(bf16[32,768]{1,0:T(8,128)(2,1)} %copy-done.18) | copy-start | bytes 147460

commit v2 on v1

--- a/solution.py
+++ b/solution.py
@@ -65,10 +65,10 @@
     rows_in = hidden_full
     dense_term = scatter_sum(jnp.dot(rows_in, w_down, preferred_element_type=jnp.float32), "col")
     mixed_act = (tokens.astype(jnp.float32) + dense_term).astype(jnp.bfloat16)
-    own_rows, own_grad = (
-        lax.all_to_all(mixed_act, "row", split_axis=0, concat_axis=1, tiled=True),
-        lax.all_to_all(out_grad, "row", split_axis=0, concat_axis=1, tiled=True),
+    own_both = lax.all_to_all(
+        jnp.stack([mixed_act, out_grad], axis=1), "row", split_axis=0, concat_axis=2, tiled=True
     )
+    own_rows, own_grad = own_both[:, 0], own_both[:, 1]
     chosen = lax.dynamic_slice_in_dim(expert_ids, my_row * block_len, block_len, 0).reshape(-1)
     weights_own = lax.dynamic_slice_in_dim(route_weights, my_row * block_len, block_len, 0)
     weights_flat = weights_own.reshape(-1).astype(jnp.float32)
@@ -91,10 +91,10 @@
     )
     send_x = jnp.repeat(send_x, group_len, axis=0)
     send_g = jnp.repeat(send_g, group_len, axis=0)
-    got_x, got_g = (
-        lax.all_to_all(send_x, "col", split_axis=0, concat_axis=0, tiled=True),
-        lax.all_to_all(send_g, "col", split_axis=0, concat_axis=0, tiled=True),
+    got_both = lax.all_to_all(
+        jnp.concatenate([send_x, send_g], axis=1), "col", split_axis=0, concat_axis=0, tiled=True
     )
+    got_x, got_g = got_both[:, :slot_cap], got_both[:, slot_cap:]
     inputs = got_x.reshape(-1, model_width)
     grads = got_g.reshape(-1, model_width)
     e_pre = jnp.dot(inputs, expert_in, preferred_element_type=jnp.float32)
@@ -107,22 +107,20 @@
     grad_in = jnp.dot(inputs.T, e_dpre, preferred_element_type=jnp.float32)
     grad_out = jnp.dot(e_hidden.T, grads, preferred_element_type=jnp.float32)
     values, returns, grad_in, grad_out = (values, returns, grad_in, grad_out)
-    back_v, back_d = (
-        lax.all_to_all(
-            values.reshape(col_count, slot_cap, model_width).astype(jnp.bfloat16),
-            "col",
-            split_axis=0,
-            concat_axis=0,
-            tiled=True,
-        ).astype(jnp.float32),
-        lax.all_to_all(
-            returns.reshape(col_count, slot_cap, model_width).astype(jnp.bfloat16),
-            "col",
-            split_axis=0,
-            concat_axis=0,
-            tiled=True,
-        ).astype(jnp.float32),
-    )
+    back_both = lax.all_to_all(
+        jnp.concatenate(
+            [
+                values.reshape(col_count, slot_cap, model_width).astype(jnp.bfloat16),
+                returns.reshape(col_count, slot_cap, model_width).astype(jnp.bfloat16),
+            ],
+            axis=1,
+        ),
+        "col",
+        split_axis=0,
+        concat_axis=0,
+        tiled=True,
+    ).astype(jnp.float32)
+    back_v, back_d = back_both[:, :slot_cap], back_both[:, slot_cap:]
     flat_v = (
         back_v.reshape(EXPERTS, group_len, slot_cap, model_width)
         .sum(axis=1)
@@ -142,12 +140,16 @@
     grad_sum = jnp.take(flat_d, lookup, axis=0).reshape(block_len, 2, model_width).sum(axis=1)
     layer_rows = (own_rows.astype(jnp.float32) + moe_sum).astype(jnp.bfloat16)
     grad_rows = (own_grad.astype(jnp.float32) + grad_sum).astype(jnp.bfloat16)
-    layer_out, mixed_grad = (
-        lax.all_to_all(layer_rows, "row", split_axis=1, concat_axis=0, tiled=True),
-        lax.all_to_all(grad_rows, "row", split_axis=1, concat_axis=0, tiled=True),
+    out_both = lax.all_to_all(
+        jnp.stack([layer_rows, grad_rows], axis=1), "row", split_axis=2, concat_axis=0, tiled=True
     )
-    expert_in_grad = scatter_sum(grad_in, "row").astype(jnp.bfloat16)
-    expert_out_grad = scatter_sum_cols(grad_out, "row").astype(jnp.bfloat16)
+    layer_out, mixed_grad = out_both[:, 0], out_both[:, 1]
+    expert_in_grad = lax.psum_scatter(
+        grad_in.astype(jnp.bfloat16).astype(jnp.float32), "row", scatter_dimension=0, tiled=True
+    ).astype(jnp.bfloat16)
+    expert_out_grad = lax.psum_scatter(
+        grad_out.astype(jnp.bfloat16).astype(jnp.float32), "row", scatter_dimension=1, tiled=True
+    ).astype(jnp.bfloat16)
     cot_panel = gather_rows(mixed_grad, "col")
     hgrad_terms = jnp.dot(cot_panel, w_down.T, preferred_element_type=jnp.float32)
     down_grad = jnp.dot(hidden_full.T, cot_panel, preferred_element_type=jnp.float32).astype(

time: 632 us -> 584 us (0.924)
  waiting for transfers between devices: 368 us -> 136 us
  blocking collectives: 85 us -> 288 us
  starting transfers between devices: 70.1 us -> 19.3 us
  between operations: 1.07 us -> 15 us
  local copies, waits for them, and re-layouts: 51.1 us -> 64.2 us
    all_to_all x11 -> x2, waiting for transfers between devices: 257 us -> 69.2 us  [the longest x1 64.4 us: on_device(): lax.all_to_all(jnp.concatenate([values.reshape(col_count, slot_cap, model...]
    all_to_all x1 -> x4, blocking collectives: 51.4 us -> 150 us  [gather_rows(): got = lax.all_to_all(spread, axis_name, 0, 0, tiled=True)]
    all_to_all x1 -> x2, blocking collectives: 7.91 us -> 88.5 us  [the longest x1 78.8 us: on_device(): lax.all_to_all(jnp.concatenate([send_x, send_g], axis=1), 'col', split_ax...]
    all_to_all x4 -> x2, waiting for transfers between devices: 111 us -> 66.8 us  [scatter_sum(): got = lax.all_to_all(blocks, axis_name, 0, 0, tiled=True)]
    all_to_all x11 -> x2, starting transfers between devices: 51.1 us -> 8.96 us  [the longest x1 4.97 us: on_device(): lax.all_to_all(jnp.concatenate([values.reshape(col_count, slot_cap, model...]
    all_to_all x1 -> x2, blocking collectives: 25.7 us -> 49.7 us  [scatter_sum(): got = lax.all_to_all(blocks, axis_name, 0, 0, tiled=True)]
    unnamed x57 -> x61, local copies, waits for them, and re-layouts: 9.21 us -> 19.1 us
    all_to_all x4 -> x2, starting transfers between devices: 19 us -> 10 us  [scatter_sum(): got = lax.all_to_all(blocks, axis_name, 0, 0, tiled=True)]
  transfers between devices with their start and end apart: 15 -> 6, of which waited for: 15 -> 4; matrix products, arithmetic and copies ran while one was open for 10% -> 12% of each run, Pallas kernels for 0% -> 0%
where the time goes in v2:
time: 584 us; the launch traced here: 576 us
  blocking collectives  288 us (49%)
  waiting for transfers between devices  136 us (23%)
  local copies, waits for them, and re-layouts  64.2 us (11%)
  matrix products  34.3 us (6%)
  other arithmetic  19.3 us (3%)
  starting transfers between devices  19.3 us (3%)
  between operations  15 us (3%)
    all_to_all x4, blocking collectives, gather_rows(): got = lax.all_to_all(spread, axis_name, 0, 0, tiled=True)  150 us
    all_to_all x1, blocking collectives, on_device(): lax.all_to_all(jnp.concatenate([send_x, send_g], axis=1), 'col', split_ax...  78.8 us
    all_to_all x2, waiting for transfers between devices, scatter_sum(): got = lax.all_to_all(blocks, axis_name, 0, 0, tiled=True)  66.8 us
    all_to_all x1, waiting for transfers between devices, on_device(): lax.all_to_all(jnp.concatenate([values.reshape(col_count, slot_cap, model...  64.4 us
    all_to_all x2, blocking collectives, scatter_sum(): got = lax.all_to_all(blocks, axis_name, 0, 0, tiled=True)  49.7 us
    unnamed x61, local copies, waits for them, and re-layouts  19.1 us
  transfers between devices with their start and end apart: 6, of which 4 were waited for; matrix products, arithmetic and copies ran while one was open for 12% of the time, Pallas kernels for 0%

profile of v2, /device:TPU:32, one launch (start us, length us, event | category | flops | bytes accessed | tf_op | source)
XLA Modules:
  0.0 576.0 jit_solution(12224151818652292849)
XLA Ops:
  8.3 51.4 %all_to_all.86 = bf16[32,32,768]{2,1,0:T(8,128)(2,1)S(1)} all-to-all(bf16[32,32,768]{2,1,0:T(8,128)(2,1)S(1)} %broadcast_in_dim.25), channel_id=1, replica_groups=mesh['row'=8,'col'=32] {'col'}, dimensions={0} | all-to-all | bytes 3145728 | tf_op jit(solution)/shard_map/all_to_all | solution.py:35
  61.1 25.7 %all_to_all.87 = bf16[8,128,768]{2,1,0:T(8,128)(2,1)S(1)} all-to-all(bf16[8,128,768]{2,1,0:T(8,128)(2,1)S(1)} %bitcast.89), channel_id=1, replica_groups=mesh['row'=8,'col'=32] {'row'}, dimensions={0} | all-to-all | bytes 3145728 | tf_op jit(solution)/shard_map/all_to_all | solution.py:42
  87.3 24.2 %all_to_all.88 = bf16[8,128,768]{2,1,0:T(8,128)(2,1)S(1)} all-to-all(bf16[8,128,768]{2,1,0:T(8,128)(2,1)S(1)} %broadcast_in_dim.26), channel_id=1, replica_groups=mesh['row'=8,'col'=32] {'row'}, dimensions={0} | all-to-all | bytes 3145728 | tf_op jit(solution)/shard_map/all_to_all | solution.py:35
  111.5 2.5 convolution_convert_fusion.8
  114.0 5.0 all-to-all-start.3
  119.5 38.6 %all-to-all-done.3 = bf16[32,32,768]{2,1,0:T(8,128)(2,1)} async-done(((bf16[32,32,768]{2,1,0:T(8,128)(2,1)}), bf16[32,32,768]{2,1,0:T(8,128)(2,1)}, u32[]{:S(2)}, u32[]{:S(2)}) %all-to-all-start.3) | async-done | bytes 1572896 | tf_op jit(solution)/shard_map/all_to_all | solution.py:42
  158.2 1.6 convert_reduce_fusion.2
  160.6 4.0 all-to-all-start.4
  165.6 4.8 all-to-all-done.4
  170.4 1.6 copy.62
  172.0 1.6 all_to_all.63
  173.5 1.5 slice_bitcast_fusion.2
  175.8 1.7 convert_element_type.161
  179.5 1.5 broadcast_in_dim.27
  181.0 1.6 reshape.217
  183.8 1.7 broadcast_in_dim.30
  186.2 1.5 pad_maximum_fusion
  187.7 78.8 %all_to_all.89 = bf16[32,6,6144]{2,1,0:T(8,128)(2,1)S(1)} all-to-all(bf16[32,6,6144]{2,1,0:T(8,128)(2,1)S(1)} %pad_maximum_fusion), channel_id=1, replica_groups=mesh['row'=8,'col'=32] {'col'}, dimensions={0} | all-to-all | bytes 4718592 | tf_op jit(solution)/shard_map/all_to_all | solution.py:94
  266.5 3.4 fusion.29
  269.9 3.9 reshape.181
  273.8 3.9 reshape.182
  277.8 2.1 fusion.30
  282.1 3.7 fusion.1
  285.8 2.9 convolution_convert_fusion.2
  288.7 2.5 convert_element_type.169
  291.2 3.9 convolution_convert_fusion.3
  295.2 2.5 convert_element_type.166
  297.7 3.2 pad_maximum_fusion.1
  300.9 5.0 all-to-all-start.6
  306.2 5.0 fusion
  311.2 64.4 %all-to-all-done.6 = bf16[32,6,6144]{2,1,0:T(8,128)(2,1)S(1)} async-done(((bf16[32,6,6144]{2,1,0:T(8,128)(2,1)}), bf16[32,6,6144]{2,1,0:T(8,128)(2,1)S(1)}, u32[]{:S(2)}, u32[]{:S(2)}) %all-to-all-start.6) | async-done | bytes 2359328 | tf_op jit(solution)/shard_map/all_to_all | solution.py:110
  376.1 1.5 bitcast_reduce_fusion.1
  380.8 5.9 %copy.58 = bf16[4,2,6144]{0,1,2:T(2,128)(2,1)S(1)} copy(bf16[4,2,6144]{2,0,1:T(4,128)(2,1)} %pad_maximum_fusion.3) | data formatting | bytes 196608 | tf_op jit(solution)/shard_map/stack | solution.py:144
  386.8 6.7 %reshape.220 = bf16[8,2,3072]{2,1,0:T(2,128)(2,1)} reshape(bf16[6144,2,4]{2,1,0:T(2,128)(2,1)S(1)} %bitcast.76) | data formatting | bytes 196608
  393.5 9.8 %all_to_all.90 = bf16[8,2,3072]{2,1,0:T(2,128)(2,1)} all-to-all(bf16[8,2,3072]{2,1,0:T(2,128)(2,1)} %reshape.220), channel_id=1, replica_groups=mesh['row'=8,'col'=32] {'row'}, dimensions={0} | all-to-all | bytes 196608 | tf_op jit(solution)/shard_map/all_to_all | solution.py:143
  403.3 9.7 %reshape.221 = bf16[6144,2,4]{2,1,0:T(2,128)(2,1)S(1)} reshape(bf16[8,2,3072]{2,1,0:T(2,128)(2,1)} %all_to_all.90) | data formatting | bytes 196608
  413.0 4.8 copy.59
  419.6 49.9 %all_to_all.91 = bf16[32,32,768]{2,1,0:T(8,128)(2,1)S(1)} all-to-all(bf16[32,32,768]{2,1,0:T(8,128)(2,1)S(1)} %broadcast_in_dim.31), channel_id=1, replica_groups=mesh['row'=8,'col'=32] {'col'}, dimensions={0} | all-to-all | bytes 3145728 | tf_op jit(solution)/shard_map/all_to_all | solution.py:35
  470.9 24.0 %all_to_all.92 = bf16[8,128,768]{2,1,0:T(8,128)(2,1)S(1)} all-to-all(bf16[8,128,768]{2,1,0:T(8,128)(2,1)S(1)} %bitcast.90), channel_id=1, replica_groups=mesh['row'=8,'col'=32] {'row'}, dimensions={0} | all-to-all | bytes 3145728 | tf_op jit(solution)/shard_map/all_to_all | solution.py:42
  495.6 24.2 %all_to_all.93 = bf16[8,128,768]{2,1,0:T(8,128)(2,1)S(1)} all-to-all(bf16[8,128,768]{2,1,0:T(8,128)(2,1)S(1)} %broadcast_in_dim.58), channel_id=1, replica_groups=mesh['row'=8,'col'=32] {'row'}, dimensions={0} | all-to-all | bytes 3145728 | tf_op jit(solution)/shard_map/all_to_all | solution.py:35
  519.7 2.6 convolution_convert_fusion.6
  522.3 5.0 all-to-all-start.11
  527.4 4.0 convolution_convert_fusion.10
  531.4 1.5 fusion.2
  534.3 2.1 convert_element_type.186
  536.4 2.0 convert_element_type.189
  538.3 28.1 %all-to-all-done.11 = bf16[32,32,768]{2,1,0:T(8,128)(2,1)} async-done(((bf16[32,32,768]{2,1,0:T(8,128)(2,1)}), bf16[32,32,768]{2,1,0:T(8,128)(2,1)}, u32[]{:S(2)}, u32[]{:S(2)}) %all-to-all-start.11) | async-done | bytes 1572896 | tf_op jit(solution)/shard_map/all_to_all | solution.py:42
  566.5 1.6 convert_reduce_fusion
  (111 shorter events, 21.9 us)
Async XLA Ops:
  7.2 270.6 %copy-start = (bf16[6144,256]{1,0:T(8,128)(2,1)S(1)}, bf16[6144,256]{1,0:T(8,128)(2,1)}, u32[]{:S(2)}) copy-start(bf16[6144,256]{1,0:T(8,128)(2,1)} %param.13) | copy-start | bytes 9437188
  8.3 51.4 %copy-start.27 = (bf16[768,768]{1,0:T(8,128)(2,1)S(1)}, bf16[768,768]{1,0:T(8,128)(2,1)}, u32[]{:S(2)}) copy-start(bf16[768,768]{1,0:T(8,128)(2,1)} %param.11) | copy-start | bytes 3538948
  59.7 1.4 copy-start.5
  87.3 24.2 %copy-start.25 = (bf16[768,768]{1,0:T(8,128)(2,1)S(1)}, bf16[768,768]{1,0:T(8,128)(2,1)}, u32[]{:S(2)}) copy-start(bf16[768,768]{1,0:T(8,128)(2,1)} %param.12) | copy-start | bytes 3538948
  111.5 2.5 copy-start.7
  114.0 5.0 copy-start.22
  114.0 44.2 %all-to-all-start.3 = ((bf16[32,32,768]{2,1,0:T(8,128)(2,1)}), bf16[32,32,768]{2,1,0:T(8,128)(2,1)}, u32[]{:S(2)}, u32[]{:S(2)}) async-start(bf16[32,32,768]{2,1,0:T(8,128)(2,1)} %bitcast.84), calls=%async_computation.3 | async-start | bytes 3145728 | tf_op jit(solution)/shard_map/all_to_all | solution.py:42
  119.3 45.3 %copy-start.20 = (s32[8]{0:T(128)}, s32[8]{0:T(128)S(1)}, u32[]{:S(2)}) copy-start(s32[8]{0:T(128)S(1)} %eq.51) | copy-start | bytes 100
  119.5 45.2 %copy-start.23 = (s32[8]{0:T(128)}, s32[8]{0:T(128)S(1)}, u32[]{:S(2)}) copy-start(s32[8]{0:T(128)S(1)} %convert_reduce_fusion.4) | copy-start | bytes 100
  158.2 1.7 copy-start.18
  158.2 1.7 copy-start.19
  160.6 9.8 %all-to-all-start.4 = ((bf16[32,2,768]{2,1,0:T(2,128)(2,1)}), bf16[32,2,768]{2,1,0:T(2,128)(2,1)}, u32[]{:S(2)}, u32[]{:S(2)}) async-start(bf16[32,2,768]{2,1,0:T(2,128)(2,1)} %copy.52), calls=%async_computation.4 | async-start | bytes 196608 | tf_op jit(solution)/shard_map/all_to_all | solution.py:68
  164.6 369.7 %reduce-scatter.3.cloned.1.call-start = ((), (), s32[]{:S(2)}) async-start(), calls=%async_computation.14 | async-start | bytes 7077888 | tf_op jit(solution)/shard_map/reduce_scatter | solution.py:147
  277.8 2.2 copy-start.3
  277.8 2.6 copy-start.4
  280.3 1.1 copy-start.12
  280.3 1.7 copy-start.2
  281.5 0.6 copy-start.17
  288.7 2.6 copy-start.13
  300.9 5.2 copy-start.21
  300.9 5.3 copy-start.24
  300.9 74.7 %all-to-all-start.6 = ((bf16[32,6,6144]{2,1,0:T(8,128)(2,1)}), bf16[32,6,6144]{2,1,0:T(8,128)(2,1)S(1)}, u32[]{:S(2)}, u32[]{:S(2)}) async-start(bf16[32,6,6144]{2,1,0:T(8,128)(2,1)} %pad_maximum_fusion.1), calls=%async_computation.6 | async-start | bytes 6291456 | tf_op jit(solution)/shard_map/all_to_all | solution.py:110
  305.8 230.6 %reduce-scatter.5.cloned.1.call-start = ((), (), s32[]{:S(2)}) async-start(), calls=%async_computation.15 | async-start | bytes 7077888 | tf_op jit(solution)/shard_map/reduce_scatter | solution.py:150
  378.6 1.5 copy-start.14
  418.7 0.7 copy-start.15
  419.6 49.9 %copy-start.26 = (bf16[768,768]{1,0:T(8,128)(2,1)S(1)}, bf16[768,768]{1,0:T(8,128)(2,1)}, u32[]{:S(2)}) copy-start(bf16[768,768]{1,0:T(8,128)(2,1)} %param.12) | copy-start | bytes 3538948
  469.5 1.4 copy-start.9
  495.6 24.2 %copy-start.28 = (bf16[768,768]{1,0:T(8,128)(2,1)S(1)}, bf16[768,768]{1,0:T(8,128)(2,1)}, u32[]{:S(2)}) copy-start(bf16[768,768]{1,0:T(8,128)(2,1)} %param.11) | copy-start | bytes 3538948
  519.7 2.6 copy-start.10
  522.3 5.0 copy-start.8
  522.3 44.2 %all-to-all-start.11 = ((bf16[32,32,768]{2,1,0:T(8,128)(2,1)}), bf16[32,32,768]{2,1,0:T(8,128)(2,1)}, u32[]{:S(2)}, u32[]{:S(2)}) async-start(bf16[32,32,768]{2,1,0:T(8,128)(2,1)} %bitcast.24), calls=%async_computation.11 | async-start | bytes 3145728 | tf_op jit(solution)/shard_map/all_to_all | solution.py:42
  527.4 4.0 copy-start.6
  527.4 4.0 copy-start.11
  534.3 34.4 %copy-start.1 = (bf16[6144,256]{1,0:T(8,128)(2,1)S(1)}, bf16[6144,256]{1,0:T(8,128)(2,1)}, u32[]{:S(2)}) copy-start(bf16[6144,256]{1,0:T(8,128)(2,1)} %param.13) | copy-start | bytes 9437188
  536.4 31.7 %copy-start.16 = (bf16[32,2,768]{2,0,1:T(8,128)(2,1)S(1)}, bf16[32,2,768]{2,0,1:T(8,128)(2,1)}, u32[]{:S(2)}) copy-start(bf16[32,2,768]{2,0,1:T(8,128)(2,1)} %copy-done.15) | copy-start | bytes 294916
Sparse Core Ops, SparseCore 0:
  285.9 39.9 reduce-scatter.2
  328.5 45.4 reduce-scatter.4

commit v3 on v2

--- a/solution.py
+++ b/solution.py
@@ -47,6 +47,31 @@
     count = lax.axis_size(axis_name)
     got = lax.all_to_all(terms.astype(jnp.bfloat16), axis_name, 1, 0, tiled=True)
     return got.reshape((count, terms.shape[0], terms.shape[1] // count)).astype(jnp.float32).sum(axis=0)
+
+
+def dense_exchange(payload, axis_name):
+    shape = payload.shape
+    flat = payload.reshape(shape[0], -1, 128)
+    got = lax.all_to_all(flat, axis_name, 0, 0, tiled=True)
+    return got.reshape(shape)
+
+
+def swap_blocks(pair, count):
+    arrays, tok, width = pair.shape
+    block = tok // count
+    parts = pair.reshape(arrays, count, block, width).transpose(1, 0, 2, 3)
+    got = lax.all_to_all(parts.reshape(count, arrays * block, width), "row", 0, 0, tiled=True)
+    got = got.reshape(count, arrays, block, width).transpose(1, 2, 0, 3)
+    return got.reshape(arrays, block, count * width)
+
+
+def unswap_blocks(pair, count):
+    arrays, block, full = pair.shape
+    width = full // count
+    parts = pair.reshape(arrays, block, count, width).transpose(2, 0, 1, 3)
+    got = lax.all_to_all(parts.reshape(count, arrays * block, width), "row", 0, 0, tiled=True)
+    got = got.reshape(count, arrays, block, width).transpose(1, 0, 2, 3)
+    return got.reshape(arrays, count * block, width)
 
 
 def on_device(tokens, w_up, w_down, expert_in, expert_out, expert_ids, route_weights, out_grad):
@@ -65,10 +90,8 @@
     rows_in = hidden_full
     dense_term = scatter_sum(jnp.dot(rows_in, w_down, preferred_element_type=jnp.float32), "col")
     mixed_act = (tokens.astype(jnp.float32) + dense_term).astype(jnp.bfloat16)
-    own_both = lax.all_to_all(
-        jnp.stack([mixed_act, out_grad], axis=1), "row", split_axis=0, concat_axis=2, tiled=True
-    )
-    own_rows, own_grad = own_both[:, 0], own_both[:, 1]
+    own_both = swap_blocks(jnp.stack([mixed_act, out_grad]), row_count)
+    own_rows, own_grad = own_both[0], own_both[1]
     chosen = lax.dynamic_slice_in_dim(expert_ids, my_row * block_len, block_len, 0).reshape(-1)
     weights_own = lax.dynamic_slice_in_dim(route_weights, my_row * block_len, block_len, 0)
     weights_flat = weights_own.reshape(-1).astype(jnp.float32)
@@ -91,9 +114,7 @@
     )
     send_x = jnp.repeat(send_x, group_len, axis=0)
     send_g = jnp.repeat(send_g, group_len, axis=0)
-    got_both = lax.all_to_all(
-        jnp.concatenate([send_x, send_g], axis=1), "col", split_axis=0, concat_axis=0, tiled=True
-    )
+    got_both = dense_exchange(jnp.concatenate([send_x, send_g], axis=1), "col")
     got_x, got_g = got_both[:, :slot_cap], got_both[:, slot_cap:]
     inputs = got_x.reshape(-1, model_width)
     grads = got_g.reshape(-1, model_width)
@@ -107,7 +128,7 @@
     grad_in = jnp.dot(inputs.T, e_dpre, preferred_element_type=jnp.float32)
     grad_out = jnp.dot(e_hidden.T, grads, preferred_element_type=jnp.float32)
     values, returns, grad_in, grad_out = (values, returns, grad_in, grad_out)
-    back_both = lax.all_to_all(
+    back_both = dense_exchange(
         jnp.concatenate(
             [
                 values.reshape(col_count, slot_cap, model_width).astype(jnp.bfloat16),
@@ -116,9 +137,6 @@
             axis=1,
         ),
         "col",
-        split_axis=0,
-        concat_axis=0,
-        tiled=True,
     ).astype(jnp.float32)
     back_v, back_d = back_both[:, :slot_cap], back_both[:, slot_cap:]
     flat_v = (
@@ -140,10 +158,8 @@
     grad_sum = jnp.take(flat_d, lookup, axis=0).reshape(block_len, 2, model_width).sum(axis=1)
     layer_rows = (own_rows.astype(jnp.float32) + moe_sum).astype(jnp.bfloat16)
     grad_rows = (own_grad.astype(jnp.float32) + grad_sum).astype(jnp.bfloat16)
-    out_both = lax.all_to_all(
-        jnp.stack([layer_rows, grad_rows], axis=1), "row", split_axis=2, concat_axis=0, tiled=True
-    )
-    layer_out, mixed_grad = out_both[:, 0], out_both[:, 1]
+    out_both = unswap_blocks(jnp.stack([layer_rows, grad_rows]), row_count)
+    layer_out, mixed_grad = out_both[0], out_both[1]
     expert_in_grad = lax.psum_scatter(
         grad_in.astype(jnp.bfloat16).astype(jnp.float32), "row", scatter_dimension=0, tiled=True
     ).astype(jnp.bfloat16)

time: 584 us -> 546 us (0.935)
  blocking collectives: 288 us -> 267 us
  waiting for transfers between devices: 136 us -> 120 us
  other arithmetic: 19.3 us -> 26.5 us
    reshape x0 -> x6, local copies, waits for them, and re-layouts: none -> 18.3 us  [the longest x2 10.3 us: dense_exchange(): flat = payload.reshape(shape[0], -1, 128)]
    all_to_all x2, blocking collectives: 88.5 us -> 70.8 us  [the longest x1 62.6 us: dense_exchange(): got = lax.all_to_all(flat, axis_name, 0, 0, tiled=True)]
    unnamed x61 -> x63, local copies, waits for them, and re-layouts: 19.1 us -> 3.3 us
    all_to_all x2, waiting for transfers between devices: 69.2 us -> 55.6 us  [the longest x1 50.7 us: dense_exchange(): got = lax.all_to_all(flat, axis_name, 0, 0, tiled=True)]
    all_to_all x4 -> x1, local copies, waits for them, and re-layouts: 8.89 us -> 0.02 us  [unswap_blocks(): lax.all_to_all(parts.reshape(count, arrays * block, width), 'row', 0, 0,...]
    convert_element_type x0 -> x1, local copies, waits for them, and re-layouts: none -> 5.98 us  [on_device(): back_both = dense_exchange(jnp.concatenate([values.reshape(col_count, slo...]
  transfers between devices with their start and end apart: 6 -> 6, of which waited for: 4 -> 4; matrix products, arithmetic and copies ran while one was open for 12% -> 11% of each run, Pallas kernels for 0% -> 0%
where the time goes in v3:
time: 546 us; the launch traced here: 544 us
  blocking collectives  267 us (49%)
  waiting for transfers between devices  120 us (22%)
  local copies, waits for them, and re-layouts  64.5 us (12%)
  matrix products  31.5 us (6%)
  other arithmetic  26.5 us (5%)
  starting transfers between devices  19.4 us (4%)
  between operations  14.5 us (3%)
    all_to_all x4, blocking collectives, gather_rows(): got = lax.all_to_all(spread, axis_name, 0, 0, tiled=True)  146 us
    all_to_all x2, waiting for transfers between devices, scatter_sum(): got = lax.all_to_all(blocks, axis_name, 0, 0, tiled=True)  64.7 us
    all_to_all x1, blocking collectives, dense_exchange(): got = lax.all_to_all(flat, axis_name, 0, 0, tiled=True)  62.6 us
    all_to_all x1, waiting for transfers between devices, dense_exchange(): got = lax.all_to_all(flat, axis_name, 0, 0, tiled=True)  50.7 us
    all_to_all x2, blocking collectives, scatter_sum(): got = lax.all_to_all(blocks, axis_name, 0, 0, tiled=True)  49.7 us
  transfers between devices with their start and end apart: 6, of which 4 were waited for; matrix products, arithmetic and copies ran while one was open for 11% of the time, Pallas kernels for 0%

profile of v3, /device:TPU:32, one launch (start us, length us, event | category | flops | bytes accessed | tf_op | source)
XLA Modules:
  0.0 543.6 jit_solution(2561501505828562935)
XLA Ops:
  8.3 51.4 %all_to_all.60 = bf16[32,32,768]{2,1,0:T(8,128)(2,1)S(1)} all-to-all(bf16[32,32,768]{2,1,0:T(8,128)(2,1)S(1)} %broadcast_in_dim.25), channel_id=1, replica_groups=mesh['row'=8,'col'=32] {'col'}, dimensions={0} | all-to-all | bytes 3145728 | tf_op jit(solution)/shard_map/all_to_all | solution.py:35
  61.1 25.7 %all_to_all.61 = bf16[8,128,768]{2,1,0:T(8,128)(2,1)S(1)} all-to-all(bf16[8,128,768]{2,1,0:T(8,128)(2,1)S(1)} %bitcast.66), channel_id=1, replica_groups=mesh['row'=8,'col'=32] {'row'}, dimensions={0} | all-to-all | bytes 3145728 | tf_op jit(solution)/shard_map/all_to_all | solution.py:42
  87.3 24.2 %all_to_all.62 = bf16[8,128,768]{2,1,0:T(8,128)(2,1)S(1)} all-to-all(bf16[8,128,768]{2,1,0:T(8,128)(2,1)S(1)} %broadcast_in_dim.26), channel_id=1, replica_groups=mesh['row'=8,'col'=32] {'row'}, dimensions={0} | all-to-all | bytes 3145728 | tf_op jit(solution)/shard_map/all_to_all | solution.py:35
  111.5 2.5 convolution_convert_fusion.8
  114.0 5.0 all-to-all-start.3
  121.0 37.2 %all-to-all-done.3 = bf16[32,32,768]{2,1,0:T(8,128)(2,1)} async-done(((bf16[32,32,768]{2,1,0:T(8,128)(2,1)}), bf16[32,32,768]{2,1,0:T(8,128)(2,1)}, u32[]{:S(2)}, u32[]{:S(2)}) %all-to-all-start.3) | async-done | bytes 1572896 | tf_op jit(solution)/shard_map/all_to_all | solution.py:42
  158.2 1.6 convert_reduce_fusion.2
  163.5 4.0 all-to-all-start.4
  168.4 4.8 all-to-all-done.4
  173.2 1.6 reshape.225
  174.8 1.5 fusion.28
  177.0 1.7 convert_element_type.168
  180.7 1.5 broadcast_in_dim.27
  182.2 1.6 reshape.271
  185.0 1.7 broadcast_in_dim.30
  187.4 3.2 pad_maximum_fusion
  190.6 6.2 %reshape.229 = bf16[32,288,128]{2,1,0:T(8,128)(2,1)} reshape(bf16[32,6,6144]{2,1,0:T(8,128)(2,1)} %pad_maximum_fusion) | data formatting | bytes 4718592 | tf_op jit(solution)/shard_map/reshape | solution.py:54
  196.7 62.6 %all_to_all.63 = bf16[32,288,128]{2,1,0:T(8,128)(2,1)} all-to-all(bf16[32,288,128]{2,1,0:T(8,128)(2,1)} %reshape.229), channel_id=1, replica_groups=mesh['row'=8,'col'=32] {'col'}, dimensions={0} | all-to-all | bytes 4718592 | tf_op jit(solution)/shard_map/all_to_all | solution.py:55
  259.4 5.8 %reshape.230 = bf16[32,6,6144]{2,1,0:T(8,128)(2,1)} reshape(bf16[32,288,128]{2,1,0:T(8,128)(2,1)} %all_to_all.63) | data formatting | bytes 4718592 | tf_op jit(solution)/shard_map/reshape | solution.py:56
  265.1 6.3 %fusion.26 = (bf16[32,3,6144]{2,1,0:T(4,128)(2,1)}, bf16[32,3,6144]{2,1,0:T(4,128)(2,1)}) fusion(bf16[32,6,6144]{2,1,0:T(8,128)(2,1)} %reshape.230), kind=kLoop, calls=%fused_computation.73 | loop fusion | bytes 4718592 | tf_op jit(solution)/shard_map/slice | solution.py:118
  271.4 3.9 reshape.231
  275.4 3.9 reshape.232
  279.3 2.1 fusion.29
  283.6 3.7 fusion.1
  287.3 2.9 convolution_convert_fusion.2
  290.2 3.9 convert_element_type.176
  294.2 2.5 convolution_convert_fusion.3
  296.7 2.1 convert_element_type.173
  298.8 3.5 pad_maximum_fusion.1
  302.3 4.1 reshape.233
  306.4 5.1 all-to-all-start.6
  311.8 3.6 fusion
  315.5 50.7 %all-to-all-done.6 = bf16[32,288,128]{2,1,0:T(8,128)(2,1)} async-done(((bf16[32,288,128]{2,1,0:T(8,128)(2,1)}), bf16[32,288,128]{2,1,0:T(8,128)(2,1)}, u32[]{:S(2)}, u32[]{:S(2)}) %all-to-all-start.6) | async-done | bytes 2359328 | tf_op jit(solution)/shard_map/all_to_all | solution.py:55
  366.2 6.0 %reshape.248 = f32[32,6,6144]{2,1,0:T(8,128)} reshape(bf16[32,288,128]{2,1,0:T(8,128)(2,1)} %all-to-all-done.6) | data formatting | bytes 7077888 | tf_op jit(solution)/shard_map/convert_element_type | solution.py:140
  372.2 6.5 %bitcast_reduce_fusion.1 = (f32[4,3,6144]{2,1,0:T(4,128)S(1)}, f32[4,3,6144]{2,1,0:T(4,128)S(1)}) fusion(f32[32,6,6144]{2,1,0:T(8,128)} %reshape.248), kind=kLoop, calls=%fused_computation.13 | loop fusion | flops 1032192 | bytes 5308416 | tf_op jit(solution)/shard_map/reduce_sum | solution.py:144
  381.3 8.2 %all_to_all.64 = bf16[8,8,768]{2,1,0:T(8,128)(2,1)S(1)} all-to-all(bf16[8,8,768]{2,1,0:T(8,128)(2,1)S(1)} %reshape.240), channel_id=1, replica_groups=mesh['row'=8,'col'=32] {'row'}, dimensions={0} | all-to-all | bytes 196608 | tf_op jit(solution)/shard_map/all_to_all | solution.py:72
  391.0 46.6 %all_to_all.65 = bf16[32,32,768]{2,1,0:T(8,128)(2,1)S(1)} all-to-all(bf16[32,32,768]{2,1,0:T(8,128)(2,1)S(1)} %broadcast_in_dim.31), channel_id=1, replica_groups=mesh['row'=8,'col'=32] {'col'}, dimensions={0} | all-to-all | bytes 3145728 | tf_op jit(solution)/shard_map/all_to_all | solution.py:35
  439.0 24.0 %all_to_all.66 = bf16[8,128,768]{2,1,0:T(8,128)(2,1)S(1)} all-to-all(bf16[8,128,768]{2,1,0:T(8,128)(2,1)S(1)} %bitcast.67), channel_id=1, replica_groups=mesh['row'=8,'col'=32] {'row'}, dimensions={0} | all-to-all | bytes 3145728 | tf_op jit(solution)/shard_map/all_to_all | solution.py:42
  463.6 24.2 %all_to_all.67 = bf16[8,128,768]{2,1,0:T(8,128)(2,1)S(1)} all-to-all(bf16[8,128,768]{2,1,0:T(8,128)(2,1)S(1)} %broadcast_in_dim.58), channel_id=1, replica_groups=mesh['row'=8,'col'=32] {'row'}, dimensions={0} | all-to-all | bytes 3145728 | tf_op jit(solution)/shard_map/all_to_all | solution.py:35
  487.8 2.6 convolution_convert_fusion.6
  490.4 5.0 all-to-all-start.11
  496.1 4.0 convolution_convert_fusion.10
  500.1 1.5 fusion.2
  501.6 1.5 copy.51
  503.0 2.1 convert_element_type.194
  505.1 1.9 convert_element_type.197
  507.0 27.5 %all-to-all-done.11 = bf16[32,32,768]{2,1,0:T(8,128)(2,1)} async-done(((bf16[32,32,768]{2,1,0:T(8,128)(2,1)}), bf16[32,32,768]{2,1,0:T(8,128)(2,1)}, u32[]{:S(2)}, u32[]{:S(2)}) %all-to-all-start.11) | async-done | bytes 1572896 | tf_op jit(solution)/shard_map/all_to_all | solution.py:42
  534.5 1.6 convert_reduce_fusion
  (121 shorter events, 24.0 us)
Async XLA Ops:
  7.2 272.1 %copy-start = (bf16[6144,256]{1,0:T(8,128)(2,1)S(1)}, bf16[6144,256]{1,0:T(8,128)(2,1)}, u32[]{:S(2)}) copy-start(bf16[6144,256]{1,0:T(8,128)(2,1)} %param.13) | copy-start | bytes 9437188
  8.3 51.4 %copy-start.29 = (bf16[768,768]{1,0:T(8,128)(2,1)S(1)}, bf16[768,768]{1,0:T(8,128)(2,1)}, u32[]{:S(2)}) copy-start(bf16[768,768]{1,0:T(8,128)(2,1)} %param.11) | copy-start | bytes 3538948
  59.7 1.4 copy-start.6
  87.3 24.2 %copy-start.27 = (bf16[768,768]{1,0:T(8,128)(2,1)S(1)}, bf16[768,768]{1,0:T(8,128)(2,1)}, u32[]{:S(2)}) copy-start(bf16[768,768]{1,0:T(8,128)(2,1)} %param.12) | copy-start | bytes 3538948
  111.5 2.5 copy-start.8
  114.0 5.0 copy-start.24
  114.0 44.2 %all-to-all-start.3 = ((bf16[32,32,768]{2,1,0:T(8,128)(2,1)}), bf16[32,32,768]{2,1,0:T(8,128)(2,1)}, u32[]{:S(2)}, u32[]{:S(2)}) async-start(bf16[32,32,768]{2,1,0:T(8,128)(2,1)} %bitcast.61), calls=%async_computation.3 | async-start | bytes 3145728 | tf_op jit(solution)/shard_map/all_to_all | solution.py:42
  119.3 48.2 %copy-start.22 = (s32[8]{0:T(128)}, s32[8]{0:T(128)S(1)}, u32[]{:S(2)}) copy-start(s32[8]{0:T(128)S(1)} %eq.51) | copy-start | bytes 100
  120.9 46.6 %copy-start.25 = (s32[8]{0:T(128)}, s32[8]{0:T(128)S(1)}, u32[]{:S(2)}) copy-start(s32[8]{0:T(128)S(1)} %convert_reduce_fusion.4) | copy-start | bytes 100
  158.2 1.7 copy-start.20
  163.5 9.8 %all-to-all-start.4 = ((bf16[8,8,768]{2,1,0:T(8,128)(2,1)}), bf16[8,8,768]{2,1,0:T(8,128)(2,1)}, u32[]{:S(2)}, u32[]{:S(2)}) async-start(bf16[8,8,768]{2,1,0:T(8,128)(2,1)} %copy.43), calls=%async_computation.4 | async-start | bytes 196608 | tf_op jit(solution)/shard_map/all_to_all | solution.py:63
  167.5 335.6 %reduce-scatter.3.cloned.1.call-start = ((), (), s32[]{:S(2)}) async-start(), calls=%async_computation.14 | async-start | bytes 7077888 | tf_op jit(solution)/shard_map/reduce_scatter | solution.py:163
  279.3 2.2 copy-start.3
  279.3 2.6 copy-start.4
  281.9 1.1 copy-start.13
  281.9 1.7 copy-start.2
  283.0 0.6 copy-start.17
  290.2 3.9 copy-start.14
  306.4 5.4 copy-start.23
  306.4 5.4 copy-start.26
  306.4 5.4 copy-start.5
  306.4 5.4 copy-start.15
  306.4 59.8 %all-to-all-start.6 = ((bf16[32,288,128]{2,1,0:T(8,128)(2,1)}), bf16[32,288,128]{2,1,0:T(8,128)(2,1)}, u32[]{:S(2)}, u32[]{:S(2)}) async-start(bf16[32,288,128]{2,1,0:T(8,128)(2,1)} %reshape.233), calls=%async_computation.6 | async-start | bytes 4718592 | tf_op jit(solution)/shard_map/all_to_all | solution.py:55
  311.5 193.6 %reduce-scatter.5.cloned.1.call-start = ((), (), s32[]{:S(2)}) async-start(), calls=%async_computation.15 | async-start | bytes 7077888 | tf_op jit(solution)/shard_map/reduce_scatter | solution.py:166
  379.6 1.5 copy-start.16
  390.2 0.6 copy-start.18
  391.0 46.6 %copy-start.28 = (bf16[768,768]{1,0:T(8,128)(2,1)S(1)}, bf16[768,768]{1,0:T(8,128)(2,1)}, u32[]{:S(2)}) copy-start(bf16[768,768]{1,0:T(8,128)(2,1)} %param.12) | copy-start | bytes 3538948
  437.5 1.4 copy-start.10
  463.6 24.2 %copy-start.30 = (bf16[768,768]{1,0:T(8,128)(2,1)S(1)}, bf16[768,768]{1,0:T(8,128)(2,1)}, u32[]{:S(2)}) copy-start(bf16[768,768]{1,0:T(8,128)(2,1)} %param.11) | copy-start | bytes 3538948
  487.8 2.6 copy-start.11
  490.4 5.1 copy-start.21
  490.4 5.7 %copy-start.9 = (bf16[8,128,768]{2,1,0:T(8,128)(2,1)S(1)}, bf16[8,128,768]{2,1,0:T(8,128)(2,1)}, u32[]{:S(2)}) copy-start(bf16[8,128,768]{2,1,0:T(8,128)(2,1)} %copy-done.8) | copy-start | bytes 4718596
  490.4 44.2 %all-to-all-start.11 = ((bf16[32,32,768]{2,1,0:T(8,128)(2,1)}), bf16[32,32,768]{2,1,0:T(8,128)(2,1)}, u32[]{:S(2)}, u32[]{:S(2)}) async-start(bf16[32,32,768]{2,1,0:T(8,128)(2,1)} %bitcast.23), calls=%async_computation.11 | async-start | bytes 3145728 | tf_op jit(solution)/shard_map/all_to_all | solution.py:42
  496.1 4.0 copy-start.7
  496.1 4.0 copy-start.12
  503.0 33.8 %copy-start.1 = (bf16[6144,256]{1,0:T(8,128)(2,1)S(1)}, bf16[6144,256]{1,0:T(8,128)(2,1)}, u32[]{:S(2)}) copy-start(bf16[6144,256]{1,0:T(8,128)(2,1)} %param.13) | copy-start | bytes 9437188
  505.1 31.1 %copy-start.19 = (bf16[32,768]{1,0:T(8,128)(2,1)S(1)}, bf16[32,768]{1,0:T(8,128)(2,1)}, u32[]{:S(2)}) copy-start(bf16[32,768]{1,0:T(8,128)(2,1)} %copy-done.18) | copy-start | bytes 147460
Sparse Core Ops, SparseCore 0:
  287.5 39.1 reduce-scatter.2
  329.2 45.7 reduce-scatter.4

commit v4 on v3

--- a/solution.py
+++ b/solution.py
@@ -92,70 +92,51 @@
     mixed_act = (tokens.astype(jnp.float32) + dense_term).astype(jnp.bfloat16)
     own_both = swap_blocks(jnp.stack([mixed_act, out_grad]), row_count)
     own_rows, own_grad = own_both[0], own_both[1]
-    chosen = lax.dynamic_slice_in_dim(expert_ids, my_row * block_len, block_len, 0).reshape(-1)
+    ids_own = lax.dynamic_slice_in_dim(expert_ids, my_row * block_len, block_len, 0)
     weights_own = lax.dynamic_slice_in_dim(route_weights, my_row * block_len, block_len, 0)
-    weights_flat = weights_own.reshape(-1).astype(jnp.float32)
-    rows_x = jnp.repeat(own_rows, 2, axis=0)
-    scaled = (weights_flat[:, None] * jnp.repeat(own_grad, 2, axis=0).astype(jnp.float32)).astype(
-        jnp.bfloat16
+    expert_range = jnp.arange(EXPERTS, dtype=jnp.int32)
+    weight_table = jnp.sum(
+        weights_own.astype(jnp.float32)[None, :, :]
+        * (ids_own[None, :, :] == expert_range[:, None, None]).astype(jnp.float32),
+        axis=2,
     )
-    slot_range = jnp.arange(slot_cap, dtype=jnp.int32)
-    placed = slot_ranks(chosen)
-    expert_range = jnp.arange(EXPERTS, dtype=jnp.int32)
-    onehot = (
-        (chosen[None, None, :] == expert_range[:, None, None])
-        & (placed[None, None, :] == slot_range[None, :, None])
-    ).astype(jnp.bfloat16)
-    send_x = jnp.einsum("eca,ad->ecd", onehot, rows_x, preferred_element_type=jnp.float32).astype(
-        jnp.bfloat16
+    scaled = (weight_table[:, :, None] * own_grad.astype(jnp.float32)[None]).astype(jnp.bfloat16)
+    per_expert = jnp.concatenate(
+        [jnp.broadcast_to(own_rows[None], (EXPERTS,) + own_rows.shape), scaled], axis=1
     )
-    send_g = jnp.einsum("eca,ad->ecd", onehot, scaled, preferred_element_type=jnp.float32).astype(
-        jnp.bfloat16
-    )
-    send_x = jnp.repeat(send_x, group_len, axis=0)
-    send_g = jnp.repeat(send_g, group_len, axis=0)
-    got_both = dense_exchange(jnp.concatenate([send_x, send_g], axis=1), "col")
-    got_x, got_g = got_both[:, :slot_cap], got_both[:, slot_cap:]
-    inputs = got_x.reshape(-1, model_width)
-    grads = got_g.reshape(-1, model_width)
-    e_pre = jnp.dot(inputs, expert_in, preferred_element_type=jnp.float32)
+    payload = jnp.broadcast_to(
+        per_expert[:, None], (EXPERTS, group_len) + per_expert.shape[1:]
+    ).reshape(col_count, 2 * block_len, model_width)
+    got = lax.all_to_all(payload, "col", 0, 0, tiled=True)
+    got_flat = got.reshape(col_count * 2 * block_len, model_width)
+    pre_full = jnp.dot(got_flat, expert_in, preferred_element_type=jnp.float32)
+    gdot_full = jnp.dot(got_flat, expert_out.T, preferred_element_type=jnp.float32)
+    hid_units = expert_in.shape[1]
+    e_pre = pre_full.reshape(col_count, 2 * block_len, hid_units)[:, :block_len]
+    g_dot = gdot_full.reshape(col_count, 2 * block_len, hid_units)[:, block_len:]
     e_hidden = gelu_tanh(e_pre).astype(jnp.bfloat16)
-    values = jnp.dot(e_hidden, expert_out, preferred_element_type=jnp.float32)
-    e_dpre = (
-        jnp.dot(grads, expert_out.T, preferred_element_type=jnp.float32) * gelu_slope(e_pre)
-    ).astype(jnp.bfloat16)
-    returns = jnp.dot(e_dpre, expert_in.T, preferred_element_type=jnp.float32)
-    grad_in = jnp.dot(inputs.T, e_dpre, preferred_element_type=jnp.float32)
-    grad_out = jnp.dot(e_hidden.T, grads, preferred_element_type=jnp.float32)
-    values, returns, grad_in, grad_out = (values, returns, grad_in, grad_out)
-    back_both = dense_exchange(
-        jnp.concatenate(
-            [
-                values.reshape(col_count, slot_cap, model_width).astype(jnp.bfloat16),
-                returns.reshape(col_count, slot_cap, model_width).astype(jnp.bfloat16),
-            ],
-            axis=1,
-        ),
+    e_dpre = (g_dot * gelu_slope(e_pre)).astype(jnp.bfloat16)
+    blank = jnp.zeros_like(e_hidden)
+
+    def at_rows(value, first):
+        halves = [value, blank] if first else [blank, value]
+        return jnp.concatenate(halves, axis=1).reshape(col_count * 2 * block_len, hid_units)
+
+    back_flat = jnp.dot(
+        at_rows(e_hidden, True), expert_out, preferred_element_type=jnp.float32
+    ) + jnp.dot(at_rows(e_dpre, False), expert_in.T, preferred_element_type=jnp.float32)
+    grad_in = jnp.dot(got_flat.T, at_rows(e_dpre, True), preferred_element_type=jnp.float32)
+    grad_out = jnp.dot(at_rows(e_hidden, False).T, got_flat, preferred_element_type=jnp.float32)
+    back = lax.all_to_all(
+        back_flat.astype(jnp.bfloat16).reshape(col_count, 2 * block_len, model_width),
         "col",
+        0,
+        0,
+        tiled=True,
     ).astype(jnp.float32)
-    back_v, back_d = back_both[:, :slot_cap], back_both[:, slot_cap:]
-    flat_v = (
-        back_v.reshape(EXPERTS, group_len, slot_cap, model_width)
-        .sum(axis=1)
-        .reshape(EXPERTS * slot_cap, model_width)
-    )
-    flat_d = (
-        back_d.reshape(EXPERTS, group_len, slot_cap, model_width)
-        .sum(axis=1)
-        .reshape(EXPERTS * slot_cap, model_width)
-    )
-    lookup = chosen * slot_cap + placed
-    moe_sum = (
-        (weights_flat[:, None] * jnp.take(flat_v, lookup, axis=0))
-        .reshape(block_len, 2, model_width)
-        .sum(axis=1)
-    )
-    grad_sum = jnp.take(flat_d, lookup, axis=0).reshape(block_len, 2, model_width).sum(axis=1)
+    source_weights = jnp.repeat(weight_table, group_len, axis=0)
+    moe_sum = jnp.sum(source_weights[:, :, None] * back[:, :block_len], axis=0)
+    grad_sum = jnp.sum(back[:, block_len:], axis=0)
     layer_rows = (own_rows.astype(jnp.float32) + moe_sum).astype(jnp.bfloat16)
     grad_rows = (own_grad.astype(jnp.float32) + grad_sum).astype(jnp.bfloat16)
     out_both = unswap_blocks(jnp.stack([layer_rows, grad_rows]), row_count)

time: 546 us -> 518 us (0.949)
  local copies, waits for them, and re-layouts: 64.5 us -> 15.3 us
  blocking collectives: 267 us -> 286 us
  waiting for transfers between devices: 120 us -> 136 us
  other arithmetic: 26.5 us -> 16.5 us
    reshape x10 -> x0, local copies, waits for them, and re-layouts: 26 us -> none  [the longest x2 10.3 us: dense_exchange(): flat = payload.reshape(shape[0], -1, 128)]
    all_to_all x1, blocking collectives: 62.6 us -> 78.6 us  [on_device(): got = lax.all_to_all(payload, 'col', 0, 0, tiled=True)]
    convert_element_type x8 -> x0, local copies, waits for them, and re-layouts: 14.9 us -> none  [the longest x1 5.98 us: on_device(): back_both = dense_exchange(jnp.concatenate([values.reshape(col_count, slo...]
    all_to_all x1, waiting for transfers between devices: 50.7 us -> 64.8 us  [on_device(): lax.all_to_all(back_flat.astype(jnp.bfloat16).reshape(col_count, 2 * bloc...]
    concatenate x2 -> x1, other arithmetic: 6.66 us -> 0.2 us  [on_device(): jnp.concatenate([jnp.broadcast_to(own_rows[None], (EXPERTS,) + own_rows.s...]
    slice x1 -> x0, local copies, waits for them, and re-layouts: 6.27 us -> none  [on_device(): got_x, got_g = (got_both[:, :slot_cap], got_both[:, slot_cap:])]
    reduce_sum x4 -> x2, other arithmetic: 7.14 us -> 1.49 us  [the longest x1 1.48 us: on_device(): moe_sum = jnp.sum(source_weights[:, :, None] * back[:, :block_len], axis=0)]
    dot_general x8 -> x6, matrix products: 18.2 us -> 16.1 us  [the longest x1 4.95 us: on_device(): jnp.dot(at_rows(e_hidden, False).T, got_flat, preferred_element_type=jnp....]
  transfers between devices with their start and end apart: 6 -> 6, of which waited for: 4 -> 4; matrix products, arithmetic and copies ran while one was open for 11% -> 6% of each run, Pallas kernels for 0% -> 0%
where the time goes in v4:
time: 518 us; the launch traced here: 517 us
  blocking collectives  286 us (55%)
  waiting for transfers between devices  136 us (26%)
  matrix products  29.5 us (6%)
  starting transfers between devices  19.6 us (4%)
  other arithmetic  16.5 us (3%)
  local copies, waits for them, and re-layouts  15.3 us (3%)
  between operations  14.4 us (3%)
    all_to_all x4, blocking collectives, gather_rows(): got = lax.all_to_all(spread, axis_name, 0, 0, tiled=True)  149 us
    all_to_all x1, blocking collectives, on_device(): got = lax.all_to_all(payload, 'col', 0, 0, tiled=True)  78.6 us
    all_to_all x2, waiting for transfers between devices, scatter_sum(): got = lax.all_to_all(blocks, axis_name, 0, 0, tiled=True)  65 us
    all_to_all x1, waiting for transfers between devices, on_device(): lax.all_to_all(back_flat.astype(jnp.bfloat16).reshape(col_count, 2 * bloc...  64.8 us
    all_to_all x2, blocking collectives, scatter_sum(): got = lax.all_to_all(blocks, axis_name, 0, 0, tiled=True)  49.7 us
  transfers between devices with their start and end apart: 6, of which 4 were waited for; matrix products, arithmetic and copies ran while one was open for 6% of the time, Pallas kernels for 0%

profile of v4, /device:TPU:32, one launch (start us, length us, event | category | flops | bytes accessed | tf_op | source)
XLA Modules:
  0.0 516.8 jit_solution(16030573045462857032)
XLA Ops:
  7.2 1.1 broadcast_in_dim.16
  8.3 51.4 %all_to_all.60 = bf16[32,32,768]{2,1,0:T(8,128)(2,1)S(1)} all-to-all(bf16[32,32,768]{2,1,0:T(8,128)(2,1)S(1)} %broadcast_in_dim.16), channel_id=1, replica_groups=mesh['row'=8,'col'=32] {'col'}, dimensions={0} | all-to-all | bytes 3145728 | tf_op jit(solution)/shard_map/all_to_all | solution.py:35
  59.7 1.4 convolution_convert_fusion.3
  61.1 25.7 %all_to_all.61 = bf16[8,128,768]{2,1,0:T(8,128)(2,1)S(1)} all-to-all(bf16[8,128,768]{2,1,0:T(8,128)(2,1)S(1)} %bitcast.78), channel_id=1, replica_groups=mesh['row'=8,'col'=32] {'row'}, dimensions={0} | all-to-all | bytes 3145728 | tf_op jit(solution)/shard_map/all_to_all | solution.py:42
  87.3 24.2 %all_to_all.62 = bf16[8,128,768]{2,1,0:T(8,128)(2,1)S(1)} all-to-all(bf16[8,128,768]{2,1,0:T(8,128)(2,1)S(1)} %broadcast_in_dim.17), channel_id=1, replica_groups=mesh['row'=8,'col'=32] {'row'}, dimensions={0} | all-to-all | bytes 3145728 | tf_op jit(solution)/shard_map/all_to_all | solution.py:35
  111.5 2.5 convolution_convert_fusion.2
  114.0 5.0 all-to-all-start.3
  119.0 1.4 stack.15
  120.6 37.5 %all-to-all-done.3 = bf16[32,32,768]{2,1,0:T(8,128)(2,1)} async-done(((bf16[32,32,768]{2,1,0:T(8,128)(2,1)}), bf16[32,32,768]{2,1,0:T(8,128)(2,1)}, u32[]{:S(2)}, u32[]{:S(2)}) %all-to-all-start.3) | async-done | bytes 1572896 | tf_op jit(solution)/shard_map/all_to_all | solution.py:42
  158.2 1.6 convert_reduce_fusion.2
  160.5 1.4 stack.14
  161.9 0.9 maximum_bitcast_fusion
  162.8 0.7 copy.71
  163.5 4.0 all-to-all-start.4
  167.5 5.7 %all-to-all-done.4 = bf16[8,8,768]{2,1,0:T(8,128)(2,1)} async-done(((bf16[8,8,768]{2,1,0:T(8,128)(2,1)}), bf16[8,8,768]{2,1,0:T(8,128)(2,1)}, u32[]{:S(2)}, u32[]{:S(2)}) %all-to-all-start.4) | async-done | bytes 98336 | tf_op jit(solution)/shard_map/all_to_all | solution.py:63
  173.3 1.6 reshape.141
  174.8 0.8 fusion.35
  176.4 78.6 %all_to_all.63 = bf16[32,8,6144]{2,1,0:T(8,128)(2,1)S(1)} all-to-all(bf16[32,8,6144]{2,1,0:T(8,128)(2,1)S(1)} %bitcast.68), channel_id=1, replica_groups=mesh['row'=8,'col'=32] {'col'}, dimensions={0} | all-to-all | bytes 6291456 | tf_op jit(solution)/shard_map/all_to_all | solution.py:110
  255.1 1.6 fusion.7
  256.7 1.4 copy-done.4
  258.1 1.0 fusion.9
  259.1 0.7 fusion.28
  260.4 5.0 fusion.4
  265.4 0.9 copy.88
  266.3 0.9 copy.89
  267.2 1.0 fusion.30
  268.3 0.9 copy-done.5
  269.1 2.7 fusion.5
  271.8 5.5 %all-to-all-start.6 = ((bf16[32,8,6144]{2,1,0:T(8,128)(2,1)}), bf16[32,8,6144]{2,1,0:T(8,128)(2,1)}, u32[]{:S(2)}, u32[]{:S(2)}) async-start(bf16[32,8,6144]{2,1,0:T(8,128)(2,1)} %fusion.5), calls=%async_computation.6 | async-start | bytes 6291456 | tf_op jit(solution)/shard_map/all_to_all | solution.py:130
  277.4 4.8 fusion.1
  282.3 64.8 %all-to-all-done.6 = bf16[32,8,6144]{2,1,0:T(8,128)(2,1)} async-done(((bf16[32,8,6144]{2,1,0:T(8,128)(2,1)}), bf16[32,8,6144]{2,1,0:T(8,128)(2,1)}, u32[]{:S(2)}, u32[]{:S(2)}) %all-to-all-start.6) | async-done | bytes 3145760 | tf_op jit(solution)/shard_map/all_to_all | solution.py:130
  347.1 2.7 convert_element_type.141
  349.8 1.5 fusion.6
  351.4 8.2 %all_to_all.64 = bf16[8,8,768]{2,1,0:T(8,128)(2,1)S(1)} all-to-all(bf16[8,8,768]{2,1,0:T(8,128)(2,1)S(1)} %reshape.146), channel_id=1, replica_groups=mesh['row'=8,'col'=32] {'row'}, dimensions={0} | all-to-all | bytes 196608 | tf_op jit(solution)/shard_map/all_to_all | solution.py:72
  361.1 49.6 %all_to_all.65 = bf16[32,32,768]{2,1,0:T(8,128)(2,1)S(1)} all-to-all(bf16[32,32,768]{2,1,0:T(8,128)(2,1)S(1)} %broadcast_in_dim.22), channel_id=1, replica_groups=mesh['row'=8,'col'=32] {'col'}, dimensions={0} | all-to-all | bytes 3145728 | tf_op jit(solution)/shard_map/all_to_all | solution.py:35
  410.7 1.4 convolution_convert_fusion.1
  412.2 24.0 %all_to_all.66 = bf16[8,128,768]{2,1,0:T(8,128)(2,1)S(1)} all-to-all(bf16[8,128,768]{2,1,0:T(8,128)(2,1)S(1)} %bitcast.79), channel_id=1, replica_groups=mesh['row'=8,'col'=32] {'row'}, dimensions={0} | all-to-all | bytes 3145728 | tf_op jit(solution)/shard_map/all_to_all | solution.py:42
  436.8 24.2 %all_to_all.67 = bf16[8,128,768]{2,1,0:T(8,128)(2,1)S(1)} all-to-all(bf16[8,128,768]{2,1,0:T(8,128)(2,1)S(1)} %broadcast_in_dim.23), channel_id=1, replica_groups=mesh['row'=8,'col'=32] {'row'}, dimensions={0} | all-to-all | bytes 3145728 | tf_op jit(solution)/shard_map/all_to_all | solution.py:35
  461.0 2.6 convolution_convert_fusion
  463.6 5.0 all-to-all-start.11
  468.6 0.6 squeeze.8
  469.3 4.0 convolution_convert_fusion.4
  473.3 1.5 fusion.14
  474.8 1.5 copy.83
  476.2 2.1 convert_element_type.160
  478.3 1.9 convert_element_type.157
  480.2 27.5 %all-to-all-done.11 = bf16[32,32,768]{2,1,0:T(8,128)(2,1)} async-done(((bf16[32,32,768]{2,1,0:T(8,128)(2,1)}), bf16[32,32,768]{2,1,0:T(8,128)(2,1)}, u32[]{:S(2)}, u32[]{:S(2)}) %all-to-all-start.11) | async-done | bytes 1572896 | tf_op jit(solution)/shard_map/all_to_all | solution.py:42
  507.7 1.6 convert_reduce_fusion
  (82 shorter events, 5.7 us)
Async XLA Ops:
  7.2 247.9 %copy-start = (bf16[256,6144]{1,0:T(8,128)(2,1)S(1)}, bf16[256,6144]{1,0:T(8,128)(2,1)}, u32[]{:S(2)}) copy-start(bf16[256,6144]{1,0:T(8,128)(2,1)} %param.12) | copy-start | bytes 9437188
  8.3 51.4 %copy-start.24 = (bf16[768,768]{1,0:T(8,128)(2,1)S(1)}, bf16[768,768]{1,0:T(8,128)(2,1)}, u32[]{:S(2)}) copy-start(bf16[768,768]{1,0:T(8,128)(2,1)} %param.9) | copy-start | bytes 3538948
  59.7 1.4 copy-start.6
  87.3 24.2 %copy-start.22 = (bf16[768,768]{1,0:T(8,128)(2,1)S(1)}, bf16[768,768]{1,0:T(8,128)(2,1)}, u32[]{:S(2)}) copy-start(bf16[768,768]{1,0:T(8,128)(2,1)} %param.10) | copy-start | bytes 3538948
  111.5 2.5 copy-start.8
  114.0 6.5 %copy-start.20 = (s32[32,2]{0,1:T(2,128)S(1)}, s32[32,2]{0,1:T(2,128)}, u32[]{:S(2)}) copy-start(s32[32,2]{0,1:T(2,128)} %param.13) | copy-start | bytes 772
  114.0 6.6 %copy-start.21 = (bf16[32,2]{0,1:T(2,128)(2,1)S(1)}, bf16[32,2]{0,1:T(2,128)(2,1)}, u32[]{:S(2)}) copy-start(bf16[32,2]{0,1:T(2,128)(2,1)} %param.14) | copy-start | bytes 388
  114.0 44.2 %all-to-all-start.3 = ((bf16[32,32,768]{2,1,0:T(8,128)(2,1)}), bf16[32,32,768]{2,1,0:T(8,128)(2,1)}, u32[]{:S(2)}, u32[]{:S(2)}) async-start(bf16[32,32,768]{2,1,0:T(8,128)(2,1)} %bitcast.73), calls=%async_computation.3 | async-start | bytes 3145728 | tf_op jit(solution)/shard_map/all_to_all | solution.py:42
  158.2 1.7 copy-start.18
  163.5 9.8 %all-to-all-start.4 = ((bf16[8,8,768]{2,1,0:T(8,128)(2,1)}), bf16[8,8,768]{2,1,0:T(8,128)(2,1)}, u32[]{:S(2)}, u32[]{:S(2)}) async-start(bf16[8,8,768]{2,1,0:T(8,128)(2,1)} %copy.71), calls=%async_computation.4 | async-start | bytes 196608 | tf_op jit(solution)/shard_map/all_to_all | solution.py:63
  167.5 308.7 %reduce-scatter.5.cloned.1.call-start = ((), (), s32[]{:S(2)}) async-start(), calls=%async_computation.15 | async-start | bytes 7077888 | tf_op jit(solution)/shard_map/reduce_scatter | solution.py:147
  255.0 4.8 copy-start.2
  255.1 3.0 copy-start.4
  259.8 0.6 copy-start.14
  267.2 1.0 copy-start.17
  267.2 1.9 copy-start.5
  271.8 5.6 %copy-start.3 = (bf16[32,8,6144]{2,1,0:T(8,128)(2,1)S(1)}, bf16[32,8,6144]{2,1,0:T(8,128)(2,1)}, u32[]{:S(2)}) copy-start(bf16[32,8,6144]{2,1,0:T(8,128)(2,1)} %copy-done.2) | copy-start | bytes 9437188
  271.8 75.2 %all-to-all-start.6 = ((bf16[32,8,6144]{2,1,0:T(8,128)(2,1)}), bf16[32,8,6144]{2,1,0:T(8,128)(2,1)}, u32[]{:S(2)}, u32[]{:S(2)}) async-start(bf16[32,8,6144]{2,1,0:T(8,128)(2,1)} %fusion.5), calls=%async_computation.6 | async-start | bytes 6291456 | tf_op jit(solution)/shard_map/all_to_all | solution.py:130
  277.3 200.9 %reduce-scatter.3.cloned.1.call-start = ((), (), s32[]{:S(2)}) async-start(), calls=%async_computation.14 | async-start | bytes 7077888 | tf_op jit(solution)/shard_map/reduce_scatter | solution.py:144
  349.8 1.5 copy-start.13
  360.3 0.6 copy-start.15
  361.1 49.6 %copy-start.23 = (bf16[768,768]{1,0:T(8,128)(2,1)S(1)}, bf16[768,768]{1,0:T(8,128)(2,1)}, u32[]{:S(2)}) copy-start(bf16[768,768]{1,0:T(8,128)(2,1)} %param.10) | copy-start | bytes 3538948
  410.7 1.4 copy-start.10
  436.8 24.2 %copy-start.25 = (bf16[768,768]{1,0:T(8,128)(2,1)S(1)}, bf16[768,768]{1,0:T(8,128)(2,1)}, u32[]{:S(2)}) copy-start(bf16[768,768]{1,0:T(8,128)(2,1)} %param.9) | copy-start | bytes 3538948
  461.0 2.6 copy-start.11
  463.6 5.0 copy-start.19
  463.6 5.7 %copy-start.9 = (bf16[8,128,768]{2,1,0:T(8,128)(2,1)S(1)}, bf16[8,128,768]{2,1,0:T(8,128)(2,1)}, u32[]{:S(2)}) copy-start(bf16[8,128,768]{2,1,0:T(8,128)(2,1)} %copy-done.8) | copy-start | bytes 4718596
  463.6 44.2 %all-to-all-start.11 = ((bf16[32,32,768]{2,1,0:T(8,128)(2,1)}), bf16[32,32,768]{2,1,0:T(8,128)(2,1)}, u32[]{:S(2)}, u32[]{:S(2)}) async-start(bf16[32,32,768]{2,1,0:T(8,128)(2,1)} %bitcast.25), calls=%async_computation.11 | async-start | bytes 3145728 | tf_op jit(solution)/shard_map/all_to_all | solution.py:42
  469.3 4.0 copy-start.7
  469.3 4.0 copy-start.12
  476.2 33.8 %copy-start.1 = (bf16[256,6144]{1,0:T(8,128)(2,1)S(1)}, bf16[256,6144]{1,0:T(8,128)(2,1)}, u32[]{:S(2)}) copy-start(bf16[256,6144]{1,0:T(8,128)(2,1)} %param.12) | copy-start | bytes 9437188
  478.3 31.1 %copy-start.16 = (bf16[32,768]{1,0:T(8,128)(2,1)S(1)}, bf16[32,768]{1,0:T(8,128)(2,1)}, u32[]{:S(2)}) copy-start(bf16[32,768]{1,0:T(8,128)(2,1)} %copy-done.15) | copy-start | bytes 147460
Sparse Core Ops, SparseCore 0:
  265.5 40.4 reduce-scatter.4
  308.6 45.5 reduce-scatter.2

commit v5 on v4

--- a/solution.py
+++ b/solution.py
@@ -84,14 +84,7 @@
     model_width = expert_out.shape[1]
     my_row = lax.axis_index("row")
     tok_panel = gather_rows(tokens, "col")
-    up_terms = jnp.dot(tok_panel, w_up, preferred_element_type=jnp.float32)
-    preact = scatter_sum(up_terms, "row")
-    hidden_full = gather_rows(gelu_tanh(preact).astype(jnp.bfloat16), "row")
-    rows_in = hidden_full
-    dense_term = scatter_sum(jnp.dot(rows_in, w_down, preferred_element_type=jnp.float32), "col")
-    mixed_act = (tokens.astype(jnp.float32) + dense_term).astype(jnp.bfloat16)
-    own_both = swap_blocks(jnp.stack([mixed_act, out_grad]), row_count)
-    own_rows, own_grad = own_both[0], own_both[1]
+    own_grad = swap_blocks(out_grad[None], row_count)[0]
     ids_own = lax.dynamic_slice_in_dim(expert_ids, my_row * block_len, block_len, 0)
     weights_own = lax.dynamic_slice_in_dim(route_weights, my_row * block_len, block_len, 0)
     expert_range = jnp.arange(EXPERTS, dtype=jnp.int32)
@@ -100,20 +93,38 @@
         * (ids_own[None, :, :] == expert_range[:, None, None]).astype(jnp.float32),
         axis=2,
     )
-    scaled = (weight_table[:, :, None] * own_grad.astype(jnp.float32)[None]).astype(jnp.bfloat16)
-    per_expert = jnp.concatenate(
-        [jnp.broadcast_to(own_rows[None], (EXPERTS,) + own_rows.shape), scaled], axis=1
-    )
-    payload = jnp.broadcast_to(
-        per_expert[:, None], (EXPERTS, group_len) + per_expert.shape[1:]
-    ).reshape(col_count, 2 * block_len, model_width)
+    table_row = jnp.pad(
+        weight_table.reshape(1, EXPERTS * block_len).astype(jnp.bfloat16),
+        ((0, 0), (0, model_width - EXPERTS * block_len)),
+    )
+    grad_pack = jnp.concatenate([own_grad, table_row], axis=0)
+    tok_panel, grad_pack = lax.optimization_barrier((tok_panel, grad_pack))
+    pack_all = lax.all_gather(grad_pack, "col", axis=0, tiled=False)
+    my_expert = lax.axis_index("col") // group_len
+    weights_recv = lax.dynamic_slice_in_dim(
+        pack_all[:, block_len, : EXPERTS * block_len], my_expert * block_len, block_len, 1
+    )
+    grad_rows_in = (
+        weights_recv.astype(jnp.float32)[:, :, None] * pack_all[:, :block_len].astype(jnp.float32)
+    ).astype(jnp.bfloat16)
+    up_terms = jnp.dot(tok_panel, w_up, preferred_element_type=jnp.float32)
+    preact = scatter_sum(up_terms, "row")
+    hidden_full = gather_rows(gelu_tanh(preact).astype(jnp.bfloat16), "row")
+    rows_in = hidden_full
+    dense_term = scatter_sum(jnp.dot(rows_in, w_down, preferred_element_type=jnp.float32), "col")
+    mixed_act = (tokens.astype(jnp.float32) + dense_term).astype(jnp.bfloat16)
+    own_rows = swap_blocks(mixed_act[None], row_count)[0]
+    scaled_flat = grad_rows_in.reshape(col_count * block_len, model_width)
+    payload = jnp.broadcast_to(own_rows[None], (col_count,) + own_rows.shape)
     got = lax.all_to_all(payload, "col", 0, 0, tiled=True)
-    got_flat = got.reshape(col_count * 2 * block_len, model_width)
-    pre_full = jnp.dot(got_flat, expert_in, preferred_element_type=jnp.float32)
-    gdot_full = jnp.dot(got_flat, expert_out.T, preferred_element_type=jnp.float32)
+    got_flat = got.reshape(col_count * block_len, model_width)
     hid_units = expert_in.shape[1]
-    e_pre = pre_full.reshape(col_count, 2 * block_len, hid_units)[:, :block_len]
-    g_dot = gdot_full.reshape(col_count, 2 * block_len, hid_units)[:, block_len:]
+    e_pre = jnp.dot(got_flat, expert_in, preferred_element_type=jnp.float32).reshape(
+        col_count, block_len, hid_units
+    )
+    g_dot = jnp.dot(scaled_flat, expert_out.T, preferred_element_type=jnp.float32).reshape(
+        col_count, block_len, hid_units
+    )
     e_hidden = gelu_tanh(e_pre).astype(jnp.bfloat16)
     e_dpre = (g_dot * gelu_slope(e_pre)).astype(jnp.bfloat16)
     blank = jnp.zeros_like(e_hidden)
@@ -125,8 +136,12 @@
     back_flat = jnp.dot(
         at_rows(e_hidden, True), expert_out, preferred_element_type=jnp.float32
     ) + jnp.dot(at_rows(e_dpre, False), expert_in.T, preferred_element_type=jnp.float32)
-    grad_in = jnp.dot(got_flat.T, at_rows(e_dpre, True), preferred_element_type=jnp.float32)
-    grad_out = jnp.dot(at_rows(e_hidden, False).T, got_flat, preferred_element_type=jnp.float32)
+    grad_in = jnp.dot(
+        got_flat.T, e_dpre.reshape(col_count * block_len, hid_units), preferred_element_type=jnp.float32
+    )
+    grad_out = jnp.dot(
+        e_hidden.reshape(col_count * block_len, hid_units).T, scaled_flat, preferred_element_type=jnp.float32
+    )
     back = lax.all_to_all(
         back_flat.astype(jnp.bfloat16).reshape(col_count, 2 * block_len, model_width),
         "col",

time: 518 us -> 505 us (0.975)
  blocking collectives: 286 us -> 172 us
  waiting for transfers between devices: 136 us -> 216 us
  starting transfers between devices: 19.6 us -> 34.4 us
  matrix products: 29.5 us -> 36.7 us
    all_to_all x1 -> x2, blocking collectives: 78.6 us -> 18.4 us  [swap_blocks(): lax.all_to_all(parts.reshape(count, arrays * block, width), 'row', 0, 0,...]
    all_to_all x4 -> x3, blocking collectives: 149 us -> 95 us  [gather_rows(): got = lax.all_to_all(spread, axis_name, 0, 0, tiled=True)]
    all_gather x0 -> x1, waiting for transfers between devices: none -> 40.8 us  [on_device(): pack_all = lax.all_gather(grad_pack, 'col', axis=0, tiled=False)]
    all_to_all x1 -> x2, waiting for transfers between devices: 5.73 us -> 39.9 us  [the longest x1 37.6 us: gather_rows(): got = lax.all_to_all(spread, axis_name, 0, 0, tiled=True)]
    all_to_all x1 -> x2, starting transfers between devices: 3.98 us -> 17.2 us  [the longest x1 11.5 us: gather_rows(): got = lax.all_to_all(spread, axis_name, 0, 0, tiled=True)]
  transfers between devices with their start and end apart: 6 -> 8, of which waited for: 4 -> 6; matrix products, arithmetic and copies ran while one was open for 6% -> 9% of each run, Pallas kernels for 0% -> 0%
where the time goes in v5:
time: 505 us; the launch traced here: 504 us
  waiting for transfers between devices  216 us (43%)
  blocking collectives  172 us (34%)
  matrix products  36.7 us (7%)
  starting transfers between devices  34.4 us (7%)
  local copies, waits for them, and re-layouts  18.5 us (4%)
  between operations  14.1 us (3%)
  other arithmetic  12.5 us (2%)
    all_to_all x3, blocking collectives, gather_rows(): got = lax.all_to_all(spread, axis_name, 0, 0, tiled=True)  95 us
    all_to_all x2, waiting for transfers between devices, scatter_sum(): got = lax.all_to_all(blocks, axis_name, 0, 0, tiled=True)  69.5 us
    all_to_all x1, waiting for transfers between devices, on_device(): lax.all_to_all(back_flat.astype(jnp.bfloat16).reshape(col_count, 2 * bloc...  64.5 us
    all_to_all x2, blocking collectives, scatter_sum(): got = lax.all_to_all(blocks, axis_name, 0, 0, tiled=True)  48 us
    all_gather x1, waiting for transfers between devices, on_device(): pack_all = lax.all_gather(grad_pack, 'col', axis=0, tiled=False)  40.8 us
    all_to_all x1, waiting for transfers between devices, gather_rows(): got = lax.all_to_all(spread, axis_name, 0, 0, tiled=True)  37.6 us
    all_to_all x2, blocking collectives, swap_blocks(): lax.all_to_all(parts.reshape(count, arrays * block, width), 'row', 0, 0,...  18.4 us
    all_to_all x1, starting transfers between devices, gather_rows(): got = lax.all_to_all(spread, axis_name, 0, 0, tiled=True)  11.5 us
  transfers between devices with their start and end apart: 8, of which 6 were waited for; matrix products, arithmetic and copies ran while one was open for 9% of the time, Pallas kernels for 0%

profile of v5, /device:TPU:32, one launch (start us, length us, event | category | flops | bytes accessed | tf_op | source)
XLA Modules:
  0.0 503.9 jit_solution(9389533836339593974)
XLA Ops:
  7.2 1.0 reshape_transpose_reshape_broadcast_in_dim.6
  8.1 9.6 %all_to_all.65 = bf16[8,4,768]{2,1,0:T(4,128)(2,1)S(1)} all-to-all(bf16[8,4,768]{2,1,0:T(4,128)(2,1)S(1)} %reshape_transpose_reshape_broadcast_in_dim.6), channel_id=1, replica_groups=mesh['row'=8,'col'=32] {'row'}, dimensions={0} | all-to-all | bytes 98304 | tf_op jit(solution)/shard_map/all_to_all | solution.py:63
  17.8 2.2 broadcast_in_dim.14
  20.0 11.5 %all-to-all-start = ((bf16[32,32,768]{2,1,0:T(8,128)(2,1)}), bf16[32,32,768]{2,1,0:T(8,128)(2,1)}, u32[]{:S(2)}, u32[]{:S(2)}) async-start(bf16[32,32,768]{2,1,0:T(8,128)(2,1)} %broadcast_in_dim.14), calls=%async_computation | async-start | bytes 3145728 | tf_op jit(solution)/shard_map/all_to_all | solution.py:35
  32.4 0.7 fusion.33
  33.0 37.6 %all-to-all-done = bf16[32,32,768]{2,1,0:T(8,128)(2,1)} async-done(((bf16[32,32,768]{2,1,0:T(8,128)(2,1)}), bf16[32,32,768]{2,1,0:T(8,128)(2,1)}, u32[]{:S(2)}, u32[]{:S(2)}) %all-to-all-start) | async-done | bytes 1572896 | tf_op jit(solution)/shard_map/all_to_all | solution.py:35
  70.7 3.1 convolution_convert_fusion.3
  73.8 24.0 %all_to_all.66 = bf16[8,128,768]{2,1,0:T(8,128)(2,1)S(1)} all-to-all(bf16[8,128,768]{2,1,0:T(8,128)(2,1)S(1)} %bitcast.89), channel_id=1, replica_groups=mesh['row'=8,'col'=32] {'row'}, dimensions={0} | all-to-all | bytes 3145728 | tf_op jit(solution)/shard_map/all_to_all | solution.py:42
  98.3 24.2 %all_to_all.67 = bf16[8,128,768]{2,1,0:T(8,128)(2,1)S(1)} all-to-all(bf16[8,128,768]{2,1,0:T(8,128)(2,1)S(1)} %broadcast_in_dim.15), channel_id=1, replica_groups=mesh['row'=8,'col'=32] {'row'}, dimensions={0} | all-to-all | bytes 3145728 | tf_op jit(solution)/shard_map/all_to_all | solution.py:35
  122.5 2.6 convolution_convert_fusion.2
  125.1 5.8 %all-to-all-start.4 = ((bf16[32,32,768]{2,1,0:T(8,128)(2,1)}), bf16[32,32,768]{2,1,0:T(8,128)(2,1)}, u32[]{:S(2)}, u32[]{:S(2)}) async-start(bf16[32,32,768]{2,1,0:T(8,128)(2,1)} %bitcast.88), calls=%async_computation.4 | async-start | bytes 3145728 | tf_op jit(solution)/shard_map/all_to_all | solution.py:42
  130.9 0.7 all-gather.4.cloned.1.call-update
  131.6 41.4 %all-to-all-done.4 = bf16[32,32,768]{2,1,0:T(8,128)(2,1)} async-done(((bf16[32,32,768]{2,1,0:T(8,128)(2,1)}), bf16[32,32,768]{2,1,0:T(8,128)(2,1)}, u32[]{:S(2)}, u32[]{:S(2)}) %all-to-all-start.4) | async-done | bytes 1572896 | tf_op jit(solution)/shard_map/all_to_all | solution.py:42
  173.0 1.7 convert_reduce_fusion.2
  175.3 1.4 reshape_transpose_reshape_broadcast_in_dim.7
  176.7 8.8 %all_to_all.68 = bf16[8,4,768]{2,1,0:T(4,128)(2,1)S(1)} all-to-all(bf16[8,4,768]{2,1,0:T(4,128)(2,1)} %reshape_transpose_reshape_broadcast_in_dim.7), channel_id=1, replica_groups=mesh['row'=8,'col'=32] {'row'}, dimensions={0} | all-to-all | bytes 98304 | tf_op jit(solution)/shard_map/all_to_all | solution.py:63
  186.1 1.9 broadcast_in_dim.18
  188.0 5.6 %all-to-all-start.6 = ((bf16[32,4,6144]{2,1,0:T(4,128)(2,1)}), bf16[32,4,6144]{2,1,0:T(4,128)(2,1)}, u32[]{:S(2)}, u32[]{:S(2)}) async-start(bf16[32,4,6144]{2,1,0:T(4,128)(2,1)} %broadcast_in_dim.18), calls=%async_computation.6 | async-start | bytes 3145728 | tf_op jit(solution)/shard_map/all_to_all | solution.py:119
  193.9 40.8 %all-gather.4.cloned.1.call-done = bf16[32,5,6144]{2,1,0:T(8,128)(2,1)} async-done(((bf16[1,5,6144]{2,1,0:T(8,128)(2,1)}), bf16[32,5,6144]{2,1,0:T(8,128)(2,1)}) %all-gather.4.cloned.1.call-update) | async-done | bytes 1966096 | tf_op jit(solution)/shard_map/all_gather | solution.py:102
  234.7 0.9 slice.26
  235.7 0.7 copy.90
  236.3 3.7 slice.27
  240.1 2.3 all-to-all-done.6
  242.3 3.4 multiply_convert_fusion.8
  246.4 4.1 fusion.4
  250.6 0.9 copy.93
  251.5 4.0 fusion.16
  256.2 1.0 fusion.32
  257.2 2.7 fusion.5
  259.9 6.1 %all-to-all-start.7 = ((bf16[32,8,6144]{2,1,0:T(8,128)(2,1)}), bf16[32,8,6144]{2,1,0:T(8,128)(2,1)S(1)}, u32[]{:S(2)}, u32[]{:S(2)}) async-start(bf16[32,8,6144]{2,1,0:T(8,128)(2,1)} %fusion.5), calls=%async_computation.7 | async-start | bytes 6291456 | tf_op jit(solution)/shard_map/all_to_all | solution.py:145
  266.0 5.4 %fusion.2 = f32[6144,256]{1,0:T(8,128)} fusion(bf16[32,4,256]{2,0,1:T(8,128)(2,1)} %copy-done.17, bf16[32,4,6144]{2,1,0:T(4,128)(2,1)} %all-to-all-done.6), kind=kOutput, calls=%fused_computation.5 | convolution fusion | flops 405798912 | bytes 7929856 | tf_op jit(solution)/shard_map/dot_general | solution.py:139
  271.4 0.7 broadcast_bitcast_fusion
  272.1 64.5 %all-to-all-done.7 = bf16[32,8,6144]{2,1,0:T(8,128)(2,1)S(1)} async-done(((bf16[32,8,6144]{2,1,0:T(8,128)(2,1)}), bf16[32,8,6144]{2,1,0:T(8,128)(2,1)S(1)}, u32[]{:S(2)}, u32[]{:S(2)}) %all-to-all-start.7) | async-done | bytes 3145760 | tf_op jit(solution)/shard_map/all_to_all | solution.py:145
  336.7 0.7 convert_element_type.160
  337.4 1.5 fusion.6
  339.1 10.8 %all_to_all.69 = bf16[8,8,768]{2,1,0:T(8,128)(2,1)S(1)} all-to-all(bf16[8,8,768]{2,1,0:T(8,128)(2,1)S(1)} %copy.83), channel_id=1, replica_groups=mesh['row'=8,'col'=32] {'row'}, dimensions={0} | all-to-all | bytes 196608 | tf_op jit(solution)/shard_map/all_to_all | solution.py:72
  351.4 46.7 %all_to_all.70 = bf16[32,32,768]{2,1,0:T(8,128)(2,1)S(1)} all-to-all(bf16[32,32,768]{2,1,0:T(8,128)(2,1)S(1)} %broadcast_in_dim.19), channel_id=1, replica_groups=mesh['row'=8,'col'=32] {'col'}, dimensions={0} | all-to-all | bytes 3145728 | tf_op jit(solution)/shard_map/all_to_all | solution.py:35
  398.1 1.4 convolution_convert_fusion.1
  399.6 24.0 %all_to_all.71 = bf16[8,128,768]{2,1,0:T(8,128)(2,1)S(1)} all-to-all(bf16[8,128,768]{2,1,0:T(8,128)(2,1)S(1)} %bitcast.90), channel_id=1, replica_groups=mesh['row'=8,'col'=32] {'row'}, dimensions={0} | all-to-all | bytes 3145728 | tf_op jit(solution)/shard_map/all_to_all | solution.py:42
  424.2 24.2 %all_to_all.72 = bf16[8,128,768]{2,1,0:T(8,128)(2,1)S(1)} all-to-all(bf16[8,128,768]{2,1,0:T(8,128)(2,1)S(1)} %broadcast_in_dim.20), channel_id=1, replica_groups=mesh['row'=8,'col'=32] {'row'}, dimensions={0} | all-to-all | bytes 3145728 | tf_op jit(solution)/shard_map/all_to_all | solution.py:35
  448.3 2.6 convolution_convert_fusion
  450.9 5.0 all-to-all-start.12
  456.6 2.5 convolution_convert_fusion.4
  459.1 3.9 convolution_convert_fusion.5
  463.0 2.1 convert_element_type.178
  465.1 1.9 convert_element_type.175
  467.0 28.1 %all-to-all-done.12 = bf16[32,32,768]{2,1,0:T(8,128)(2,1)} async-done(((bf16[32,32,768]{2,1,0:T(8,128)(2,1)}), bf16[32,32,768]{2,1,0:T(8,128)(2,1)}, u32[]{:S(2)}, u32[]{:S(2)}) %all-to-all-start.12) | async-done | bytes 1572896 | tf_op jit(solution)/shard_map/all_to_all | solution.py:42
  495.1 1.6 convert_reduce_fusion
  (84 shorter events, 7.9 us)
Async XLA Ops:
  7.2 235.2 %copy-start = (bf16[6144,256]{1,0:T(8,128)(2,1)S(1)}, bf16[6144,256]{1,0:T(8,128)(2,1)}, u32[]{:S(2)}) copy-start(bf16[6144,256]{1,0:T(8,128)(2,1)} %param.11) | copy-start | bytes 9437188
  17.8 14.6 %copy-start.12 = (bf16[8,4,768]{2,1,0:T(4,128)(2,1)}, bf16[8,4,768]{2,1,0:T(4,128)(2,1)S(1)}, u32[]{:S(2)}) copy-start(bf16[8,4,768]{2,1,0:T(4,128)(2,1)S(1)} %all_to_all.65) | copy-start | bytes 147460
  20.0 11.6 %copy-start.20 = (s32[32,2]{0,1:T(2,128)S(1)}, s32[32,2]{0,1:T(2,128)}, u32[]{:S(2)}) copy-start(s32[32,2]{0,1:T(2,128)} %param.13) | copy-start | bytes 772
  20.0 11.6 %copy-start.21 = (bf16[32,2]{0,1:T(2,128)(2,1)S(1)}, bf16[32,2]{0,1:T(2,128)(2,1)}, u32[]{:S(2)}) copy-start(bf16[32,2]{0,1:T(2,128)(2,1)} %param.14) | copy-start | bytes 388
  20.0 50.7 %all-to-all-start = ((bf16[32,32,768]{2,1,0:T(8,128)(2,1)}), bf16[32,32,768]{2,1,0:T(8,128)(2,1)}, u32[]{:S(2)}, u32[]{:S(2)}) async-start(bf16[32,32,768]{2,1,0:T(8,128)(2,1)} %broadcast_in_dim.14), calls=%async_computation | async-start | bytes 3145728 | tf_op jit(solution)/shard_map/all_to_all | solution.py:35
  31.7 0.6 copy-start.18
  98.3 24.2 %copy-start.22 = (bf16[768,768]{1,0:T(8,128)(2,1)S(1)}, bf16[768,768]{1,0:T(8,128)(2,1)}, u32[]{:S(2)}) copy-start(bf16[768,768]{1,0:T(8,128)(2,1)} %param.10) | copy-start | bytes 3538948
  122.5 2.6 copy-start.4
  125.1 48.0 %all-to-all-start.4 = ((bf16[32,32,768]{2,1,0:T(8,128)(2,1)}), bf16[32,32,768]{2,1,0:T(8,128)(2,1)}, u32[]{:S(2)}, u32[]{:S(2)}) async-start(bf16[32,32,768]{2,1,0:T(8,128)(2,1)} %bitcast.88), calls=%async_computation.4 | async-start | bytes 3145728 | tf_op jit(solution)/shard_map/all_to_all | solution.py:42
  130.9 103.9 %all-gather.4.cloned.1.call-start = ((), (), s32[]{:S(2)}) async-start(), calls=%async_computation.17 | async-start | bytes 3244032 | tf_op jit(solution)/shard_map/all_gather | solution.py:102
  173.0 1.7 copy-start.15
  185.5 0.6 copy-start.8
  188.0 54.3 %all-to-all-start.6 = ((bf16[32,4,6144]{2,1,0:T(4,128)(2,1)}), bf16[32,4,6144]{2,1,0:T(4,128)(2,1)}, u32[]{:S(2)}, u32[]{:S(2)}) async-start(bf16[32,4,6144]{2,1,0:T(4,128)(2,1)} %broadcast_in_dim.18), calls=%async_computation.6 | async-start | bytes 3145728 | tf_op jit(solution)/shard_map/all_to_all | solution.py:119
  193.6 269.3 %reduce-scatter.5.cloned.1.call-start = ((), (), s32[]{:S(2)}) async-start(), calls=%async_computation.16 | async-start | bytes 7077888 | tf_op jit(solution)/shard_map/reduce_scatter | solution.py:162
  236.3 3.7 copy-start.19
  242.3 4.1 copy-start.2
  245.8 0.6 copy-start.14
  251.5 4.7 copy-start.3
  255.5 0.6 copy-start.17
  259.9 76.8 %all-to-all-start.7 = ((bf16[32,8,6144]{2,1,0:T(8,128)(2,1)}), bf16[32,8,6144]{2,1,0:T(8,128)(2,1)S(1)}, u32[]{:S(2)}, u32[]{:S(2)}) async-start(bf16[32,8,6144]{2,1,0:T(8,128)(2,1)} %fusion.5), calls=%async_computation.7 | async-start | bytes 6291456 | tf_op jit(solution)/shard_map/all_to_all | solution.py:145
  266.0 199.1 %reduce-scatter.3.cloned.1.call-start = ((), (), s32[]{:S(2)}) async-start(), calls=%async_computation.15 | async-start | bytes 7077888 | tf_op jit(solution)/shard_map/reduce_scatter | solution.py:159
  337.4 1.5 copy-start.9
  337.4 1.5 copy-start.13
  350.6 0.6 copy-start.10
  351.4 46.7 %copy-start.23 = (bf16[768,768]{1,0:T(8,128)(2,1)S(1)}, bf16[768,768]{1,0:T(8,128)(2,1)}, u32[]{:S(2)}) copy-start(bf16[768,768]{1,0:T(8,128)(2,1)} %param.10) | copy-start | bytes 3538948
  424.2 24.2 %copy-start.24 = (bf16[768,768]{1,0:T(8,128)(2,1)S(1)}, bf16[768,768]{1,0:T(8,128)(2,1)}, u32[]{:S(2)}) copy-start(bf16[768,768]{1,0:T(8,128)(2,1)} %param.9) | copy-start | bytes 3538948
  448.3 2.6 copy-start.6
  450.9 5.0 %copy-start.16 = (bf16[1,8,4,768]{3,1,2,0:T(8,128)(2,1)S(1)}, bf16[1,8,4,768]{3,1,2,0:T(8,128)(2,1)}, u32[]{:S(2)}) copy-start(bf16[1,8,4,768]{3,1,2,0:T(8,128)(2,1)} %get-tuple-element.13) | copy-start | bytes 147460
  450.9 5.7 %copy-start.5 = (bf16[8,128,768]{2,1,0:T(8,128)(2,1)S(1)}, bf16[8,128,768]{2,1,0:T(8,128)(2,1)}, u32[]{:S(2)}) copy-start(bf16[8,128,768]{2,1,0:T(8,128)(2,1)} %copy-done.4) | copy-start | bytes 4718596
  450.9 44.2 %all-to-all-start.12 = ((bf16[32,32,768]{2,1,0:T(8,128)(2,1)}), bf16[32,32,768]{2,1,0:T(8,128)(2,1)}, u32[]{:S(2)}, u32[]{:S(2)}) async-start(bf16[32,32,768]{2,1,0:T(8,128)(2,1)} %bitcast.30), calls=%async_computation.12 | async-start | bytes 3145728 | tf_op jit(solution)/shard_map/all_to_all | solution.py:42
  456.6 2.5 copy-start.7
  463.0 34.4 %copy-start.1 = (bf16[6144,256]{1,0:T(8,128)(2,1)S(1)}, bf16[6144,256]{1,0:T(8,128)(2,1)}, u32[]{:S(2)}) copy-start(bf16[6144,256]{1,0:T(8,128)(2,1)} %param.11) | copy-start | bytes 9437188
  465.1 31.7 %copy-start.11 = (bf16[32,768]{1,0:T(8,128)(2,1)S(1)}, bf16[32,768]{1,0:T(8,128)(2,1)}, u32[]{:S(2)}) copy-start(bf16[32,768]{1,0:T(8,128)(2,1)} %copy-done.10) | copy-start | bytes 147460
Sparse Core Ops, SparseCore 0:
  134.8 99.8 all-gather.3
  250.7 45.6 reduce-scatter.4
  299.0 44.5 reduce-scatter.2

commit v6 on v5

--- a/solution.py
+++ b/solution.py
@@ -143,19 +143,27 @@
         e_hidden.reshape(col_count * block_len, hid_units).T, scaled_flat, preferred_element_type=jnp.float32
     )
     back = lax.all_to_all(
-        back_flat.astype(jnp.bfloat16).reshape(col_count, 2 * block_len, model_width),
-        "col",
+        back_flat.astype(jnp.bfloat16)
+        .reshape(col_count, 2 * block_len, row_count, model_width // row_count)
+        .transpose(2, 0, 1, 3)
+        .reshape(row_count * col_count, 2 * block_len, model_width // row_count),
+        ("row", "col"),
         0,
         0,
         tiled=True,
-    ).astype(jnp.float32)
-    source_weights = jnp.repeat(weight_table, group_len, axis=0)
-    moe_sum = jnp.sum(source_weights[:, :, None] * back[:, :block_len], axis=0)
-    grad_sum = jnp.sum(back[:, block_len:], axis=0)
-    layer_rows = (own_rows.astype(jnp.float32) + moe_sum).astype(jnp.bfloat16)
-    grad_rows = (own_grad.astype(jnp.float32) + grad_sum).astype(jnp.bfloat16)
-    out_both = unswap_blocks(jnp.stack([layer_rows, grad_rows]), row_count)
-    layer_out, mixed_grad = out_both[0], out_both[1]
+    ).astype(jnp.float32).reshape(row_count, col_count, 2 * block_len, model_width // row_count)
+    local_table = jnp.sum(
+        route_weights.astype(jnp.float32)[:, None, :]
+        * (expert_ids[:, None, :] == expert_range[None, :, None]).astype(jnp.float32),
+        axis=2,
+    )
+    source_weights = jnp.repeat(
+        local_table.reshape(row_count, block_len, EXPERTS).transpose(0, 2, 1), group_len, axis=1
+    )
+    moe_sum = jnp.sum(source_weights[:, :, :, None] * back[:, :, :block_len], axis=1)
+    grad_sum = jnp.sum(back[:, :, block_len:], axis=1)
+    layer_out = (mixed_act.astype(jnp.float32) + moe_sum.reshape(tok_col, -1)).astype(jnp.bfloat16)
+    mixed_grad = (out_grad.astype(jnp.float32) + grad_sum.reshape(tok_col, -1)).astype(jnp.bfloat16)
     expert_in_grad = lax.psum_scatter(
         grad_in.astype(jnp.bfloat16).astype(jnp.float32), "row", scatter_dimension=0, tiled=True
     ).astype(jnp.bfloat16)

time: 505 us -> 505 us (level)
  blocking collectives: 172 us -> 160 us
  starting transfers between devices: 34.4 us -> 41.7 us
    all_to_all x1 -> x0, blocking collectives: 10.8 us -> none  [unswap_blocks(): lax.all_to_all(parts.reshape(count, arrays * block, width), 'row', 0, 0,...]
    all_to_all x1, starting transfers between devices: 6.1 us -> 13.4 us  [on_device(): lax.all_to_all(back_flat.astype(jnp.bfloat16).reshape(col_count, 2 * bloc...]
where the time goes in v6:
time: 505 us; the launch traced here: 503 us
  waiting for transfers between devices  219 us (43%)
  blocking collectives  160 us (32%)
  starting transfers between devices  41.7 us (8%)
  matrix products  35.1 us (7%)
  local copies, waits for them, and re-layouts  19.5 us (4%)
  other arithmetic  14.2 us (3%)
  between operations  14.1 us (3%)
    all_to_all x3, blocking collectives, gather_rows(): got = lax.all_to_all(spread, axis_name, 0, 0, tiled=True)  93.3 us
    all_to_all x2, waiting for transfers between devices, scatter_sum(): got = lax.all_to_all(blocks, axis_name, 0, 0, tiled=True)  69.5 us
    all_to_all x1, waiting for transfers between devices, on_device(): lax.all_to_all(back_flat.astype(jnp.bfloat16).reshape(col_count, 2 * bloc...  67.2 us
    all_to_all x2, blocking collectives, scatter_sum(): got = lax.all_to_all(blocks, axis_name, 0, 0, tiled=True)  48.5 us
    all_gather x1, waiting for transfers between devices, on_device(): pack_all = lax.all_gather(grad_pack, 'col', axis=0, tiled=False)  41.5 us
    all_to_all x1, waiting for transfers between devices, gather_rows(): got = lax.all_to_all(spread, axis_name, 0, 0, tiled=True)  38.2 us
    all_to_all x2, blocking collectives, swap_blocks(): lax.all_to_all(parts.reshape(count, arrays * block, width), 'row', 0, 0,...  18.4 us
    all_to_all x1, starting transfers between devices, on_device(): lax.all_to_all(back_flat.astype(jnp.bfloat16).reshape(col_count, 2 * bloc...  13.4 us
  transfers between devices with their start and end apart: 8, of which 6 were waited for; matrix products, arithmetic and copies ran while one was open for 9% of the time, Pallas kernels for 0%

profile of v6, /device:TPU:32, one launch (start us, length us, event | category | flops | bytes accessed | tf_op | source)
XLA Modules:
  0.0 503.4 jit_solution(18288638706634828644)
XLA Ops:
  7.2 1.0 reshape_transpose_reshape_broadcast_in_dim.6
  8.2 9.6 %all_to_all.60 = bf16[8,4,768]{2,1,0:T(4,128)(2,1)S(1)} all-to-all(bf16[8,4,768]{2,1,0:T(4,128)(2,1)S(1)} %reshape_transpose_reshape_broadcast_in_dim.6), channel_id=1, replica_groups=mesh['row'=8,'col'=32] {'row'}, dimensions={0} | all-to-all | bytes 98304 | tf_op jit(solution)/shard_map/all_to_all | solution.py:63
  17.8 2.2 broadcast_in_dim.14
  19.9 11.5 %all-to-all-start = ((bf16[32,32,768]{2,1,0:T(8,128)(2,1)}), bf16[32,32,768]{2,1,0:T(8,128)(2,1)}, u32[]{:S(2)}, u32[]{:S(2)}) async-start(bf16[32,32,768]{2,1,0:T(8,128)(2,1)} %broadcast_in_dim.14), calls=%async_computation | async-start | bytes 3145728 | tf_op jit(solution)/shard_map/all_to_all | solution.py:35
  31.8 0.7 fusion.32
  32.4 38.2 %all-to-all-done = bf16[32,32,768]{2,1,0:T(8,128)(2,1)} async-done(((bf16[32,32,768]{2,1,0:T(8,128)(2,1)}), bf16[32,32,768]{2,1,0:T(8,128)(2,1)}, u32[]{:S(2)}, u32[]{:S(2)}) %all-to-all-start) | async-done | bytes 1572896 | tf_op jit(solution)/shard_map/all_to_all | solution.py:35
  70.7 3.1 convolution_convert_fusion.3
  73.8 24.0 %all_to_all.61 = bf16[8,128,768]{2,1,0:T(8,128)(2,1)S(1)} all-to-all(bf16[8,128,768]{2,1,0:T(8,128)(2,1)S(1)} %bitcast.88), channel_id=1, replica_groups=mesh['row'=8,'col'=32] {'row'}, dimensions={0} | all-to-all | bytes 3145728 | tf_op jit(solution)/shard_map/all_to_all | solution.py:42
  98.3 24.2 %all_to_all.62 = bf16[8,128,768]{2,1,0:T(8,128)(2,1)S(1)} all-to-all(bf16[8,128,768]{2,1,0:T(8,128)(2,1)S(1)} %broadcast_in_dim.15), channel_id=1, replica_groups=mesh['row'=8,'col'=32] {'row'}, dimensions={0} | all-to-all | bytes 3145728 | tf_op jit(solution)/shard_map/all_to_all | solution.py:35
  122.5 2.6 convolution_convert_fusion.2
  125.1 5.8 %all-to-all-start.4 = ((bf16[32,32,768]{2,1,0:T(8,128)(2,1)}), bf16[32,32,768]{2,1,0:T(8,128)(2,1)}, u32[]{:S(2)}, u32[]{:S(2)}) async-start(bf16[32,32,768]{2,1,0:T(8,128)(2,1)} %bitcast.87), calls=%async_computation.4 | async-start | bytes 3145728 | tf_op jit(solution)/shard_map/all_to_all | solution.py:42
  130.9 0.7 all-gather.4.cloned.1.call-update
  131.6 41.4 %all-to-all-done.4 = bf16[32,32,768]{2,1,0:T(8,128)(2,1)} async-done(((bf16[32,32,768]{2,1,0:T(8,128)(2,1)}), bf16[32,32,768]{2,1,0:T(8,128)(2,1)}, u32[]{:S(2)}, u32[]{:S(2)}) %all-to-all-start.4) | async-done | bytes 1572896 | tf_op jit(solution)/shard_map/all_to_all | solution.py:42
  173.0 1.7 convert_reduce_fusion.2
  175.3 1.4 reshape_transpose_reshape_broadcast_in_dim.7
  176.7 8.8 %all_to_all.63 = bf16[8,4,768]{2,1,0:T(4,128)(2,1)S(1)} all-to-all(bf16[8,4,768]{2,1,0:T(4,128)(2,1)} %reshape_transpose_reshape_broadcast_in_dim.7), channel_id=1, replica_groups=mesh['row'=8,'col'=32] {'row'}, dimensions={0} | all-to-all | bytes 98304 | tf_op jit(solution)/shard_map/all_to_all | solution.py:63
  185.5 1.9 broadcast_in_dim.18
  187.4 5.6 %all-to-all-start.6 = ((bf16[32,4,6144]{2,1,0:T(4,128)(2,1)}), bf16[32,4,6144]{2,1,0:T(4,128)(2,1)}, u32[]{:S(2)}, u32[]{:S(2)}) async-start(bf16[32,4,6144]{2,1,0:T(4,128)(2,1)} %broadcast_in_dim.18), calls=%async_computation.6 | async-start | bytes 3145728 | tf_op jit(solution)/shard_map/all_to_all | solution.py:119
  193.3 41.5 %all-gather.4.cloned.1.call-done = bf16[32,5,6144]{2,1,0:T(8,128)(2,1)} async-done(((bf16[1,5,6144]{2,1,0:T(8,128)(2,1)}), bf16[32,5,6144]{2,1,0:T(8,128)(2,1)}) %all-gather.4.cloned.1.call-update) | async-done | bytes 1966096 | tf_op jit(solution)/shard_map/all_gather | solution.py:102
  234.8 0.9 slice.16
  235.7 0.7 copy.67
  236.4 3.7 slice.17
  240.1 1.6 all-to-all-done.6
  241.7 3.4 multiply_convert_fusion.8
  245.7 4.2 fusion.4
  249.9 0.9 copy.69
  250.8 4.0 fusion.15
  255.4 1.0 fusion.31
  256.4 1.1 fusion
  257.5 1.8 copy.64
  259.4 13.4 %all-to-all-start.7 = ((bf16[256,8,768]{2,1,0:T(8,128)(2,1)}), bf16[256,8,768]{2,1,0:T(8,128)(2,1)S(1)}, u32[]{:S(2)}, u32[]{:S(2)}) async-start(bf16[256,8,768]{2,1,0:T(8,128)(2,1)} %bitcast.20), calls=%async_computation.7 | async-start | bytes 6291456 | tf_op jit(solution)/shard_map/all_to_all | solution.py:145
  272.8 5.5 %fusion.2 = f32[6144,256]{1,0:T(8,128)} fusion(bf16[32,4,256]{2,0,1:T(8,128)(2,1)} %copy-done.16, bf16[32,4,6144]{2,1,0:T(4,128)(2,1)} %all-to-all-done.6), kind=kOutput, calls=%fused_computation.5 | convolution fusion | flops 405798912 | bytes 7929856 | tf_op jit(solution)/shard_map/dot_general | solution.py:139
  279.5 0.8 reshape.142
  280.3 0.7 broadcast_bitcast_fusion
  281.0 67.2 %all-to-all-done.7 = bf16[256,8,768]{2,1,0:T(8,128)(2,1)S(1)} async-done(((bf16[256,8,768]{2,1,0:T(8,128)(2,1)}), bf16[256,8,768]{2,1,0:T(8,128)(2,1)S(1)}, u32[]{:S(2)}, u32[]{:S(2)}) %all-to-all-start.7) | async-done | bytes 3145760 | tf_op jit(solution)/shard_map/all_to_all | solution.py:145
  349.1 2.3 slice_reduce_fusion
  352.2 45.0 %all_to_all.64 = bf16[32,32,768]{2,1,0:T(8,128)(2,1)S(1)} all-to-all(bf16[32,32,768]{2,1,0:T(8,128)(2,1)S(1)} %broadcast_in_dim.19), channel_id=1, replica_groups=mesh['row'=8,'col'=32] {'col'}, dimensions={0} | all-to-all | bytes 3145728 | tf_op jit(solution)/shard_map/all_to_all | solution.py:35
  397.2 1.4 convolution_convert_fusion.1
  398.6 24.4 %all_to_all.65 = bf16[8,128,768]{2,1,0:T(8,128)(2,1)S(1)} all-to-all(bf16[8,128,768]{2,1,0:T(8,128)(2,1)S(1)} %bitcast.89), channel_id=1, replica_groups=mesh['row'=8,'col'=32] {'row'}, dimensions={0} | all-to-all | bytes 3145728 | tf_op jit(solution)/shard_map/all_to_all | solution.py:42
  423.6 24.2 %all_to_all.66 = bf16[8,128,768]{2,1,0:T(8,128)(2,1)S(1)} all-to-all(bf16[8,128,768]{2,1,0:T(8,128)(2,1)S(1)} %broadcast_in_dim.20), channel_id=1, replica_groups=mesh['row'=8,'col'=32] {'row'}, dimensions={0} | all-to-all | bytes 3145728 | tf_op jit(solution)/shard_map/all_to_all | solution.py:35
  447.8 2.6 convolution_convert_fusion
  450.4 5.1 %all-to-all-start.11 = ((bf16[32,32,768]{2,1,0:T(8,128)(2,1)}), bf16[32,32,768]{2,1,0:T(8,128)(2,1)}, u32[]{:S(2)}, u32[]{:S(2)}) async-start(bf16[32,32,768]{2,1,0:T(8,128)(2,1)} %bitcast.26), calls=%async_computation.11 | async-start | bytes 3145728 | tf_op jit(solution)/shard_map/all_to_all | solution.py:42
  456.2 2.5 convolution_convert_fusion.4
  458.6 3.9 convolution_convert_fusion.5
  462.5 2.1 convert_element_type.172
  464.6 1.9 convert_element_type.169
  466.5 28.1 %all-to-all-done.11 = bf16[32,32,768]{2,1,0:T(8,128)(2,1)} async-done(((bf16[32,32,768]{2,1,0:T(8,128)(2,1)}), bf16[32,32,768]{2,1,0:T(8,128)(2,1)}, u32[]{:S(2)}, u32[]{:S(2)}) %all-to-all-start.11) | async-done | bytes 1572896 | tf_op jit(solution)/shard_map/all_to_all | solution.py:42
  494.6 1.6 convert_reduce_fusion
  (81 shorter events, 8.0 us)
Async XLA Ops:
  7.2 234.5 %copy-start = (bf16[6144,256]{1,0:T(8,128)(2,1)S(1)}, bf16[6144,256]{1,0:T(8,128)(2,1)}, u32[]{:S(2)}) copy-start(bf16[6144,256]{1,0:T(8,128)(2,1)} %param.11) | copy-start | bytes 9437188
  19.9 11.6 %copy-start.18 = (s32[32,2]{0,1:T(2,128)S(1)}, s32[32,2]{0,1:T(2,128)}, u32[]{:S(2)}) copy-start(s32[32,2]{0,1:T(2,128)} %param.13) | copy-start | bytes 772
  19.9 11.6 %copy-start.20 = (bf16[32,2]{0,1:T(2,128)(2,1)S(1)}, bf16[32,2]{0,1:T(2,128)(2,1)}, u32[]{:S(2)}) copy-start(bf16[32,2]{0,1:T(2,128)(2,1)} %param.14) | copy-start | bytes 388
  19.9 50.7 %all-to-all-start = ((bf16[32,32,768]{2,1,0:T(8,128)(2,1)}), bf16[32,32,768]{2,1,0:T(8,128)(2,1)}, u32[]{:S(2)}, u32[]{:S(2)}) async-start(bf16[32,32,768]{2,1,0:T(8,128)(2,1)} %broadcast_in_dim.14), calls=%async_computation | async-start | bytes 3145728 | tf_op jit(solution)/shard_map/all_to_all | solution.py:35
  98.3 24.2 %copy-start.22 = (bf16[768,768]{1,0:T(8,128)(2,1)S(1)}, bf16[768,768]{1,0:T(8,128)(2,1)}, u32[]{:S(2)}) copy-start(bf16[768,768]{1,0:T(8,128)(2,1)} %param.10) | copy-start | bytes 3538948
  122.5 2.6 copy-start.4
  125.1 48.0 %all-to-all-start.4 = ((bf16[32,32,768]{2,1,0:T(8,128)(2,1)}), bf16[32,32,768]{2,1,0:T(8,128)(2,1)}, u32[]{:S(2)}, u32[]{:S(2)}) async-start(bf16[32,32,768]{2,1,0:T(8,128)(2,1)} %bitcast.87), calls=%async_computation.4 | async-start | bytes 3145728 | tf_op jit(solution)/shard_map/all_to_all | solution.py:42
  130.9 103.9 %all-gather.4.cloned.1.call-start = ((), (), s32[]{:S(2)}) async-start(), calls=%async_computation.16 | async-start | bytes 3244032 | tf_op jit(solution)/shard_map/all_gather | solution.py:102
  173.0 1.7 copy-start.14
  187.4 54.3 %all-to-all-start.6 = ((bf16[32,4,6144]{2,1,0:T(4,128)(2,1)}), bf16[32,4,6144]{2,1,0:T(4,128)(2,1)}, u32[]{:S(2)}, u32[]{:S(2)}) async-start(bf16[32,4,6144]{2,1,0:T(4,128)(2,1)} %broadcast_in_dim.18), calls=%async_computation.6 | async-start | bytes 3145728 | tf_op jit(solution)/shard_map/all_to_all | solution.py:119
  193.0 269.5 %reduce-scatter.5.cloned.1.call-start = ((), (), s32[]{:S(2)}) async-start(), calls=%async_computation.15 | async-start | bytes 7077888 | tf_op jit(solution)/shard_map/reduce_scatter | solution.py:170
  236.4 3.7 copy-start.17
  241.7 4.1 copy-start.2
  245.1 0.6 copy-start.13
  250.8 4.6 copy-start.3
  254.8 0.6 copy-start.16
  259.4 88.8 %all-to-all-start.7 = ((bf16[256,8,768]{2,1,0:T(8,128)(2,1)}), bf16[256,8,768]{2,1,0:T(8,128)(2,1)S(1)}, u32[]{:S(2)}, u32[]{:S(2)}) async-start(bf16[256,8,768]{2,1,0:T(8,128)(2,1)} %bitcast.20), calls=%async_computation.7 | async-start | bytes 6291456 | tf_op jit(solution)/shard_map/all_to_all | solution.py:145
  272.7 191.9 %reduce-scatter.3.cloned.1.call-start = ((), (), s32[]{:S(2)}) async-start(), calls=%async_computation.14 | async-start | bytes 7077888 | tf_op jit(solution)/shard_map/reduce_scatter | solution.py:167
  278.2 0.7 copy-start.21
  278.2 0.7 copy-start.19
  348.1 0.9 copy-start.8
  349.0 2.3 copy-start.15
  351.4 0.6 copy-start.9
  352.2 45.0 %copy-start.23 = (bf16[768,768]{1,0:T(8,128)(2,1)S(1)}, bf16[768,768]{1,0:T(8,128)(2,1)}, u32[]{:S(2)}) copy-start(bf16[768,768]{1,0:T(8,128)(2,1)} %param.10) | copy-start | bytes 3538948
  423.6 24.2 %copy-start.24 = (bf16[768,768]{1,0:T(8,128)(2,1)S(1)}, bf16[768,768]{1,0:T(8,128)(2,1)}, u32[]{:S(2)}) copy-start(bf16[768,768]{1,0:T(8,128)(2,1)} %param.9) | copy-start | bytes 3538948
  447.8 2.6 copy-start.6
  450.4 5.1 %copy-start.12 = (f32[8,4,768]{2,1,0:T(4,128)S(1)}, f32[8,4,768]{2,1,0:T(4,128)}, u32[]{:S(2)}) copy-start(f32[8,4,768]{2,1,0:T(4,128)} %get-tuple-element.11) | copy-start | bytes 294916
  450.4 5.2 %copy-start.11 = (bf16[32,768]{1,0:T(8,128)(2,1)S(1)}, bf16[32,768]{1,0:T(8,128)(2,1)}, u32[]{:S(2)}) copy-start(bf16[32,768]{1,0:T(8,128)(2,1)} %add_convert_fusion.3) | copy-start | bytes 147460
  450.4 5.8 %copy-start.5 = (bf16[8,128,768]{2,1,0:T(8,128)(2,1)S(1)}, bf16[8,128,768]{2,1,0:T(8,128)(2,1)}, u32[]{:S(2)}) copy-start(bf16[8,128,768]{2,1,0:T(8,128)(2,1)} %copy-done.4) | copy-start | bytes 4718596
  450.4 44.2 %all-to-all-start.11 = ((bf16[32,32,768]{2,1,0:T(8,128)(2,1)}), bf16[32,32,768]{2,1,0:T(8,128)(2,1)}, u32[]{:S(2)}, u32[]{:S(2)}) async-start(bf16[32,32,768]{2,1,0:T(8,128)(2,1)} %bitcast.26), calls=%async_computation.11 | async-start | bytes 3145728 | tf_op jit(solution)/shard_map/all_to_all | solution.py:42
  456.2 2.5 copy-start.7
  462.5 34.4 %copy-start.1 = (bf16[6144,256]{1,0:T(8,128)(2,1)S(1)}, bf16[6144,256]{1,0:T(8,128)(2,1)}, u32[]{:S(2)}) copy-start(bf16[6144,256]{1,0:T(8,128)(2,1)} %param.11) | copy-start | bytes 9437188
  464.6 31.7 %copy-start.10 = (bf16[32,768]{1,0:T(8,128)(2,1)S(1)}, bf16[32,768]{1,0:T(8,128)(2,1)}, u32[]{:S(2)}) copy-start(bf16[32,768]{1,0:T(8,128)(2,1)} %copy-done.9) | copy-start | bytes 147460
Sparse Core Ops, SparseCore 0:
  134.8 99.8 all-gather.3
  250.0 68.8 reduce-scatter.4
  321.5 50.1 reduce-scatter.2

commit v7 on v5

--- a/solution.py
+++ b/solution.py
@@ -1,9 +1,10 @@
 import jax
 import jax.numpy as jnp
 from jax import lax
-from jax.sharding import PartitionSpec as P
+from jax.sharding import Mesh, PartitionSpec as P
 
 EXPERTS = 4
+COL = ("cy", "cz")
 
 
 gelu_scale = 0.7978845608028654
@@ -76,14 +77,14 @@
 
 def on_device(tokens, w_up, w_down, expert_in, expert_out, expert_ids, route_weights, out_grad):
     row_count = lax.axis_size("row")
-    col_count = lax.axis_size("col")
+    col_count = lax.axis_size("cy") * lax.axis_size("cz")
     tok_col = tokens.shape[0]
     block_len = tok_col // row_count
     group_len = col_count // EXPERTS
     slot_cap = max(2, 3 * block_len // 4)
     model_width = expert_out.shape[1]
     my_row = lax.axis_index("row")
-    tok_panel = gather_rows(tokens, "col")
+    tok_panel = gather_rows(tokens, COL)
     own_grad = swap_blocks(out_grad[None], row_count)[0]
     ids_own = lax.dynamic_slice_in_dim(expert_ids, my_row * block_len, block_len, 0)
     weights_own = lax.dynamic_slice_in_dim(route_weights, my_row * block_len, block_len, 0)
@@ -99,8 +100,8 @@
     )
     grad_pack = jnp.concatenate([own_grad, table_row], axis=0)
     tok_panel, grad_pack = lax.optimization_barrier((tok_panel, grad_pack))
-    pack_all = lax.all_gather(grad_pack, "col", axis=0, tiled=False)
-    my_expert = lax.axis_index("col") // group_len
+    pack_all = lax.all_gather(grad_pack, COL, axis=0, tiled=False)
+    my_expert = lax.axis_index(COL) // group_len
     weights_recv = lax.dynamic_slice_in_dim(
         pack_all[:, block_len, : EXPERTS * block_len], my_expert * block_len, block_len, 1
     )
@@ -111,12 +112,12 @@
     preact = scatter_sum(up_terms, "row")
     hidden_full = gather_rows(gelu_tanh(preact).astype(jnp.bfloat16), "row")
     rows_in = hidden_full
-    dense_term = scatter_sum(jnp.dot(rows_in, w_down, preferred_element_type=jnp.float32), "col")
+    dense_term = scatter_sum(jnp.dot(rows_in, w_down, preferred_element_type=jnp.float32), COL)
     mixed_act = (tokens.astype(jnp.float32) + dense_term).astype(jnp.bfloat16)
     own_rows = swap_blocks(mixed_act[None], row_count)[0]
     scaled_flat = grad_rows_in.reshape(col_count * block_len, model_width)
     payload = jnp.broadcast_to(own_rows[None], (col_count,) + own_rows.shape)
-    got = lax.all_to_all(payload, "col", 0, 0, tiled=True)
+    got = lax.all_to_all(payload, COL, 0, 0, tiled=True)
     got_flat = got.reshape(col_count * block_len, model_width)
     hid_units = expert_in.shape[1]
     e_pre = jnp.dot(got_flat, expert_in, preferred_element_type=jnp.float32).reshape(
@@ -133,70 +134,78 @@
         halves = [value, blank] if first else [blank, value]
         return jnp.concatenate(halves, axis=1).reshape(col_count * 2 * block_len, hid_units)
 
-    back_flat = jnp.dot(
-        at_rows(e_hidden, True), expert_out, preferred_element_type=jnp.float32
-    ) + jnp.dot(at_rows(e_dpre, False), expert_in.T, preferred_element_type=jnp.float32)
+    value_terms = weights_recv.astype(jnp.float32).reshape(col_count * block_len, 1) * jnp.dot(
+        e_hidden.reshape(col_count * block_len, hid_units), expert_out, preferred_element_type=jnp.float32
+    )
+    returns = jnp.dot(
+        e_dpre.reshape(col_count * block_len, hid_units), expert_in.T, preferred_element_type=jnp.float32
+    )
     grad_in = jnp.dot(
         got_flat.T, e_dpre.reshape(col_count * block_len, hid_units), preferred_element_type=jnp.float32
     )
     grad_out = jnp.dot(
         e_hidden.reshape(col_count * block_len, hid_units).T, scaled_flat, preferred_element_type=jnp.float32
     )
+    y_count = lax.axis_size("cy")
+    z_count = lax.axis_size("cz")
+    by_z = value_terms.reshape(y_count, z_count, block_len, model_width).transpose(1, 0, 2, 3)
+    value_part = lax.psum_scatter(by_z, "cz", scatter_dimension=0, tiled=True)
     back = lax.all_to_all(
-        back_flat.astype(jnp.bfloat16).reshape(col_count, 2 * block_len, model_width),
-        "col",
-        0,
-        0,
-        tiled=True,
+        returns.astype(jnp.bfloat16).reshape(col_count, block_len, model_width), COL, 0, 0, tiled=True
     ).astype(jnp.float32)
-    source_weights = jnp.repeat(weight_table, group_len, axis=0)
-    moe_sum = jnp.sum(source_weights[:, :, None] * back[:, :block_len], axis=0)
-    grad_sum = jnp.sum(back[:, block_len:], axis=0)
-    layer_rows = (own_rows.astype(jnp.float32) + moe_sum).astype(jnp.bfloat16)
+    grad_sum = jnp.sum(back, axis=0)
     grad_rows = (own_grad.astype(jnp.float32) + grad_sum).astype(jnp.bfloat16)
-    out_both = unswap_blocks(jnp.stack([layer_rows, grad_rows]), row_count)
-    layer_out, mixed_grad = out_both[0], out_both[1]
+    mixed_grad = unswap_blocks(grad_rows[None], row_count)[0]
     expert_in_grad = lax.psum_scatter(
         grad_in.astype(jnp.bfloat16).astype(jnp.float32), "row", scatter_dimension=0, tiled=True
     ).astype(jnp.bfloat16)
     expert_out_grad = lax.psum_scatter(
         grad_out.astype(jnp.bfloat16).astype(jnp.float32), "row", scatter_dimension=1, tiled=True
     ).astype(jnp.bfloat16)
-    cot_panel = gather_rows(mixed_grad, "col")
+    cot_panel = gather_rows(mixed_grad, COL)
+    value_part, cot_panel = lax.optimization_barrier((value_part, cot_panel))
     hgrad_terms = jnp.dot(cot_panel, w_down.T, preferred_element_type=jnp.float32)
     down_grad = jnp.dot(hidden_full.T, cot_panel, preferred_element_type=jnp.float32).astype(
         jnp.bfloat16
     )
     hidden_grad = scatter_sum(hgrad_terms, "row")
+    value_all = lax.all_gather(value_part[0], "cy", axis=0, tiled=False)
+    moe_sum = jnp.sum(
+        lax.dynamic_index_in_dim(value_all, lax.axis_index("cy"), 1, keepdims=False), axis=0
+    )
+    layer_rows = (own_rows.astype(jnp.float32) + moe_sum).astype(jnp.bfloat16)
+    layer_out = unswap_blocks(layer_rows[None], row_count)[0]
     dpre_full = gather_rows((hidden_grad * gelu_slope(preact)).astype(jnp.bfloat16), "row")
     up_grad = jnp.dot(tok_panel.T, dpre_full, preferred_element_type=jnp.float32).astype(
         jnp.bfloat16
     )
     rows_in = dpre_full
-    input_term = scatter_sum(jnp.dot(rows_in, w_up.T, preferred_element_type=jnp.float32), "col")
+    input_term = scatter_sum(jnp.dot(rows_in, w_up.T, preferred_element_type=jnp.float32), COL)
     tokens_grad = (mixed_grad.astype(jnp.float32) + input_term).astype(jnp.bfloat16)
     return (layer_out, tokens_grad, up_grad, down_grad, expert_in_grad, expert_out_grad)
 
 
 def solution(mesh):
     in_specs = (
-        P("col", "row"),
-        P("row", "col"),
-        P("col", "row"),
-        P(None, "col"),
-        P("col", None),
-        P("col", None),
-        P("col", None),
-        P("col", "row"),
+        P(COL, "row"),
+        P("row", COL),
+        P(COL, "row"),
+        P(None, COL),
+        P(COL, None),
+        P(COL, None),
+        P(COL, None),
+        P(COL, "row"),
     )
     out_specs = (
-        P("col", "row"),
-        P("col", "row"),
-        P("row", "col"),
-        P("col", "row"),
-        P("row", "col"),
-        P("col", "row"),
-    )
+        P(COL, "row"),
+        P(COL, "row"),
+        P("row", COL),
+        P(COL, "row"),
+        P("row", COL),
+        P(COL, "row"),
+    )
+    rows, cols = mesh.devices.shape
+    split_mesh = Mesh(mesh.devices.reshape(rows, EXPERTS, cols // EXPERTS), ("row", "cy", "cz"))
     return jax.shard_map(
-        on_device, mesh=mesh, in_specs=in_specs, out_specs=out_specs, check_vma=False
-    )
+        on_device, mesh=split_mesh, in_specs=in_specs, out_specs=out_specs, check_vma=False
+    )

time: 505 us -> 551 us (1.091)
  waiting for transfers between devices: 216 us -> 290 us
  blocking collectives: 172 us -> 104 us
  starting transfers between devices: 34.4 us -> 52.7 us
  local copies, waits for them, and re-layouts: 18.5 us -> 33.4 us
    all_to_all x3 -> x1, blocking collectives: 95 us -> 24.2 us  [gather_rows(): got = lax.all_to_all(spread, axis_name, 0, 0, tiled=True)]
    unnamed x3 -> x6, waiting for transfers between devices: 0.71 us -> 66 us
    all_to_all x1 -> x3, waiting for transfers between devices: 37.6 us -> 66.7 us  [gather_rows(): got = lax.all_to_all(spread, axis_name, 0, 0, tiled=True)]
    all_to_all x2 -> x3, waiting for transfers between devices: 66.8 us -> 39 us  [the longest x1 37.2 us: on_device(): lax.all_to_all(returns.astype(jnp.bfloat16).reshape(col_count, block_len,...]
    all_to_all x1 -> x3, starting transfers between devices: 11.5 us -> 20.6 us  [gather_rows(): got = lax.all_to_all(spread, axis_name, 0, 0, tiled=True)]
    reshape x1 -> x4, local copies, waits for them, and re-layouts: 0.02 us -> 8.08 us  [the longest x1 3.79 us: on_device(): returns.astype(jnp.bfloat16).reshape(col_count, block_len, model_width)]
    all_to_all x2 -> x3, starting transfers between devices: 11.7 us -> 17 us  [the longest x1 8.14 us: on_device(): lax.all_to_all(returns.astype(jnp.bfloat16).reshape(col_count, block_len,...]
    all_gather x1 -> x2, waiting for transfers between devices: 40.8 us -> 41.2 us  [the longest x1 41.2 us: on_device(): pack_all = lax.all_gather(grad_pack, COL, axis=0, tiled=False)]
  transfers between devices with their start and end apart: 8 -> 13, of which waited for: 6 -> 9; matrix products, arithmetic and copies ran while one was open for 9% -> 11% of each run, Pallas kernels for 0% -> 0%
where the time goes in v7:
time: 551 us; the launch traced here: 549 us
  waiting for transfers between devices  290 us (53%)
  blocking collectives  104 us (19%)
  starting transfers between devices  52.7 us (10%)
  matrix products  38.7 us (7%)
  local copies, waits for them, and re-layouts  33.4 us (6%)
  other arithmetic  16.1 us (3%)
  between operations  14.1 us (3%)
    all_to_all x2, waiting for transfers between devices, scatter_sum(): got = lax.all_to_all(blocks, axis_name, 0, 0, tiled=True)  73.2 us
    all_to_all x3, waiting for transfers between devices, gather_rows(): got = lax.all_to_all(spread, axis_name, 0, 0, tiled=True)  66.7 us
    unnamed x6, waiting for transfers between devices  66 us
    all_to_all x2, blocking collectives, scatter_sum(): got = lax.all_to_all(blocks, axis_name, 0, 0, tiled=True)  48.1 us
    all_gather x1, waiting for transfers between devices, on_device(): pack_all = lax.all_gather(grad_pack, COL, axis=0, tiled=False)  41.2 us
    all_to_all x1, waiting for transfers between devices, on_device(): lax.all_to_all(returns.astype(jnp.bfloat16).reshape(col_count, block_len,...  37.2 us
    all_to_all x1, blocking collectives, gather_rows(): got = lax.all_to_all(spread, axis_name, 0, 0, tiled=True)  24.2 us
    all_to_all x3, starting transfers between devices, gather_rows(): got = lax.all_to_all(spread, axis_name, 0, 0, tiled=True)  20.6 us
  transfers between devices with their start and end apart: 13, of which 9 were waited for; matrix products, arithmetic and copies ran while one was open for 11% of the time, Pallas kernels for 0%

profile of v7, /device:TPU:32, one launch (start us, length us, event | category | flops | bytes accessed | tf_op | source)
XLA Modules:
  0.0 548.7 jit_solution(6473121901729789227)
XLA Ops:
  8.1 9.6 %all_to_all.70 = bf16[8,4,768]{2,1,0:T(4,128)(2,1)S(1)} all-to-all(bf16[8,4,768]{2,1,0:T(4,128)(2,1)S(1)} %reshape_transpose_reshape_broadcast_in_dim.6), channel_id=1, replica_groups=mesh['row'=8,'cy'=4,'cz'=8] {'row'}, dimensions={0} | all-to-all | bytes 98304 | tf_op jit(solution)/shard_map/all_to_all | solution.py:64
  17.8 2.2 broadcast_in_dim.14
  20.0 11.5 %all-to-all-start = ((bf16[32,32,768]{2,1,0:T(8,128)(2,1)}), bf16[32,32,768]{2,1,0:T(8,128)(2,1)}, u32[]{:S(2)}, u32[]{:S(2)}) async-start(bf16[32,32,768]{2,1,0:T(8,128)(2,1)} %broadcast_in_dim.14), calls=%async_computation | async-start | bytes 3145728 | tf_op jit(solution)/shard_map/all_to_all | solution.py:36
  32.4 38.2 %all-to-all-done = bf16[32,32,768]{2,1,0:T(8,128)(2,1)} async-done(((bf16[32,32,768]{2,1,0:T(8,128)(2,1)}), bf16[32,32,768]{2,1,0:T(8,128)(2,1)}, u32[]{:S(2)}, u32[]{:S(2)}) %all-to-all-start) | async-done | bytes 1572896 | tf_op jit(solution)/shard_map/all_to_all | solution.py:36
  70.7 3.1 convolution_convert_fusion.4
  73.8 24.0 %all_to_all.71 = bf16[8,128,768]{2,1,0:T(8,128)(2,1)S(1)} all-to-all(bf16[8,128,768]{2,1,0:T(8,128)(2,1)S(1)} %bitcast.87), channel_id=1, replica_groups=mesh['row'=8,'cy'=4,'cz'=8] {'row'}, dimensions={0} | all-to-all | bytes 3145728 | tf_op jit(solution)/shard_map/all_to_all | solution.py:43
  98.3 24.2 %all_to_all.72 = bf16[8,128,768]{2,1,0:T(8,128)(2,1)S(1)} all-to-all(bf16[8,128,768]{2,1,0:T(8,128)(2,1)S(1)} %broadcast_in_dim.15), channel_id=1, replica_groups=mesh['row'=8,'cy'=4,'cz'=8] {'row'}, dimensions={0} | all-to-all | bytes 3145728 | tf_op jit(solution)/shard_map/all_to_all | solution.py:36
  122.5 2.6 convolution_convert_fusion.3
  125.1 5.8 %all-to-all-start.4 = ((bf16[32,32,768]{2,1,0:T(8,128)(2,1)}), bf16[32,32,768]{2,1,0:T(8,128)(2,1)}, u32[]{:S(2)}, u32[]{:S(2)}) async-start(bf16[32,32,768]{2,1,0:T(8,128)(2,1)} %bitcast.86), calls=%async_computation.4 | async-start | bytes 3145728 | tf_op jit(solution)/shard_map/all_to_all | solution.py:43
  131.6 41.4 %all-to-all-done.4 = bf16[32,32,768]{2,1,0:T(8,128)(2,1)} async-done(((bf16[32,32,768]{2,1,0:T(8,128)(2,1)}), bf16[32,32,768]{2,1,0:T(8,128)(2,1)}, u32[]{:S(2)}, u32[]{:S(2)}) %all-to-all-start.4) | async-done | bytes 1572896 | tf_op jit(solution)/shard_map/all_to_all | solution.py:43
  173.0 1.7 convert_reduce_fusion.3
  176.7 8.8 %all_to_all.73 = bf16[8,4,768]{2,1,0:T(4,128)(2,1)S(1)} all-to-all(bf16[8,4,768]{2,1,0:T(4,128)(2,1)} %reshape_transpose_reshape_broadcast_in_dim.7), channel_id=1, replica_groups=mesh['row'=8,'cy'=4,'cz'=8] {'row'}, dimensions={0} | all-to-all | bytes 98304 | tf_op jit(solution)/shard_map/all_to_all | solution.py:64
  186.1 1.9 broadcast_in_dim.17
  188.0 5.6 %all-to-all-start.6 = ((bf16[32,4,6144]{2,1,0:T(4,128)(2,1)}), bf16[32,4,6144]{2,1,0:T(4,128)(2,1)}, u32[]{:S(2)}, u32[]{:S(2)}) async-start(bf16[32,4,6144]{2,1,0:T(4,128)(2,1)} %broadcast_in_dim.17), calls=%async_computation.6 | async-start | bytes 3145728 | tf_op jit(solution)/shard_map/all_to_all | solution.py:120
  193.6 41.2 %all-gather.7.cloned.1.call-done = bf16[32,5,6144]{2,1,0:T(8,128)(2,1)} async-done(((bf16[1,5,6144]{2,1,0:T(8,128)(2,1)}), bf16[32,5,6144]{2,1,0:T(8,128)(2,1)}) %all-gather.7.cloned.1.call-update) | async-done | bytes 1966096 | tf_op jit(solution)/shard_map/all_gather | solution.py:103
  234.8 1.5 slice.8
  236.7 2.1 fusion.33
  240.2 3.7 slice.9
  243.9 3.5 multiply_convert_fusion.8
  247.4 1.4 fusion.13
  250.2 1.5 reshape.143
  251.7 3.2 convolution_convert_fusion
  254.8 3.8 reshape.144
  258.6 8.1 %all-to-all-start.7 = ((bf16[32,4,6144]{2,1,0:T(4,128)(2,1)}), bf16[32,4,6144]{2,1,0:T(4,128)(2,1)}, u32[]{:S(2)}, u32[]{:S(2)}) async-start(bf16[32,4,6144]{2,1,0:T(4,128)(2,1)} %reshape.144), calls=%async_computation.7 | async-start | bytes 3145728 | tf_op jit(solution)/shard_map/all_to_all | solution.py:153
  268.3 2.5 convolution_multiply_fusion
  270.8 2.2 reshape.142
  273.0 37.2 %all-to-all-done.7 = bf16[32,4,6144]{2,1,0:T(4,128)(2,1)} async-done(((bf16[32,4,6144]{2,1,0:T(4,128)(2,1)}), bf16[32,4,6144]{2,1,0:T(4,128)(2,1)}, u32[]{:S(2)}, u32[]{:S(2)}) %all-to-all-start.7) | async-done | bytes 1572896 | tf_op jit(solution)/shard_map/all_to_all | solution.py:153
  310.2 2.1 convert_reduce_fusion.2
  312.3 12.9 %all_to_all.74 = bf16[8,4,768]{2,1,0:T(4,128)(2,1)S(1)} all-to-all(bf16[8,4,768]{2,1,0:T(4,128)(2,1)S(1)} %fusion.30), channel_id=1, replica_groups=mesh['row'=8,'cy'=4,'cz'=8] {'row'}, dimensions={0} | all-to-all | bytes 98304 | tf_op jit(solution)/shard_map/all_to_all | solution.py:73
  326.6 5.3 all-to-all-start.9
  332.5 65.2 %all-reduce.4.cloned.1.call-done = f32[8,4,4,6144]{3,2,0,1:T(4,128)} async-done(((f32[8,4,4,6144]{3,2,0,1:T(4,128)}), f32[8,4,4,6144]{3,2,0,1:T(4,128)}) %all-reduce.4.cloned.1.call-update) | async-done | bytes 3145744
  397.8 2.4 constant_dynamic-slice_fusion.2
  400.3 5.4 fusion.1
  407.1 4.9 fusion.3
  414.8 24.1 %all_to_all.75 = bf16[8,128,768]{2,1,0:T(8,128)(2,1)S(1)} all-to-all(bf16[8,128,768]{2,1,0:T(8,128)(2,1)S(1)} %bitcast.88), channel_id=1, replica_groups=mesh['row'=8,'cy'=4,'cz'=8] {'row'}, dimensions={0} | all-to-all | bytes 3145728 | tf_op jit(solution)/shard_map/all_to_all | solution.py:43
  440.6 3.7 all-to-all-start.12
  446.1 28.5 %all-to-all-done.12 = bf16[8,128,768]{2,1,0:T(8,128)(2,1)S(1)} async-done(((bf16[8,128,768]{2,1,0:T(8,128)(2,1)}), bf16[8,128,768]{2,1,0:T(8,128)(2,1)S(1)}, u32[]{:S(2)}, u32[]{:S(2)}) %all-to-all-start.12) | async-done | bytes 1572896 | tf_op jit(solution)/shard_map/all_to_all | solution.py:36
  474.5 3.3 all-to-all-start.10
  477.9 3.9 convolution_convert_fusion.1
  481.8 1.8 all-to-all-done.10
  483.6 8.9 %all-to-all-start.13 = ((bf16[32,32,768]{2,1,0:T(8,128)(2,1)}), bf16[32,32,768]{2,1,0:T(8,128)(2,1)}, u32[]{:S(2)}, u32[]{:S(2)}) async-start(bf16[32,32,768]{2,1,0:T(8,128)(2,1)} %bitcast.85), calls=%async_computation.13 | async-start | bytes 3145728 | tf_op jit(solution)/shard_map/all_to_all | solution.py:43
  492.5 2.5 convolution_convert_fusion.5
  495.6 4.3 convolution_convert_fusion.6
  500.0 31.8 %all-to-all-done.13 = bf16[32,32,768]{2,1,0:T(8,128)(2,1)} async-done(((bf16[32,32,768]{2,1,0:T(8,128)(2,1)}), bf16[32,32,768]{2,1,0:T(8,128)(2,1)}, u32[]{:S(2)}, u32[]{:S(2)}) %all-to-all-start.13) | async-done | bytes 1572896 | tf_op jit(solution)/shard_map/all_to_all | solution.py:43
  531.7 1.8 convert_reduce_fusion
  534.2 1.9 convert_element_type.183
  536.1 4.2 reduce-scatter.6.cloned.1.call-done
  540.3 1.9 convert_element_type.186
  (93 shorter events, 21.5 us)
Async XLA Ops:
  7.2 236.7 %copy-start = (bf16[6144,256]{1,0:T(8,128)(2,1)S(1)}, bf16[6144,256]{1,0:T(8,128)(2,1)}, u32[]{:S(2)}) copy-start(bf16[6144,256]{1,0:T(8,128)(2,1)} %param.11) | copy-start | bytes 9437188
  17.8 14.0 %copy-start.12 = (bf16[8,4,768]{2,1,0:T(4,128)(2,1)}, bf16[8,4,768]{2,1,0:T(4,128)(2,1)S(1)}, u32[]{:S(2)}) copy-start(bf16[8,4,768]{2,1,0:T(4,128)(2,1)S(1)} %all_to_all.70) | copy-start | bytes 147460
  20.0 11.6 %copy-start.20 = (s32[32,2]{0,1:T(2,128)S(1)}, s32[32,2]{0,1:T(2,128)}, u32[]{:S(2)}) copy-start(s32[32,2]{0,1:T(2,128)} %param.13) | copy-start | bytes 772
  20.0 11.6 %copy-start.21 = (bf16[32,2]{0,1:T(2,128)(2,1)S(1)}, bf16[32,2]{0,1:T(2,128)(2,1)}, u32[]{:S(2)}) copy-start(bf16[32,2]{0,1:T(2,128)(2,1)} %param.14) | copy-start | bytes 388
  20.0 50.7 %all-to-all-start = ((bf16[32,32,768]{2,1,0:T(8,128)(2,1)}), bf16[32,32,768]{2,1,0:T(8,128)(2,1)}, u32[]{:S(2)}, u32[]{:S(2)}) async-start(bf16[32,32,768]{2,1,0:T(8,128)(2,1)} %broadcast_in_dim.14), calls=%async_computation | async-start | bytes 3145728 | tf_op jit(solution)/shard_map/all_to_all | solution.py:36
  98.3 24.2 %copy-start.22 = (bf16[768,768]{1,0:T(8,128)(2,1)S(1)}, bf16[768,768]{1,0:T(8,128)(2,1)}, u32[]{:S(2)}) copy-start(bf16[768,768]{1,0:T(8,128)(2,1)} %param.10) | copy-start | bytes 3538948
  122.5 2.6 copy-start.5
  125.1 48.0 %all-to-all-start.4 = ((bf16[32,32,768]{2,1,0:T(8,128)(2,1)}), bf16[32,32,768]{2,1,0:T(8,128)(2,1)}, u32[]{:S(2)}, u32[]{:S(2)}) async-start(bf16[32,32,768]{2,1,0:T(8,128)(2,1)} %bitcast.86), calls=%async_computation.4 | async-start | bytes 3145728 | tf_op jit(solution)/shard_map/all_to_all | solution.py:43
  130.9 103.9 %all-gather.7.cloned.1.call-start = ((), (), s32[]{:S(2)}) async-start(), calls=%async_computation.19 | async-start | bytes 3244032 | tf_op jit(solution)/shard_map/all_gather | solution.py:103
  173.0 1.7 copy-start.15
  185.5 0.6 copy-start.8
  188.0 55.9 %all-to-all-start.6 = ((bf16[32,4,6144]{2,1,0:T(4,128)(2,1)}), bf16[32,4,6144]{2,1,0:T(4,128)(2,1)}, u32[]{:S(2)}, u32[]{:S(2)}) async-start(bf16[32,4,6144]{2,1,0:T(4,128)(2,1)} %broadcast_in_dim.17), calls=%async_computation.6 | async-start | bytes 3145728 | tf_op jit(solution)/shard_map/all_to_all | solution.py:120
  243.9 3.5 copy-start.2
  243.9 3.5 copy-start.4
  243.9 3.5 copy-start.18
  248.9 0.6 copy-start.16
  258.6 9.0 %copy-start.14 = (bf16[32,4,256]{2,0,1:T(8,128)(2,1)S(1)}, bf16[32,4,256]{2,0,1:T(8,128)(2,1)}, u32[]{:S(2)}) copy-start(bf16[32,4,256]{2,0,1:T(8,128)(2,1)} %get-tuple-element.16) | copy-start | bytes 196612
  258.6 51.6 %all-to-all-start.7 = ((bf16[32,4,6144]{2,1,0:T(4,128)(2,1)}), bf16[32,4,6144]{2,1,0:T(4,128)(2,1)}, u32[]{:S(2)}, u32[]{:S(2)}) async-start(bf16[32,4,6144]{2,1,0:T(4,128)(2,1)} %reshape.144), calls=%async_computation.7 | async-start | bytes 3145728 | tf_op jit(solution)/shard_map/all_to_all | solution.py:153
  266.8 131.0 %all-reduce.4.cloned.1.call-start = ((), (), s32[]{:S(2)}) async-start(), calls=%async_computation.20 | async-start | bytes 6291456
  273.0 39.3 %copy-start.13 = (bf16[8,4,768]{2,1,0:T(4,128)(2,1)S(1)}, bf16[8,4,768]{2,1,0:T(4,128)(2,1)}, u32[]{:S(2)}) copy-start(bf16[8,4,768]{2,1,0:T(4,128)(2,1)} %copy-done.12) | copy-start | bytes 147460
  325.2 1.3 copy-start.10
  326.5 5.4 copy-start.24
  326.5 73.7 %copy-start.17 = (bf16[32,4,256]{2,0,1:T(8,128)(2,1)S(1)}, bf16[32,4,256]{2,0,1:T(8,128)(2,1)}, u32[]{:S(2)}) copy-start(bf16[32,4,256]{2,0,1:T(8,128)(2,1)} %copy-done.16) | copy-start | bytes 196612
  326.6 73.6 %all-to-all-start.9 = ((bf16[32,32,768]{2,1,0:T(8,128)(2,1)}), bf16[32,32,768]{2,1,0:T(8,128)(2,1)S(1)}, u32[]{:S(2)}, u32[]{:S(2)}) async-start(bf16[32,32,768]{2,1,0:T(8,128)(2,1)} %broadcast_in_dim.19), calls=%async_computation.9 | async-start | bytes 3145728 | tf_op jit(solution)/shard_map/all_to_all | solution.py:36
  331.9 112.5 %all-gather.5.cloned.1.call-start = ((), (), s32[]{:S(2)}) async-start(), calls=%async_computation.16 | async-start | bytes 1966080 | tf_op jit(solution)/shard_map/all_gather | solution.py:172
  400.2 133.9 %reduce-scatter.4.cloned.1.call-start = ((), (), s32[]{:S(2)}) async-start(), calls=%async_computation.17 | async-start | bytes 7077888 | tf_op jit(solution)/shard_map/reduce_scatter | solution.py:159
  405.7 1.4 copy-start.3
  405.7 1.4 copy-start.19
  405.7 134.5 %reduce-scatter.6.cloned.1.call-start = ((), (), s32[]{:S(2)}) async-start(), calls=%async_computation.18 | async-start | bytes 7077888 | tf_op jit(solution)/shard_map/reduce_scatter | solution.py:162
  412.1 1.3 copy-start.23
  440.6 4.8 copy-start.9
  440.6 33.9 %all-to-all-start.12 = ((bf16[8,128,768]{2,1,0:T(8,128)(2,1)}), bf16[8,128,768]{2,1,0:T(8,128)(2,1)S(1)}, u32[]{:S(2)}, u32[]{:S(2)}) async-start(bf16[8,128,768]{2,1,0:T(8,128)(2,1)} %broadcast_in_dim.20), calls=%async_computation.12 | async-start | bytes 3145728 | tf_op jit(solution)/shard_map/all_to_all | solution.py:36
  474.5 7.3 %copy-start.7 = (bf16[8,128,768]{2,1,0:T(8,128)(2,1)}, bf16[8,128,768]{2,1,0:T(8,128)(2,1)S(1)}, u32[]{:S(2)}) copy-start(bf16[8,128,768]{2,1,0:T(8,128)(2,1)S(1)} %all-to-all-done.12) | copy-start | bytes 4718596
  474.5 9.1 %all-to-all-start.10 = ((bf16[8,4,768]{2,1,0:T(4,128)(2,1)}), bf16[8,4,768]{2,1,0:T(4,128)(2,1)S(1)}, u32[]{:S(2)}, u32[]{:S(2)}) async-start(bf16[8,4,768]{2,1,0:T(4,128)(2,1)} %fusion.31), calls=%async_computation.10 | async-start | bytes 98304 | tf_op jit(solution)/shard_map/all_to_all | solution.py:73
  483.6 8.9 %copy-start.6 = (bf16[8,128,768]{2,1,0:T(8,128)(2,1)S(1)}, bf16[8,128,768]{2,1,0:T(8,128)(2,1)}, u32[]{:S(2)}) copy-start(bf16[8,128,768]{2,1,0:T(8,128)(2,1)} %copy-done.5) | copy-start | bytes 4718596
  483.6 48.1 %all-to-all-start.13 = ((bf16[32,32,768]{2,1,0:T(8,128)(2,1)}), bf16[32,32,768]{2,1,0:T(8,128)(2,1)}, u32[]{:S(2)}, u32[]{:S(2)}) async-start(bf16[32,32,768]{2,1,0:T(8,128)(2,1)} %bitcast.85), calls=%async_computation.13 | async-start | bytes 3145728 | tf_op jit(solution)/shard_map/all_to_all | solution.py:43
  499.9 33.6 %copy-start.11 = (bf16[32,768]{1,0:T(8,128)(2,1)S(1)}, bf16[32,768]{1,0:T(8,128)(2,1)}, u32[]{:S(2)}) copy-start(bf16[32,768]{1,0:T(8,128)(2,1)} %copy-done.10) | copy-start | bytes 147460
  531.7 10.5 %copy-start.1 = (bf16[6144,256]{1,0:T(8,128)(2,1)S(1)}, bf16[6144,256]{1,0:T(8,128)(2,1)}, u32[]{:S(2)}) copy-start(bf16[6144,256]{1,0:T(8,128)(2,1)} %param.11) | copy-start | bytes 9437188
Sparse Core Ops, SparseCore 0:
  134.8 99.8 all-gather.6
  273.1 124.6 all-reduce.3
  400.3 27.2 all-gather.4
  430.0 62.3 reduce-scatter.3
  494.9 45.3 reduce-scatter.5

commit v8 on v7

--- a/solution.py
+++ b/solution.py
@@ -148,7 +148,11 @@
     )
     y_count = lax.axis_size("cy")
     z_count = lax.axis_size("cz")
-    by_z = value_terms.reshape(y_count, z_count, block_len, model_width).transpose(1, 0, 2, 3)
+    by_z = (
+        value_terms.astype(jnp.bfloat16)
+        .reshape(y_count, z_count, block_len, model_width)
+        .transpose(1, 0, 2, 3)
+    )
     value_part = lax.psum_scatter(by_z, "cz", scatter_dimension=0, tiled=True)
     back = lax.all_to_all(
         returns.astype(jnp.bfloat16).reshape(col_count, block_len, model_width), COL, 0, 0, tiled=True
@@ -171,7 +175,10 @@
     hidden_grad = scatter_sum(hgrad_terms, "row")
     value_all = lax.all_gather(value_part[0], "cy", axis=0, tiled=False)
     moe_sum = jnp.sum(
-        lax.dynamic_index_in_dim(value_all, lax.axis_index("cy"), 1, keepdims=False), axis=0
+        lax.dynamic_index_in_dim(value_all, lax.axis_index("cy"), 1, keepdims=False).astype(
+            jnp.float32
+        ),
+        axis=0,
     )
     layer_rows = (own_rows.astype(jnp.float32) + moe_sum).astype(jnp.bfloat16)
     layer_out = unswap_blocks(layer_rows[None], row_count)[0]

time: 551 us -> 517 us (0.938)
  waiting for transfers between devices: 290 us -> 243 us
  blocking collectives: 104 us -> 116 us
    unnamed x6 -> x5, waiting for transfers between devices: 66 us -> 2.6 us
    all_to_all x3, waiting for transfers between devices: 66.7 us -> 84.2 us  [gather_rows(): got = lax.all_to_all(spread, axis_name, 0, 0, tiled=True)]
    all_gather x0 -> x1, blocking collectives: none -> 14.1 us  [on_device(): value_all = lax.all_gather(value_part[0], 'cy', axis=0, tiled=False)]
  transfers between devices with their start and end apart: 13 -> 12, of which waited for: 9 -> 10; matrix products, arithmetic and copies ran while one was open for 11% -> 12% of each run, Pallas kernels for 0% -> 0%
where the time goes in v8:
time: 517 us; the launch traced here: 515 us
  waiting for transfers between devices  243 us (47%)
  blocking collectives  116 us (22%)
  starting transfers between devices  52.3 us (10%)
  matrix products  41.3 us (8%)
  local copies, waits for them, and re-layouts  34.4 us (7%)
  between operations  14.1 us (3%)
  other arithmetic  13.6 us (3%)
    all_to_all x3, waiting for transfers between devices, gather_rows(): got = lax.all_to_all(spread, axis_name, 0, 0, tiled=True)  84.2 us
    all_to_all x2, waiting for transfers between devices, scatter_sum(): got = lax.all_to_all(blocks, axis_name, 0, 0, tiled=True)  73.1 us
    all_to_all x2, blocking collectives, scatter_sum(): got = lax.all_to_all(blocks, axis_name, 0, 0, tiled=True)  48.7 us
    all_gather x1, waiting for transfers between devices, on_device(): pack_all = lax.all_gather(grad_pack, COL, axis=0, tiled=False)  41.1 us
    all_to_all x1, waiting for transfers between devices, on_device(): lax.all_to_all(returns.astype(jnp.bfloat16).reshape(col_count, block_len,...  38.3 us
    all_to_all x1, blocking collectives, gather_rows(): got = lax.all_to_all(spread, axis_name, 0, 0, tiled=True)  24.2 us
    all_to_all x3, starting transfers between devices, gather_rows(): got = lax.all_to_all(spread, axis_name, 0, 0, tiled=True)  21.1 us
    all_to_all x2, blocking collectives, swap_blocks(): lax.all_to_all(parts.reshape(count, arrays * block, width), 'row', 0, 0,...  18.4 us
  transfers between devices with their start and end apart: 12, of which 10 were waited for; matrix products, arithmetic and copies ran while one was open for 12% of the time, Pallas kernels for 0%

profile of v8, /device:TPU:32, one launch (start us, length us, event | category | flops | bytes accessed | tf_op | source)
XLA Modules:
  0.0 515.0 jit_solution(16476402740457843398)
XLA Ops:
  8.1 9.6 %all_to_all.70 = bf16[8,4,768]{2,1,0:T(4,128)(2,1)S(1)} all-to-all(bf16[8,4,768]{2,1,0:T(4,128)(2,1)S(1)} %reshape_transpose_reshape_broadcast_in_dim.6), channel_id=1, replica_groups=mesh['row'=8,'cy'=4,'cz'=8] {'row'}, dimensions={0} | all-to-all | bytes 98304 | tf_op jit(solution)/shard_map/all_to_all | solution.py:64
  17.8 2.2 broadcast_in_dim.14
  20.0 11.5 %all-to-all-start = ((bf16[32,32,768]{2,1,0:T(8,128)(2,1)}), bf16[32,32,768]{2,1,0:T(8,128)(2,1)}, u32[]{:S(2)}, u32[]{:S(2)}) async-start(bf16[32,32,768]{2,1,0:T(8,128)(2,1)} %broadcast_in_dim.14), calls=%async_computation | async-start | bytes 3145728 | tf_op jit(solution)/shard_map/all_to_all | solution.py:36
  32.4 38.2 %all-to-all-done = bf16[32,32,768]{2,1,0:T(8,128)(2,1)} async-done(((bf16[32,32,768]{2,1,0:T(8,128)(2,1)}), bf16[32,32,768]{2,1,0:T(8,128)(2,1)}, u32[]{:S(2)}, u32[]{:S(2)}) %all-to-all-start) | async-done | bytes 1572896 | tf_op jit(solution)/shard_map/all_to_all | solution.py:36
  70.7 3.1 convolution_convert_fusion.4
  73.8 24.0 %all_to_all.71 = bf16[8,128,768]{2,1,0:T(8,128)(2,1)S(1)} all-to-all(bf16[8,128,768]{2,1,0:T(8,128)(2,1)S(1)} %bitcast.87), channel_id=1, replica_groups=mesh['row'=8,'cy'=4,'cz'=8] {'row'}, dimensions={0} | all-to-all | bytes 3145728 | tf_op jit(solution)/shard_map/all_to_all | solution.py:43
  98.3 24.2 %all_to_all.72 = bf16[8,128,768]{2,1,0:T(8,128)(2,1)S(1)} all-to-all(bf16[8,128,768]{2,1,0:T(8,128)(2,1)S(1)} %broadcast_in_dim.15), channel_id=1, replica_groups=mesh['row'=8,'cy'=4,'cz'=8] {'row'}, dimensions={0} | all-to-all | bytes 3145728 | tf_op jit(solution)/shard_map/all_to_all | solution.py:36
  122.5 2.6 convolution_convert_fusion.3
  125.1 5.8 %all-to-all-start.4 = ((bf16[32,32,768]{2,1,0:T(8,128)(2,1)}), bf16[32,32,768]{2,1,0:T(8,128)(2,1)}, u32[]{:S(2)}, u32[]{:S(2)}) async-start(bf16[32,32,768]{2,1,0:T(8,128)(2,1)} %bitcast.86), calls=%async_computation.4 | async-start | bytes 3145728 | tf_op jit(solution)/shard_map/all_to_all | solution.py:43
  131.6 41.4 %all-to-all-done.4 = bf16[32,32,768]{2,1,0:T(8,128)(2,1)} async-done(((bf16[32,32,768]{2,1,0:T(8,128)(2,1)}), bf16[32,32,768]{2,1,0:T(8,128)(2,1)}, u32[]{:S(2)}, u32[]{:S(2)}) %all-to-all-start.4) | async-done | bytes 1572896 | tf_op jit(solution)/shard_map/all_to_all | solution.py:43
  173.0 1.7 convert_reduce_fusion.3
  176.7 8.8 %all_to_all.73 = bf16[8,4,768]{2,1,0:T(4,128)(2,1)S(1)} all-to-all(bf16[8,4,768]{2,1,0:T(4,128)(2,1)} %reshape_transpose_reshape_broadcast_in_dim.7), channel_id=1, replica_groups=mesh['row'=8,'cy'=4,'cz'=8] {'row'}, dimensions={0} | all-to-all | bytes 98304 | tf_op jit(solution)/shard_map/all_to_all | solution.py:64
  186.1 1.9 broadcast_in_dim.17
  188.0 5.6 %all-to-all-start.6 = ((bf16[32,4,6144]{2,1,0:T(4,128)(2,1)}), bf16[32,4,6144]{2,1,0:T(4,128)(2,1)}, u32[]{:S(2)}, u32[]{:S(2)}) async-start(bf16[32,4,6144]{2,1,0:T(4,128)(2,1)} %broadcast_in_dim.17), calls=%async_computation.6 | async-start | bytes 3145728 | tf_op jit(solution)/shard_map/all_to_all | solution.py:120
  193.6 41.1 %all-gather.4.cloned.1.call-done = bf16[32,5,6144]{2,1,0:T(8,128)(2,1)} async-done(((bf16[1,5,6144]{2,1,0:T(8,128)(2,1)}), bf16[32,5,6144]{2,1,0:T(8,128)(2,1)}) %all-gather.4.cloned.1.call-update) | async-done | bytes 1966096 | tf_op jit(solution)/shard_map/all_gather | solution.py:103
  236.7 2.1 fusion.34
  240.2 2.2 all-to-all-done.6
  242.4 3.3 multiply_convert_fusion.8
  248.5 3.6 fusion.4
  252.1 3.8 reshape.143
  256.8 2.6 slice.9
  260.6 4.2 fusion.3
  264.7 3.8 fusion.14
  269.9 1.5 reshape.144
  271.4 3.1 convolution_convert_fusion
  274.5 3.8 reshape.145
  278.3 6.1 %all-to-all-start.7 = ((bf16[32,4,6144]{2,1,0:T(4,128)(2,1)}), bf16[32,4,6144]{2,1,0:T(4,128)(2,1)S(1)}, u32[]{:S(2)}, u32[]{:S(2)}) async-start(bf16[32,4,6144]{2,1,0:T(4,128)(2,1)} %reshape.145), calls=%async_computation.7 | async-start | bytes 3145728 | tf_op jit(solution)/shard_map/all_to_all | solution.py:157
  284.5 5.4 %fusion.1 = f32[6144,256]{1,0:T(8,128)} fusion(bf16[32,4,256]{2,0,1:T(8,128)(2,1)S(1)} %copy-done.17, bf16[32,4,6144]{2,1,0:T(4,128)(2,1)} %all-to-all-done.6), kind=kOutput, calls=%fused_computation.3 | convolution fusion | flops 405798912 | bytes 7929856 | tf_op jit(solution)/shard_map/dot_general | solution.py:143
  289.9 38.3 %all-to-all-done.7 = bf16[32,4,6144]{2,1,0:T(4,128)(2,1)S(1)} async-done(((bf16[32,4,6144]{2,1,0:T(4,128)(2,1)}), bf16[32,4,6144]{2,1,0:T(4,128)(2,1)S(1)}, u32[]{:S(2)}, u32[]{:S(2)}) %all-to-all-start.7) | async-done | bytes 1572896 | tf_op jit(solution)/shard_map/all_to_all | solution.py:157
  328.9 10.6 %all_to_all.74 = bf16[8,4,768]{2,1,0:T(4,128)(2,1)S(1)} all-to-all(bf16[8,4,768]{2,1,0:T(4,128)(2,1)S(1)} %fusion.31), channel_id=1, replica_groups=mesh['row'=8,'cy'=4,'cz'=8] {'row'}, dimensions={0} | all-to-all | bytes 98304 | tf_op jit(solution)/shard_map/all_to_all | solution.py:73
  340.9 5.8 %all-to-all-start.9 = ((bf16[32,32,768]{2,1,0:T(8,128)(2,1)}), bf16[32,32,768]{2,1,0:T(8,128)(2,1)S(1)}, u32[]{:S(2)}, u32[]{:S(2)}) async-start(bf16[32,32,768]{2,1,0:T(8,128)(2,1)} %broadcast_in_dim.19), calls=%async_computation.9 | async-start | bytes 3145728 | tf_op jit(solution)/shard_map/all_to_all | solution.py:36
  347.3 1.9 all-reduce.4.cloned.1.call-done
  349.2 2.3 constant_dynamic-slice_fusion.2
  351.5 34.4 %all-to-all-done.9 = bf16[32,32,768]{2,1,0:T(8,128)(2,1)S(1)} async-done(((bf16[32,32,768]{2,1,0:T(8,128)(2,1)}), bf16[32,32,768]{2,1,0:T(8,128)(2,1)S(1)}, u32[]{:S(2)}, u32[]{:S(2)}) %all-to-all-start.9) | async-done | bytes 1572896 | tf_op jit(solution)/shard_map/all_to_all | solution.py:36
  387.3 24.7 %all_to_all.75 = bf16[8,128,768]{2,1,0:T(8,128)(2,1)S(1)} all-to-all(bf16[8,128,768]{2,1,0:T(8,128)(2,1)S(1)} %bitcast.88), channel_id=1, replica_groups=mesh['row'=8,'cy'=4,'cz'=8] {'row'}, dimensions={0} | all-to-all | bytes 3145728 | tf_op jit(solution)/shard_map/all_to_all | solution.py:43
  413.7 3.7 all-to-all-start.12
  417.5 14.1 %all_gather.11 = bf16[4,4,4,6144]{3,2,0,1:T(4,128)(2,1)S(1)} all-gather(bf16[1,4,4,6144]{3,2,0,1:T(4,128)(2,1)S(1)} %copy-done.6), channel_id=1, replica_groups=mesh['row'=8,'cy'=4,'cz'=8] {'cy'}, dimensions={0}, use_global_device_ids=true | all-gather | bytes 983040 | tf_op jit(solution)/shard_map/all_gather | solution.py:176
  432.3 11.6 %all-to-all-done.12 = bf16[8,128,768]{2,1,0:T(8,128)(2,1)S(1)} async-done(((bf16[8,128,768]{2,1,0:T(8,128)(2,1)}), bf16[8,128,768]{2,1,0:T(8,128)(2,1)S(1)}, u32[]{:S(2)}, u32[]{:S(2)}) %all-to-all-start.12) | async-done | bytes 1572896 | tf_op jit(solution)/shard_map/all_to_all | solution.py:36
  443.9 3.3 all-to-all-start.10
  447.2 3.9 convolution_convert_fusion.1
  451.1 1.8 all-to-all-done.10
  452.9 10.0 %all-to-all-start.13 = ((bf16[32,32,768]{2,1,0:T(8,128)(2,1)}), bf16[32,32,768]{2,1,0:T(8,128)(2,1)}, u32[]{:S(2)}, u32[]{:S(2)}) async-start(bf16[32,32,768]{2,1,0:T(8,128)(2,1)} %bitcast.85), calls=%async_computation.13 | async-start | bytes 3145728 | tf_op jit(solution)/shard_map/all_to_all | solution.py:43
  463.0 2.5 convolution_convert_fusion.5
  466.1 4.4 convolution_convert_fusion.6
  470.5 31.7 %all-to-all-done.13 = bf16[32,32,768]{2,1,0:T(8,128)(2,1)} async-done(((bf16[32,32,768]{2,1,0:T(8,128)(2,1)}), bf16[32,32,768]{2,1,0:T(8,128)(2,1)}, u32[]{:S(2)}, u32[]{:S(2)}) %all-to-all-start.13) | async-done | bytes 1572896 | tf_op jit(solution)/shard_map/all_to_all | solution.py:43
  502.2 1.8 convert_reduce_fusion
  504.6 1.9 convert_element_type.195
  506.5 1.9 convert_element_type.192
  (89 shorter events, 23.1 us)
Async XLA Ops:
  7.2 235.2 %copy-start = (bf16[6144,256]{1,0:T(8,128)(2,1)S(1)}, bf16[6144,256]{1,0:T(8,128)(2,1)}, u32[]{:S(2)}) copy-start(bf16[6144,256]{1,0:T(8,128)(2,1)} %param.11) | copy-start | bytes 9437188
  17.8 14.0 %copy-start.11 = (bf16[8,4,768]{2,1,0:T(4,128)(2,1)}, bf16[8,4,768]{2,1,0:T(4,128)(2,1)S(1)}, u32[]{:S(2)}) copy-start(bf16[8,4,768]{2,1,0:T(4,128)(2,1)S(1)} %all_to_all.70) | copy-start | bytes 147460
  20.0 11.6 %copy-start.19 = (s32[32,2]{0,1:T(2,128)S(1)}, s32[32,2]{0,1:T(2,128)}, u32[]{:S(2)}) copy-start(s32[32,2]{0,1:T(2,128)} %param.13) | copy-start | bytes 772
  20.0 11.6 %copy-start.20 = (bf16[32,2]{0,1:T(2,128)(2,1)S(1)}, bf16[32,2]{0,1:T(2,128)(2,1)}, u32[]{:S(2)}) copy-start(bf16[32,2]{0,1:T(2,128)(2,1)} %param.14) | copy-start | bytes 388
  20.0 50.7 %all-to-all-start = ((bf16[32,32,768]{2,1,0:T(8,128)(2,1)}), bf16[32,32,768]{2,1,0:T(8,128)(2,1)}, u32[]{:S(2)}, u32[]{:S(2)}) async-start(bf16[32,32,768]{2,1,0:T(8,128)(2,1)} %broadcast_in_dim.14), calls=%async_computation | async-start | bytes 3145728 | tf_op jit(solution)/shard_map/all_to_all | solution.py:36
  98.3 24.2 %copy-start.21 = (bf16[768,768]{1,0:T(8,128)(2,1)S(1)}, bf16[768,768]{1,0:T(8,128)(2,1)}, u32[]{:S(2)}) copy-start(bf16[768,768]{1,0:T(8,128)(2,1)} %param.10) | copy-start | bytes 3538948
  122.5 2.6 copy-start.3
  125.1 48.0 %all-to-all-start.4 = ((bf16[32,32,768]{2,1,0:T(8,128)(2,1)}), bf16[32,32,768]{2,1,0:T(8,128)(2,1)}, u32[]{:S(2)}, u32[]{:S(2)}) async-start(bf16[32,32,768]{2,1,0:T(8,128)(2,1)} %bitcast.86), calls=%async_computation.4 | async-start | bytes 3145728 | tf_op jit(solution)/shard_map/all_to_all | solution.py:43
  130.9 103.9 %all-gather.4.cloned.1.call-start = ((), (), s32[]{:S(2)}) async-start(), calls=%async_computation.18 | async-start | bytes 3244032 | tf_op jit(solution)/shard_map/all_gather | solution.py:103
  173.0 1.7 copy-start.15
  185.5 0.6 copy-start.7
  188.0 54.4 %all-to-all-start.6 = ((bf16[32,4,6144]{2,1,0:T(4,128)(2,1)}), bf16[32,4,6144]{2,1,0:T(4,128)(2,1)}, u32[]{:S(2)}, u32[]{:S(2)}) async-start(bf16[32,4,6144]{2,1,0:T(4,128)(2,1)} %broadcast_in_dim.17), calls=%async_computation.6 | async-start | bytes 3145728 | tf_op jit(solution)/shard_map/all_to_all | solution.py:120
  193.6 155.6 %all-reduce.4.cloned.1.call-start = ((), (), s32[]{:S(2)}) async-start(), calls=%async_computation.19 | async-start | bytes 3145728
  245.7 0.6 copy-start.13
  255.9 248.7 %reduce-scatter.6.cloned.1.call-start = ((), (), s32[]{:S(2)}) async-start(), calls=%async_computation.17 | async-start | bytes 7077888 | tf_op jit(solution)/shard_map/reduce_scatter | solution.py:166
  256.8 3.7 copy-start.14
  256.8 3.7 copy-start.18
  259.4 1.1 copy-start.2
  268.6 0.6 copy-start.16
  278.3 6.2 %copy-start.17 = (bf16[32,4,256]{2,0,1:T(8,128)(2,1)S(1)}, bf16[32,4,256]{2,0,1:T(8,128)(2,1)}, u32[]{:S(2)}) copy-start(bf16[32,4,256]{2,0,1:T(8,128)(2,1)} %copy-done.16) | copy-start | bytes 196612
  278.3 50.0 %all-to-all-start.7 = ((bf16[32,4,6144]{2,1,0:T(4,128)(2,1)}), bf16[32,4,6144]{2,1,0:T(4,128)(2,1)S(1)}, u32[]{:S(2)}, u32[]{:S(2)}) async-start(bf16[32,4,6144]{2,1,0:T(4,128)(2,1)} %reshape.145), calls=%async_computation.7 | async-start | bytes 3145728 | tf_op jit(solution)/shard_map/all_to_all | solution.py:157
  284.5 222.1 %reduce-scatter.4.cloned.1.call-start = ((), (), s32[]{:S(2)}) async-start(), calls=%async_computation.16 | async-start | bytes 7077888 | tf_op jit(solution)/shard_map/reduce_scatter | solution.py:163
  289.9 39.0 %copy-start.12 = (bf16[8,4,768]{2,1,0:T(4,128)(2,1)S(1)}, bf16[8,4,768]{2,1,0:T(4,128)(2,1)}, u32[]{:S(2)}) copy-start(bf16[8,4,768]{2,1,0:T(4,128)(2,1)} %copy-done.11) | copy-start | bytes 147460
  339.5 1.3 copy-start.9
  340.9 5.9 %copy-start.23 = (u32[256]{0:T(256)S(1)}, u32[256]{0:T(256)}, u32[]{:S(2)}) copy-start(u32[256]{0:T(256)} %constant.65) | copy-start | bytes 3076
  340.9 45.0 %copy-start.22 = (bf16[768,768]{1,0:T(8,128)(2,1)S(1)}, bf16[768,768]{1,0:T(8,128)(2,1)}, u32[]{:S(2)}) copy-start(bf16[768,768]{1,0:T(8,128)(2,1)} %param.10) | copy-start | bytes 3538948
  340.9 45.0 %all-to-all-start.9 = ((bf16[32,32,768]{2,1,0:T(8,128)(2,1)}), bf16[32,32,768]{2,1,0:T(8,128)(2,1)S(1)}, u32[]{:S(2)}, u32[]{:S(2)}) async-start(bf16[32,32,768]{2,1,0:T(8,128)(2,1)} %broadcast_in_dim.19), calls=%async_computation.9 | async-start | bytes 3145728 | tf_op jit(solution)/shard_map/all_to_all | solution.py:36
  413.7 3.7 copy-start.6
  413.7 17.9 %copy-start.8 = (bf16[8,4,768]{2,1,0:T(4,128)(2,1)S(1)}, bf16[8,4,768]{2,1,0:T(4,128)(2,1)}, u32[]{:S(2)}) copy-start(bf16[8,4,768]{2,1,0:T(4,128)(2,1)} %copy-done.7) | copy-start | bytes 147460
  413.7 30.1 %all-to-all-start.12 = ((bf16[8,128,768]{2,1,0:T(8,128)(2,1)}), bf16[8,128,768]{2,1,0:T(8,128)(2,1)S(1)}, u32[]{:S(2)}, u32[]{:S(2)}) async-start(bf16[8,128,768]{2,1,0:T(8,128)(2,1)} %broadcast_in_dim.20), calls=%async_computation.12 | async-start | bytes 3145728 | tf_op jit(solution)/shard_map/all_to_all | solution.py:36
  443.8 7.2 %copy-start.5 = (bf16[8,128,768]{2,1,0:T(8,128)(2,1)}, bf16[8,128,768]{2,1,0:T(8,128)(2,1)S(1)}, u32[]{:S(2)}) copy-start(bf16[8,128,768]{2,1,0:T(8,128)(2,1)S(1)} %all-to-all-done.12) | copy-start | bytes 4718596
  443.9 9.1 %all-to-all-start.10 = ((bf16[8,4,768]{2,1,0:T(4,128)(2,1)}), bf16[8,4,768]{2,1,0:T(4,128)(2,1)S(1)}, u32[]{:S(2)}, u32[]{:S(2)}) async-start(bf16[8,4,768]{2,1,0:T(4,128)(2,1)} %fusion.32), calls=%async_computation.10 | async-start | bytes 98304 | tf_op jit(solution)/shard_map/all_to_all | solution.py:73
  452.9 10.0 %copy-start.4 = (bf16[8,128,768]{2,1,0:T(8,128)(2,1)S(1)}, bf16[8,128,768]{2,1,0:T(8,128)(2,1)}, u32[]{:S(2)}) copy-start(bf16[8,128,768]{2,1,0:T(8,128)(2,1)} %copy-done.3) | copy-start | bytes 4718596
  452.9 49.2 %all-to-all-start.13 = ((bf16[32,32,768]{2,1,0:T(8,128)(2,1)}), bf16[32,32,768]{2,1,0:T(8,128)(2,1)}, u32[]{:S(2)}, u32[]{:S(2)}) async-start(bf16[32,32,768]{2,1,0:T(8,128)(2,1)} %bitcast.85), calls=%async_computation.13 | async-start | bytes 3145728 | tf_op jit(solution)/shard_map/all_to_all | solution.py:43
  470.5 33.5 %copy-start.10 = (bf16[32,768]{1,0:T(8,128)(2,1)S(1)}, bf16[32,768]{1,0:T(8,128)(2,1)}, u32[]{:S(2)}) copy-start(bf16[32,768]{1,0:T(8,128)(2,1)} %copy-done.9) | copy-start | bytes 147460
  502.2 6.3 %copy-start.1 = (bf16[6144,256]{1,0:T(8,128)(2,1)S(1)}, bf16[6144,256]{1,0:T(8,128)(2,1)}, u32[]{:S(2)}) copy-start(bf16[6144,256]{1,0:T(8,128)(2,1)} %param.11) | copy-start | bytes 9437188
Sparse Core Ops, SparseCore 0:
  134.8 99.8 all-gather.3
  256.1 93.0 all-reduce.3
  351.7 51.8 reduce-scatter.5
  406.0 63.9 reduce-scatter.3

commit v9 on v6

--- a/solution.py
+++ b/solution.py
@@ -83,7 +83,6 @@
     slot_cap = max(2, 3 * block_len // 4)
     model_width = expert_out.shape[1]
     my_row = lax.axis_index("row")
-    tok_panel = gather_rows(tokens, "col")
     own_grad = swap_blocks(out_grad[None], row_count)[0]
     ids_own = lax.dynamic_slice_in_dim(expert_ids, my_row * block_len, block_len, 0)
     weights_own = lax.dynamic_slice_in_dim(route_weights, my_row * block_len, block_len, 0)
@@ -98,7 +97,8 @@
         ((0, 0), (0, model_width - EXPERTS * block_len)),
     )
     grad_pack = jnp.concatenate([own_grad, table_row], axis=0)
-    tok_panel, grad_pack = lax.optimization_barrier((tok_panel, grad_pack))
+    tokens_ready, grad_pack = lax.optimization_barrier((tokens, grad_pack))
+    tok_panel = gather_rows(tokens_ready, "col")
     pack_all = lax.all_gather(grad_pack, "col", axis=0, tiled=False)
     my_expert = lax.axis_index("col") // group_len
     weights_recv = lax.dynamic_slice_in_dim(
@@ -110,6 +110,7 @@
     up_terms = jnp.dot(tok_panel, w_up, preferred_element_type=jnp.float32)
     preact = scatter_sum(up_terms, "row")
     hidden_full = gather_rows(gelu_tanh(preact).astype(jnp.bfloat16), "row")
+    hidden_full, pack_all = lax.optimization_barrier((hidden_full, pack_all))
     rows_in = hidden_full
     dense_term = scatter_sum(jnp.dot(rows_in, w_down, preferred_element_type=jnp.float32), "col")
     mixed_act = (tokens.astype(jnp.float32) + dense_term).astype(jnp.bfloat16)

time: 505 us -> 493 us (0.976)
  waiting for transfers between devices: 219 us -> 195 us
  blocking collectives: 160 us -> 172 us
    all_to_all x2 -> x3, blocking collectives: 48.5 us -> 93.7 us  [scatter_sum(): got = lax.all_to_all(blocks, axis_name, 0, 0, tiled=True)]
    all_to_all x2 -> x1, waiting for transfers between devices: 69.5 us -> 26.6 us  [scatter_sum(): got = lax.all_to_all(blocks, axis_name, 0, 0, tiled=True)]
    all_gather x1, waiting for transfers between devices: 41.5 us -> 8.28 us  [on_device(): pack_all = lax.all_gather(grad_pack, 'col', axis=0, tiled=False)]
    all_to_all x1, waiting for transfers between devices: 1.55 us -> 33.6 us  [on_device(): got = lax.all_to_all(payload, 'col', 0, 0, tiled=True)]
    all_to_all x3 -> x2, blocking collectives: 93.3 us -> 69.1 us  [gather_rows(): got = lax.all_to_all(spread, axis_name, 0, 0, tiled=True)]
    all_to_all x1 -> x2, waiting for transfers between devices: 38.2 us -> 55.1 us  [gather_rows(): got = lax.all_to_all(spread, axis_name, 0, 0, tiled=True)]
    all_to_all x2 -> x1, blocking collectives: 18.4 us -> 8.78 us  [swap_blocks(): lax.all_to_all(parts.reshape(count, arrays * block, width), 'row', 0, 0,...]
    all_to_all x1, starting transfers between devices: 13.4 us -> 6.92 us  [on_device(): lax.all_to_all(back_flat.astype(jnp.bfloat16).reshape(col_count, 2 * bloc...]
  transfers between devices with their start and end apart: 8 -> 9, of which waited for: 6 -> 7; matrix products, arithmetic and copies ran while one was open for 9% -> 10% of each run, Pallas kernels for 0% -> 0%
where the time goes in v9:
time: 493 us; the launch traced here: 491 us
  waiting for transfers between devices  195 us (40%)
  blocking collectives  172 us (35%)
  starting transfers between devices  37.2 us (8%)
  matrix products  37.2 us (8%)
  local copies, waits for them, and re-layouts  22.5 us (5%)
  between operations  14 us (3%)
  other arithmetic  13.4 us (3%)
    all_to_all x3, blocking collectives, scatter_sum(): got = lax.all_to_all(blocks, axis_name, 0, 0, tiled=True)  93.7 us
    all_to_all x2, blocking collectives, gather_rows(): got = lax.all_to_all(spread, axis_name, 0, 0, tiled=True)  69.1 us
    all_to_all x1, waiting for transfers between devices, on_device(): lax.all_to_all(back_flat.astype(jnp.bfloat16).reshape(col_count, 2 * bloc...  67.2 us
    all_to_all x2, waiting for transfers between devices, gather_rows(): got = lax.all_to_all(spread, axis_name, 0, 0, tiled=True)  55.1 us
    all_to_all x1, waiting for transfers between devices, on_device(): got = lax.all_to_all(payload, 'col', 0, 0, tiled=True)  33.6 us
    all_to_all x1, waiting for transfers between devices, scatter_sum(): got = lax.all_to_all(blocks, axis_name, 0, 0, tiled=True)  26.6 us
    all_to_all x2, starting transfers between devices, gather_rows(): got = lax.all_to_all(spread, axis_name, 0, 0, tiled=True)  15.7 us
  transfers between devices with their start and end apart: 9, of which 7 were waited for; matrix products, arithmetic and copies ran while one was open for 10% of the time, Pallas kernels for 0%

profile of v9, /device:TPU:32, one launch (start us, length us, event | category | flops | bytes accessed | tf_op | source)
XLA Modules:
  0.0 491.3 jit_solution(17078247930205767843)
XLA Ops:
  7.2 1.6 reshape_transpose_reshape_broadcast_in_dim.6
  8.8 4.3 all-to-all-start
  13.1 0.7 constant_dynamic-slice_fusion.2
  13.8 0.7 fusion.33
  14.7 4.0 all-to-all-done
  19.3 2.1 broadcast_in_dim.14
  21.4 11.4 %all-to-all-start.1 = ((bf16[32,32,768]{2,1,0:T(8,128)(2,1)}), bf16[32,32,768]{2,1,0:T(8,128)(2,1)}, u32[]{:S(2)}, u32[]{:S(2)}) async-start(bf16[32,32,768]{2,1,0:T(8,128)(2,1)} %broadcast_in_dim.14), calls=%async_computation.1 | async-start | bytes 3145728 | tf_op jit(solution)/shard_map/all_to_all | solution.py:35
  32.9 0.7 all-gather.4.cloned.1.call-update
  33.6 41.8 %all-to-all-done.1 = bf16[32,32,768]{2,1,0:T(8,128)(2,1)} async-done(((bf16[32,32,768]{2,1,0:T(8,128)(2,1)}), bf16[32,32,768]{2,1,0:T(8,128)(2,1)}, u32[]{:S(2)}, u32[]{:S(2)}) %all-to-all-start.1) | async-done | bytes 1572896 | tf_op jit(solution)/shard_map/all_to_all | solution.py:35
  75.4 3.1 convolution_convert_fusion.3
  78.5 24.0 %all_to_all.60 = bf16[8,128,768]{2,1,0:T(8,128)(2,1)S(1)} all-to-all(bf16[8,128,768]{2,1,0:T(8,128)(2,1)S(1)} %bitcast.85), channel_id=1, replica_groups=mesh['row'=8,'col'=32] {'row'}, dimensions={0} | all-to-all | bytes 3145728 | tf_op jit(solution)/shard_map/all_to_all | solution.py:42
  102.9 1.3 broadcast_in_dim.15
  104.2 4.3 all-to-all-start.3
  108.5 8.3 %all-gather.4.cloned.1.call-done = bf16[32,5,6144]{2,1,0:T(8,128)(2,1)} async-done(((bf16[1,5,6144]{2,1,0:T(8,128)(2,1)}), bf16[32,5,6144]{2,1,0:T(8,128)(2,1)}) %all-gather.4.cloned.1.call-update) | async-done | bytes 1966096 | tf_op jit(solution)/shard_map/all_gather | solution.py:102
  116.8 13.3 %all-to-all-done.3 = bf16[8,128,768]{2,1,0:T(8,128)(2,1)} async-done(((bf16[8,128,768]{2,1,0:T(8,128)(2,1)}), bf16[8,128,768]{2,1,0:T(8,128)(2,1)}, u32[]{:S(2)}, u32[]{:S(2)}) %all-to-all-start.3) | async-done | bytes 1572896 | tf_op jit(solution)/shard_map/all_to_all | solution.py:35
  130.0 3.1 convolution_convert_fusion.2
  133.2 45.3 %all_to_all.61 = bf16[32,32,768]{2,1,0:T(8,128)(2,1)S(1)} all-to-all(bf16[32,32,768]{2,1,0:T(8,128)(2,1)S(1)} %bitcast.86), channel_id=1, replica_groups=mesh['row'=8,'col'=32] {'col'}, dimensions={0} | all-to-all | bytes 3145728 | tf_op jit(solution)/shard_map/all_to_all | solution.py:42
  179.9 1.4 reshape_transpose_reshape_broadcast_in_dim.7
  181.3 8.8 %all_to_all.62 = bf16[8,4,768]{2,1,0:T(4,128)(2,1)S(1)} all-to-all(bf16[8,4,768]{2,1,0:T(4,128)(2,1)} %reshape_transpose_reshape_broadcast_in_dim.7), channel_id=1, replica_groups=mesh['row'=8,'col'=32] {'row'}, dimensions={0} | all-to-all | bytes 98304 | tf_op jit(solution)/shard_map/all_to_all | solution.py:63
  190.1 1.9 broadcast_in_dim.18
  192.0 4.9 all-to-all-start.6
  197.1 0.9 slice.16
  198.8 3.7 slice.17
  202.5 33.6 %all-to-all-done.6 = bf16[32,4,6144]{2,1,0:T(4,128)(2,1)} async-done(((bf16[32,4,6144]{2,1,0:T(4,128)(2,1)}), bf16[32,4,6144]{2,1,0:T(4,128)(2,1)}, u32[]{:S(2)}, u32[]{:S(2)}) %all-to-all-start.6) | async-done | bytes 1572896 | tf_op jit(solution)/shard_map/all_to_all | solution.py:120
  236.1 3.4 multiply_convert_fusion.8
  240.1 4.1 fusion.4
  244.3 0.9 copy.69
  245.2 4.0 fusion.15
  249.8 1.0 fusion.31
  250.8 1.1 fusion
  251.9 1.8 copy.64
  253.8 6.9 %all-to-all-start.7 = ((bf16[256,8,768]{2,1,0:T(8,128)(2,1)}), bf16[256,8,768]{2,1,0:T(8,128)(2,1)S(1)}, u32[]{:S(2)}, u32[]{:S(2)}) async-start(bf16[256,8,768]{2,1,0:T(8,128)(2,1)} %bitcast.20), calls=%async_computation.7 | async-start | bytes 6291456 | tf_op jit(solution)/shard_map/all_to_all | solution.py:146
  260.7 5.5 %fusion.2 = f32[6144,256]{1,0:T(8,128)} fusion(bf16[32,4,256]{2,0,1:T(8,128)(2,1)} %copy-done.14, bf16[32,4,6144]{2,1,0:T(4,128)(2,1)} %all-to-all-done.6), kind=kOutput, calls=%fused_computation.5 | convolution fusion | flops 405798912 | bytes 7929856 | tf_op jit(solution)/shard_map/dot_general | solution.py:140
  267.5 0.8 reshape.142
  268.9 67.2 %all-to-all-done.7 = bf16[256,8,768]{2,1,0:T(8,128)(2,1)S(1)} async-done(((bf16[256,8,768]{2,1,0:T(8,128)(2,1)}), bf16[256,8,768]{2,1,0:T(8,128)(2,1)S(1)}, u32[]{:S(2)}, u32[]{:S(2)}) %all-to-all-start.7) | async-done | bytes 3145760 | tf_op jit(solution)/shard_map/all_to_all | solution.py:146
  337.0 2.3 slice_reduce_fusion
  340.1 44.9 %all_to_all.63 = bf16[32,32,768]{2,1,0:T(8,128)(2,1)S(1)} all-to-all(bf16[32,32,768]{2,1,0:T(8,128)(2,1)S(1)} %broadcast_in_dim.19), channel_id=1, replica_groups=mesh['row'=8,'col'=32] {'col'}, dimensions={0} | all-to-all | bytes 3145728 | tf_op jit(solution)/shard_map/all_to_all | solution.py:35
  385.1 1.4 convolution_convert_fusion.1
  386.5 24.4 %all_to_all.64 = bf16[8,128,768]{2,1,0:T(8,128)(2,1)S(1)} all-to-all(bf16[8,128,768]{2,1,0:T(8,128)(2,1)S(1)} %bitcast.87), channel_id=1, replica_groups=mesh['row'=8,'col'=32] {'row'}, dimensions={0} | all-to-all | bytes 3145728 | tf_op jit(solution)/shard_map/all_to_all | solution.py:42
  411.6 24.2 %all_to_all.65 = bf16[8,128,768]{2,1,0:T(8,128)(2,1)S(1)} all-to-all(bf16[8,128,768]{2,1,0:T(8,128)(2,1)S(1)} %broadcast_in_dim.20), channel_id=1, replica_groups=mesh['row'=8,'col'=32] {'row'}, dimensions={0} | all-to-all | bytes 3145728 | tf_op jit(solution)/shard_map/all_to_all | solution.py:35
  435.7 2.6 convolution_convert_fusion
  438.3 5.1 %all-to-all-start.11 = ((bf16[32,32,768]{2,1,0:T(8,128)(2,1)}), bf16[32,32,768]{2,1,0:T(8,128)(2,1)}, u32[]{:S(2)}, u32[]{:S(2)}) async-start(bf16[32,32,768]{2,1,0:T(8,128)(2,1)} %bitcast.26), calls=%async_computation.11 | async-start | bytes 3145728 | tf_op jit(solution)/shard_map/all_to_all | solution.py:42
  444.1 4.0 convolution_convert_fusion.4
  448.1 3.9 convolution_convert_fusion.5
  452.0 2.1 convert_element_type.172
  454.0 1.9 convert_element_type.169
  456.0 26.6 %all-to-all-done.11 = bf16[32,32,768]{2,1,0:T(8,128)(2,1)} async-done(((bf16[32,32,768]{2,1,0:T(8,128)(2,1)}), bf16[32,32,768]{2,1,0:T(8,128)(2,1)}, u32[]{:S(2)}, u32[]{:S(2)}) %all-to-all-start.11) | async-done | bytes 1572896 | tf_op jit(solution)/shard_map/all_to_all | solution.py:42
  482.5 1.6 convert_reduce_fusion
  (72 shorter events, 10.5 us)
Async XLA Ops:
  7.2 228.9 %copy-start = (bf16[6144,256]{1,0:T(8,128)(2,1)S(1)}, bf16[6144,256]{1,0:T(8,128)(2,1)}, u32[]{:S(2)}) copy-start(bf16[6144,256]{1,0:T(8,128)(2,1)} %param.11) | copy-start | bytes 9437188
  8.8 9.8 %all-to-all-start = ((bf16[8,4,768]{2,1,0:T(4,128)(2,1)}), bf16[8,4,768]{2,1,0:T(4,128)(2,1)S(1)}, u32[]{:S(2)}, u32[]{:S(2)}) async-start(bf16[8,4,768]{2,1,0:T(4,128)(2,1)} %reshape_transpose_reshape_broadcast_in_dim.6), calls=%async_computation | async-start | bytes 98304 | tf_op jit(solution)/shard_map/all_to_all | solution.py:63
  21.4 54.0 %all-to-all-start.1 = ((bf16[32,32,768]{2,1,0:T(8,128)(2,1)}), bf16[32,32,768]{2,1,0:T(8,128)(2,1)}, u32[]{:S(2)}, u32[]{:S(2)}) async-start(bf16[32,32,768]{2,1,0:T(8,128)(2,1)} %broadcast_in_dim.14), calls=%async_computation.1 | async-start | bytes 3145728 | tf_op jit(solution)/shard_map/all_to_all | solution.py:35
  32.8 83.9 %all-gather.4.cloned.1.call-start = ((), (), s32[]{:S(2)}) async-start(), calls=%async_computation.16 | async-start | bytes 3244032 | tf_op jit(solution)/shard_map/all_gather | solution.py:102
  104.2 25.9 %all-to-all-start.3 = ((bf16[8,128,768]{2,1,0:T(8,128)(2,1)}), bf16[8,128,768]{2,1,0:T(8,128)(2,1)}, u32[]{:S(2)}, u32[]{:S(2)}) async-start(bf16[8,128,768]{2,1,0:T(8,128)(2,1)} %broadcast_in_dim.15), calls=%async_computation.3 | async-start | bytes 3145728 | tf_op jit(solution)/shard_map/all_to_all | solution.py:35
  178.5 0.8 copy-start.12
  192.0 44.1 %all-to-all-start.6 = ((bf16[32,4,6144]{2,1,0:T(4,128)(2,1)}), bf16[32,4,6144]{2,1,0:T(4,128)(2,1)}, u32[]{:S(2)}, u32[]{:S(2)}) async-start(bf16[32,4,6144]{2,1,0:T(4,128)(2,1)} %broadcast_in_dim.18), calls=%async_computation.6 | async-start | bytes 3145728 | tf_op jit(solution)/shard_map/all_to_all | solution.py:120
  196.9 255.1 %reduce-scatter.5.cloned.1.call-start = ((), (), s32[]{:S(2)}) async-start(), calls=%async_computation.15 | async-start | bytes 7077888 | tf_op jit(solution)/shard_map/reduce_scatter | solution.py:171
  198.8 3.7 copy-start.15
  236.1 4.1 copy-start.2
  239.5 0.6 copy-start.11
  245.2 4.6 copy-start.3
  249.2 0.6 copy-start.14
  253.8 82.3 %all-to-all-start.7 = ((bf16[256,8,768]{2,1,0:T(8,128)(2,1)}), bf16[256,8,768]{2,1,0:T(8,128)(2,1)S(1)}, u32[]{:S(2)}, u32[]{:S(2)}) async-start(bf16[256,8,768]{2,1,0:T(8,128)(2,1)} %bitcast.20), calls=%async_computation.7 | async-start | bytes 6291456 | tf_op jit(solution)/shard_map/all_to_all | solution.py:146
  260.7 193.4 %reduce-scatter.3.cloned.1.call-start = ((), (), s32[]{:S(2)}) async-start(), calls=%async_computation.14 | async-start | bytes 7077888 | tf_op jit(solution)/shard_map/reduce_scatter | solution.py:168
  266.2 0.7 copy-start.17
  266.2 0.7 copy-start.16
  336.1 0.9 copy-start.6
  337.0 2.3 copy-start.13
  339.3 0.6 copy-start.7
  340.1 45.0 %copy-start.18 = (bf16[768,768]{1,0:T(8,128)(2,1)S(1)}, bf16[768,768]{1,0:T(8,128)(2,1)}, u32[]{:S(2)}) copy-start(bf16[768,768]{1,0:T(8,128)(2,1)} %param.10) | copy-start | bytes 3538948
  411.6 24.2 %copy-start.19 = (bf16[768,768]{1,0:T(8,128)(2,1)S(1)}, bf16[768,768]{1,0:T(8,128)(2,1)}, u32[]{:S(2)}) copy-start(bf16[768,768]{1,0:T(8,128)(2,1)} %param.9) | copy-start | bytes 3538948
  435.7 2.6 copy-start.4
  438.3 5.1 %copy-start.10 = (f32[8,4,768]{2,1,0:T(4,128)S(1)}, f32[8,4,768]{2,1,0:T(4,128)}, u32[]{:S(2)}) copy-start(f32[8,4,768]{2,1,0:T(4,128)} %get-tuple-element.13) | copy-start | bytes 294916
  438.3 5.2 %copy-start.9 = (bf16[32,768]{1,0:T(8,128)(2,1)S(1)}, bf16[32,768]{1,0:T(8,128)(2,1)}, u32[]{:S(2)}) copy-start(bf16[32,768]{1,0:T(8,128)(2,1)} %add_convert_fusion.3) | copy-start | bytes 147460
  438.3 44.2 %all-to-all-start.11 = ((bf16[32,32,768]{2,1,0:T(8,128)(2,1)}), bf16[32,32,768]{2,1,0:T(8,128)(2,1)}, u32[]{:S(2)}, u32[]{:S(2)}) async-start(bf16[32,32,768]{2,1,0:T(8,128)(2,1)} %bitcast.26), calls=%async_computation.11 | async-start | bytes 3145728 | tf_op jit(solution)/shard_map/all_to_all | solution.py:42
  444.1 4.0 copy-start.5
  452.0 32.9 %copy-start.1 = (bf16[6144,256]{1,0:T(8,128)(2,1)S(1)}, bf16[6144,256]{1,0:T(8,128)(2,1)}, u32[]{:S(2)}) copy-start(bf16[6144,256]{1,0:T(8,128)(2,1)} %param.11) | copy-start | bytes 9437188
  454.0 30.2 %copy-start.8 = (bf16[32,768]{1,0:T(8,128)(2,1)S(1)}, bf16[32,768]{1,0:T(8,128)(2,1)}, u32[]{:S(2)}) copy-start(bf16[32,768]{1,0:T(8,128)(2,1)} %copy-done.7) | copy-start | bytes 147460
Sparse Core Ops, SparseCore 0:
  36.8 79.9 all-gather.3
  244.4 62.4 reduce-scatter.4
  309.4 50.1 reduce-scatter.2

commit v10 on v9

--- a/solution.py
+++ b/solution.py
@@ -110,9 +110,11 @@
     up_terms = jnp.dot(tok_panel, w_up, preferred_element_type=jnp.float32)
     preact = scatter_sum(up_terms, "row")
     hidden_full = gather_rows(gelu_tanh(preact).astype(jnp.bfloat16), "row")
-    hidden_full, pack_all = lax.optimization_barrier((hidden_full, pack_all))
     rows_in = hidden_full
-    dense_term = scatter_sum(jnp.dot(rows_in, w_down, preferred_element_type=jnp.float32), "col")
+    down_terms, pack_all = lax.optimization_barrier(
+        (jnp.dot(rows_in, w_down, preferred_element_type=jnp.float32), pack_all)
+    )
+    dense_term = scatter_sum(down_terms, "col")
     mixed_act = (tokens.astype(jnp.float32) + dense_term).astype(jnp.bfloat16)
     own_rows = swap_blocks(mixed_act[None], row_count)[0]
     scaled_flat = grad_rows_in.reshape(col_count * block_len, model_width)

time: 493 us -> 491 us (level)
  blocking collectives: 172 us -> 196 us
  waiting for transfers between devices: 195 us -> 175 us
    all_to_all x2 -> x3, blocking collectives: 69.1 us -> 93.3 us  [gather_rows(): got = lax.all_to_all(spread, axis_name, 0, 0, tiled=True)]
    all_to_all x2 -> x1, waiting for transfers between devices: 55.1 us -> 41.8 us  [gather_rows(): got = lax.all_to_all(spread, axis_name, 0, 0, tiled=True)]
    all_gather x1, waiting for transfers between devices: 8.28 us -> 0.01 us  [on_device(): pack_all = lax.all_gather(grad_pack, 'col', axis=0, tiled=False)]
    all_to_all x2 -> x1, starting transfers between devices: 15.7 us -> 11.4 us  [gather_rows(): got = lax.all_to_all(spread, axis_name, 0, 0, tiled=True)]
  transfers between devices with their start and end apart: 9 -> 8, of which waited for: 7 -> 5; matrix products, arithmetic and copies ran while one was open for 10% -> 10% of each run, Pallas kernels for 0% -> 0%
where the time goes in v10:
time: 491 us; the launch traced here: 489 us
  blocking collectives  196 us (40%)
  waiting for transfers between devices  175 us (36%)
  matrix products  35.1 us (7%)
  starting transfers between devices  33 us (7%)
  local copies, waits for them, and re-layouts  22.5 us (5%)
  between operations  14 us (3%)
  other arithmetic  13.4 us (3%)
    all_to_all x3, blocking collectives, scatter_sum(): got = lax.all_to_all(blocks, axis_name, 0, 0, tiled=True)  93.9 us
    all_to_all x3, blocking collectives, gather_rows(): got = lax.all_to_all(spread, axis_name, 0, 0, tiled=True)  93.3 us
    all_to_all x1, waiting for transfers between devices, on_device(): lax.all_to_all(back_flat.astype(jnp.bfloat16).reshape(col_count, 2 * bloc...  67.2 us
    all_to_all x1, waiting for transfers between devices, gather_rows(): got = lax.all_to_all(spread, axis_name, 0, 0, tiled=True)  41.8 us
    all_to_all x1, waiting for transfers between devices, on_device(): got = lax.all_to_all(payload, 'col', 0, 0, tiled=True)  33.5 us
    all_to_all x1, waiting for transfers between devices, scatter_sum(): got = lax.all_to_all(blocks, axis_name, 0, 0, tiled=True)  28.1 us
    all_to_all x1, starting transfers between devices, gather_rows(): got = lax.all_to_all(spread, axis_name, 0, 0, tiled=True)  11.4 us
  transfers between devices with their start and end apart: 8, of which 5 were waited for; matrix products, arithmetic and copies ran while one was open for 10% of the time, Pallas kernels for 0%

profile of v10, /device:TPU:32, one launch (start us, length us, event | category | flops | bytes accessed | tf_op | source)
XLA Modules:
  0.0 489.2 jit_solution(7330491538299597089)
XLA Ops:
  7.2 1.6 reshape_transpose_reshape_broadcast_in_dim.6
  8.8 4.3 all-to-all-start
  13.1 0.7 constant_dynamic-slice_fusion.2
  13.8 0.7 fusion.33
  14.7 4.0 all-to-all-done
  18.6 0.7 fusion.32
  19.3 2.1 broadcast_in_dim.14
  21.4 11.4 %all-to-all-start.1 = ((bf16[32,32,768]{2,1,0:T(8,128)(2,1)}), bf16[32,32,768]{2,1,0:T(8,128)(2,1)}, u32[]{:S(2)}, u32[]{:S(2)}) async-start(bf16[32,32,768]{2,1,0:T(8,128)(2,1)} %broadcast_in_dim.14), calls=%async_computation.1 | async-start | bytes 3145728 | tf_op jit(solution)/shard_map/all_to_all | solution.py:35
  32.9 0.7 all-gather.4.cloned.1.call-update
  33.6 41.8 %all-to-all-done.1 = bf16[32,32,768]{2,1,0:T(8,128)(2,1)} async-done(((bf16[32,32,768]{2,1,0:T(8,128)(2,1)}), bf16[32,32,768]{2,1,0:T(8,128)(2,1)}, u32[]{:S(2)}, u32[]{:S(2)}) %all-to-all-start.1) | async-done | bytes 1572896 | tf_op jit(solution)/shard_map/all_to_all | solution.py:35
  75.4 3.1 convolution_convert_fusion.2
  78.5 24.0 %all_to_all.60 = bf16[8,128,768]{2,1,0:T(8,128)(2,1)S(1)} all-to-all(bf16[8,128,768]{2,1,0:T(8,128)(2,1)S(1)} %bitcast.88), channel_id=1, replica_groups=mesh['row'=8,'col'=32] {'row'}, dimensions={0} | all-to-all | bytes 3145728 | tf_op jit(solution)/shard_map/all_to_all | solution.py:42
  103.0 24.2 %all_to_all.61 = bf16[8,128,768]{2,1,0:T(8,128)(2,1)S(1)} all-to-all(bf16[8,128,768]{2,1,0:T(8,128)(2,1)S(1)} %broadcast_in_dim.15), channel_id=1, replica_groups=mesh['row'=8,'col'=32] {'row'}, dimensions={0} | all-to-all | bytes 3145728 | tf_op jit(solution)/shard_map/all_to_all | solution.py:35
  127.2 1.2 copy-done.4
  128.4 2.5 fusion.36
  130.9 45.4 %all_to_all.62 = bf16[32,32,768]{2,1,0:T(8,128)(2,1)S(1)} all-to-all(bf16[32,32,768]{2,1,0:T(8,128)(2,1)} %bitcast.87), channel_id=1, replica_groups=mesh['row'=8,'col'=32] {'col'}, dimensions={0} | all-to-all | bytes 3145728 | tf_op jit(solution)/shard_map/all_to_all | solution.py:42
  177.8 1.4 reshape_transpose_reshape_broadcast_in_dim.7
  179.2 8.8 %all_to_all.63 = bf16[8,4,768]{2,1,0:T(4,128)(2,1)S(1)} all-to-all(bf16[8,4,768]{2,1,0:T(4,128)(2,1)} %reshape_transpose_reshape_broadcast_in_dim.7), channel_id=1, replica_groups=mesh['row'=8,'col'=32] {'row'}, dimensions={0} | all-to-all | bytes 98304 | tf_op jit(solution)/shard_map/all_to_all | solution.py:63
  188.0 1.9 broadcast_in_dim.18
  189.8 4.9 %all-to-all-start.6 = ((bf16[32,4,6144]{2,1,0:T(4,128)(2,1)}), bf16[32,4,6144]{2,1,0:T(4,128)(2,1)}, u32[]{:S(2)}, u32[]{:S(2)}) async-start(bf16[32,4,6144]{2,1,0:T(4,128)(2,1)} %broadcast_in_dim.18), calls=%async_computation.6 | async-start | bytes 3145728 | tf_op jit(solution)/shard_map/all_to_all | solution.py:122
  195.0 0.9 slice.16
  196.6 3.7 slice.17
  200.3 33.5 %all-to-all-done.6 = bf16[32,4,6144]{2,1,0:T(4,128)(2,1)} async-done(((bf16[32,4,6144]{2,1,0:T(4,128)(2,1)}), bf16[32,4,6144]{2,1,0:T(4,128)(2,1)}, u32[]{:S(2)}, u32[]{:S(2)}) %all-to-all-start.6) | async-done | bytes 1572896 | tf_op jit(solution)/shard_map/all_to_all | solution.py:122
  233.9 3.4 multiply_convert_fusion.8
  238.0 4.1 fusion.4
  242.1 0.9 copy.69
  243.0 4.0 fusion.15
  247.6 1.0 fusion.31
  248.6 1.1 fusion
  249.7 1.8 copy.64
  251.5 7.0 %all-to-all-start.7 = ((bf16[256,8,768]{2,1,0:T(8,128)(2,1)}), bf16[256,8,768]{2,1,0:T(8,128)(2,1)S(1)}, u32[]{:S(2)}, u32[]{:S(2)}) async-start(bf16[256,8,768]{2,1,0:T(8,128)(2,1)} %bitcast.20), calls=%async_computation.7 | async-start | bytes 6291456 | tf_op jit(solution)/shard_map/all_to_all | solution.py:148
  258.6 5.5 %fusion.2 = f32[6144,256]{1,0:T(8,128)} fusion(bf16[32,4,256]{2,0,1:T(8,128)(2,1)} %copy-done.16, bf16[32,4,6144]{2,1,0:T(4,128)(2,1)} %all-to-all-done.6), kind=kOutput, calls=%fused_computation.5 | convolution fusion | flops 405798912 | bytes 7929856 | tf_op jit(solution)/shard_map/dot_general | solution.py:142
  265.4 0.8 reshape.142
  266.1 0.7 broadcast_bitcast_fusion
  266.8 67.2 %all-to-all-done.7 = bf16[256,8,768]{2,1,0:T(8,128)(2,1)S(1)} async-done(((bf16[256,8,768]{2,1,0:T(8,128)(2,1)}), bf16[256,8,768]{2,1,0:T(8,128)(2,1)S(1)}, u32[]{:S(2)}, u32[]{:S(2)}) %all-to-all-start.7) | async-done | bytes 3145760 | tf_op jit(solution)/shard_map/all_to_all | solution.py:148
  334.9 2.3 slice_reduce_fusion
  338.0 45.0 %all_to_all.64 = bf16[32,32,768]{2,1,0:T(8,128)(2,1)S(1)} all-to-all(bf16[32,32,768]{2,1,0:T(8,128)(2,1)S(1)} %broadcast_in_dim.19), channel_id=1, replica_groups=mesh['row'=8,'col'=32] {'col'}, dimensions={0} | all-to-all | bytes 3145728 | tf_op jit(solution)/shard_map/all_to_all | solution.py:35
  383.0 1.4 convolution_convert_fusion.1
  384.4 24.4 %all_to_all.65 = bf16[8,128,768]{2,1,0:T(8,128)(2,1)S(1)} all-to-all(bf16[8,128,768]{2,1,0:T(8,128)(2,1)S(1)} %bitcast.89), channel_id=1, replica_groups=mesh['row'=8,'col'=32] {'row'}, dimensions={0} | all-to-all | bytes 3145728 | tf_op jit(solution)/shard_map/all_to_all | solution.py:42
  409.4 24.2 %all_to_all.66 = bf16[8,128,768]{2,1,0:T(8,128)(2,1)S(1)} all-to-all(bf16[8,128,768]{2,1,0:T(8,128)(2,1)S(1)} %broadcast_in_dim.20), channel_id=1, replica_groups=mesh['row'=8,'col'=32] {'row'}, dimensions={0} | all-to-all | bytes 3145728 | tf_op jit(solution)/shard_map/all_to_all | solution.py:35
  433.6 2.6 convolution_convert_fusion
  436.2 5.1 %all-to-all-start.11 = ((bf16[32,32,768]{2,1,0:T(8,128)(2,1)}), bf16[32,32,768]{2,1,0:T(8,128)(2,1)}, u32[]{:S(2)}, u32[]{:S(2)}) async-start(bf16[32,32,768]{2,1,0:T(8,128)(2,1)} %bitcast.26), calls=%async_computation.11 | async-start | bytes 3145728 | tf_op jit(solution)/shard_map/all_to_all | solution.py:42
  442.0 2.5 convolution_convert_fusion.3
  444.5 3.9 convolution_convert_fusion.4
  448.3 2.1 convert_element_type.172
  450.4 1.9 convert_element_type.169
  452.3 28.1 %all-to-all-done.11 = bf16[32,32,768]{2,1,0:T(8,128)(2,1)} async-done(((bf16[32,32,768]{2,1,0:T(8,128)(2,1)}), bf16[32,32,768]{2,1,0:T(8,128)(2,1)}, u32[]{:S(2)}, u32[]{:S(2)}) %all-to-all-start.11) | async-done | bytes 1572896 | tf_op jit(solution)/shard_map/all_to_all | solution.py:42
  480.4 1.6 convert_reduce_fusion
  (77 shorter events, 9.2 us)
Async XLA Ops:
  7.2 226.7 %copy-start = (bf16[6144,256]{1,0:T(8,128)(2,1)S(1)}, bf16[6144,256]{1,0:T(8,128)(2,1)}, u32[]{:S(2)}) copy-start(bf16[6144,256]{1,0:T(8,128)(2,1)} %param.11) | copy-start | bytes 9437188
  8.8 9.8 %all-to-all-start = ((bf16[8,4,768]{2,1,0:T(4,128)(2,1)}), bf16[8,4,768]{2,1,0:T(4,128)(2,1)S(1)}, u32[]{:S(2)}, u32[]{:S(2)}) async-start(bf16[8,4,768]{2,1,0:T(4,128)(2,1)} %reshape_transpose_reshape_broadcast_in_dim.6), calls=%async_computation | async-start | bytes 98304 | tf_op jit(solution)/shard_map/all_to_all | solution.py:63
  21.4 54.0 %all-to-all-start.1 = ((bf16[32,32,768]{2,1,0:T(8,128)(2,1)}), bf16[32,32,768]{2,1,0:T(8,128)(2,1)}, u32[]{:S(2)}, u32[]{:S(2)}) async-start(bf16[32,32,768]{2,1,0:T(8,128)(2,1)} %broadcast_in_dim.14), calls=%async_computation.1 | async-start | bytes 3145728 | tf_op jit(solution)/shard_map/all_to_all | solution.py:35
  32.8 98.1 %all-gather.4.cloned.1.call-start = ((), (), s32[]{:S(2)}) async-start(), calls=%async_computation.16 | async-start | bytes 3244032 | tf_op jit(solution)/shard_map/all_gather | solution.py:102
  103.0 25.4 %copy-start.20 = (bf16[768,768]{1,0:T(8,128)(2,1)S(1)}, bf16[768,768]{1,0:T(8,128)(2,1)}, u32[]{:S(2)}) copy-start(bf16[768,768]{1,0:T(8,128)(2,1)} %param.10) | copy-start | bytes 3538948
  127.2 1.2 copy-start.4
  176.3 0.8 copy-start.14
  189.8 44.0 %all-to-all-start.6 = ((bf16[32,4,6144]{2,1,0:T(4,128)(2,1)}), bf16[32,4,6144]{2,1,0:T(4,128)(2,1)}, u32[]{:S(2)}, u32[]{:S(2)}) async-start(bf16[32,4,6144]{2,1,0:T(4,128)(2,1)} %broadcast_in_dim.18), calls=%async_computation.6 | async-start | bytes 3145728 | tf_op jit(solution)/shard_map/all_to_all | solution.py:122
  194.7 253.6 %reduce-scatter.5.cloned.1.call-start = ((), (), s32[]{:S(2)}) async-start(), calls=%async_computation.15 | async-start | bytes 7077888 | tf_op jit(solution)/shard_map/reduce_scatter | solution.py:173
  196.6 3.7 copy-start.17
  233.9 4.1 copy-start.2
  237.3 0.6 copy-start.13
  243.0 4.6 copy-start.3
  247.0 0.6 copy-start.16
  251.5 82.4 %all-to-all-start.7 = ((bf16[256,8,768]{2,1,0:T(8,128)(2,1)}), bf16[256,8,768]{2,1,0:T(8,128)(2,1)S(1)}, u32[]{:S(2)}, u32[]{:S(2)}) async-start(bf16[256,8,768]{2,1,0:T(8,128)(2,1)} %bitcast.20), calls=%async_computation.7 | async-start | bytes 6291456 | tf_op jit(solution)/shard_map/all_to_all | solution.py:148
  258.6 191.8 %reduce-scatter.3.cloned.1.call-start = ((), (), s32[]{:S(2)}) async-start(), calls=%async_computation.14 | async-start | bytes 7077888 | tf_op jit(solution)/shard_map/reduce_scatter | solution.py:170
  264.1 0.7 copy-start.19
  264.1 0.7 copy-start.18
  334.0 0.9 copy-start.8
  334.9 2.3 copy-start.15
  337.2 0.6 copy-start.9
  338.0 45.0 %copy-start.21 = (bf16[768,768]{1,0:T(8,128)(2,1)S(1)}, bf16[768,768]{1,0:T(8,128)(2,1)}, u32[]{:S(2)}) copy-start(bf16[768,768]{1,0:T(8,128)(2,1)} %param.10) | copy-start | bytes 3538948
  409.4 24.2 %copy-start.22 = (bf16[768,768]{1,0:T(8,128)(2,1)S(1)}, bf16[768,768]{1,0:T(8,128)(2,1)}, u32[]{:S(2)}) copy-start(bf16[768,768]{1,0:T(8,128)(2,1)} %param.9) | copy-start | bytes 3538948
  433.6 2.6 copy-start.6
  436.2 5.1 %copy-start.12 = (f32[8,4,768]{2,1,0:T(4,128)S(1)}, f32[8,4,768]{2,1,0:T(4,128)}, u32[]{:S(2)}) copy-start(f32[8,4,768]{2,1,0:T(4,128)} %get-tuple-element.13) | copy-start | bytes 294916
  436.2 5.2 %copy-start.11 = (bf16[32,768]{1,0:T(8,128)(2,1)S(1)}, bf16[32,768]{1,0:T(8,128)(2,1)}, u32[]{:S(2)}) copy-start(bf16[32,768]{1,0:T(8,128)(2,1)} %add_convert_fusion.3) | copy-start | bytes 147460
  436.2 5.8 %copy-start.5 = (bf16[8,128,768]{2,1,0:T(8,128)(2,1)S(1)}, bf16[8,128,768]{2,1,0:T(8,128)(2,1)}, u32[]{:S(2)}) copy-start(bf16[8,128,768]{2,1,0:T(8,128)(2,1)} %copy-done.4) | copy-start | bytes 4718596
  436.2 44.2 %all-to-all-start.11 = ((bf16[32,32,768]{2,1,0:T(8,128)(2,1)}), bf16[32,32,768]{2,1,0:T(8,128)(2,1)}, u32[]{:S(2)}, u32[]{:S(2)}) async-start(bf16[32,32,768]{2,1,0:T(8,128)(2,1)} %bitcast.26), calls=%async_computation.11 | async-start | bytes 3145728 | tf_op jit(solution)/shard_map/all_to_all | solution.py:42
  442.0 2.5 copy-start.7
  448.3 34.4 %copy-start.1 = (bf16[6144,256]{1,0:T(8,128)(2,1)S(1)}, bf16[6144,256]{1,0:T(8,128)(2,1)}, u32[]{:S(2)}) copy-start(bf16[6144,256]{1,0:T(8,128)(2,1)} %param.11) | copy-start | bytes 9437188
  450.4 31.7 %copy-start.10 = (bf16[32,768]{1,0:T(8,128)(2,1)S(1)}, bf16[32,768]{1,0:T(8,128)(2,1)}, u32[]{:S(2)}) copy-start(bf16[32,768]{1,0:T(8,128)(2,1)} %copy-done.9) | copy-start | bytes 147460
Sparse Core Ops, SparseCore 0:
  36.8 79.9 all-gather.3
  242.2 62.4 reduce-scatter.4
  307.3 50.1 reduce-scatter.2

commit v11 on v9

--- a/solution.py
+++ b/solution.py
@@ -110,9 +110,9 @@
     up_terms = jnp.dot(tok_panel, w_up, preferred_element_type=jnp.float32)
     preact = scatter_sum(up_terms, "row")
     hidden_full = gather_rows(gelu_tanh(preact).astype(jnp.bfloat16), "row")
-    hidden_full, pack_all = lax.optimization_barrier((hidden_full, pack_all))
     rows_in = hidden_full
     dense_term = scatter_sum(jnp.dot(rows_in, w_down, preferred_element_type=jnp.float32), "col")
+    dense_term, pack_all = lax.optimization_barrier((dense_term, pack_all))
     mixed_act = (tokens.astype(jnp.float32) + dense_term).astype(jnp.bfloat16)
     own_rows = swap_blocks(mixed_act[None], row_count)[0]
     scaled_flat = grad_rows_in.reshape(col_count * block_len, model_width)

time: 493 us -> 508 us (1.030)
  blocking collectives: 172 us -> 228 us
  waiting for transfers between devices: 195 us -> 166 us
  starting transfers between devices: 37.2 us -> 28.3 us
    all_to_all x2 -> x3, blocking collectives: 69.1 us -> 120 us  [gather_rows(): got = lax.all_to_all(spread, axis_name, 0, 0, tiled=True)]
    all_to_all x2 -> x1, waiting for transfers between devices: 55.1 us -> 20.8 us  [gather_rows(): got = lax.all_to_all(spread, axis_name, 0, 0, tiled=True)]
    all_to_all x2 -> x1, starting transfers between devices: 15.7 us -> 4.3 us  [gather_rows(): got = lax.all_to_all(spread, axis_name, 0, 0, tiled=True)]
    all_to_all x3, blocking collectives: 93.7 us -> 99.2 us  [scatter_sum(): got = lax.all_to_all(blocks, axis_name, 0, 0, tiled=True)]
  transfers between devices with their start and end apart: 9 -> 8, of which waited for: 7 -> 6; matrix products, arithmetic and copies ran while one was open for 10% -> 9% of each run, Pallas kernels for 0% -> 0%
where the time goes in v11:
time: 508 us; the launch traced here: 507 us
  blocking collectives  228 us (45%)
  waiting for transfers between devices  166 us (33%)
  matrix products  34.1 us (7%)
  starting transfers between devices  28.3 us (6%)
  local copies, waits for them, and re-layouts  20.8 us (4%)
  other arithmetic  14.9 us (3%)
  between operations  14 us (3%)
    all_to_all x3, blocking collectives, gather_rows(): got = lax.all_to_all(spread, axis_name, 0, 0, tiled=True)  120 us
    all_to_all x3, blocking collectives, scatter_sum(): got = lax.all_to_all(blocks, axis_name, 0, 0, tiled=True)  99.2 us
    all_to_all x1, waiting for transfers between devices, on_device(): lax.all_to_all(back_flat.astype(jnp.bfloat16).reshape(col_count, 2 * bloc...  67.2 us
    all_to_all x1, waiting for transfers between devices, on_device(): got = lax.all_to_all(payload, 'col', 0, 0, tiled=True)  33.6 us
    all_to_all x1, waiting for transfers between devices, scatter_sum(): got = lax.all_to_all(blocks, axis_name, 0, 0, tiled=True)  27.9 us
    all_to_all x1, waiting for transfers between devices, gather_rows(): got = lax.all_to_all(spread, axis_name, 0, 0, tiled=True)  20.8 us
    all_gather x1, waiting for transfers between devices, on_device(): pack_all = lax.all_gather(grad_pack, 'col', axis=0, tiled=False)  12 us
  transfers between devices with their start and end apart: 8, of which 6 were waited for; matrix products, arithmetic and copies ran while one was open for 9% of the time, Pallas kernels for 0%

profile of v11, /device:TPU:32, one launch (start us, length us, event | category | flops | bytes accessed | tf_op | source)
XLA Modules:
  0.0 506.7 jit_solution(15011932686920327773)
XLA Ops:
  7.2 1.6 reshape_transpose_reshape_broadcast_in_dim.6
  8.8 4.3 all-to-all-start
  13.1 0.7 constant_dynamic-slice_fusion.2
  13.8 0.7 fusion.33
  14.7 4.0 all-to-all-done
  19.3 1.0 broadcast_in_dim.14
  20.3 51.3 %all_to_all.60 = bf16[32,32,768]{2,1,0:T(8,128)(2,1)S(1)} all-to-all(bf16[32,32,768]{2,1,0:T(8,128)(2,1)S(1)} %broadcast_in_dim.14), channel_id=1, replica_groups=mesh['row'=8,'col'=32] {'col'}, dimensions={0} | all-to-all | bytes 3145728 | tf_op jit(solution)/shard_map/all_to_all | solution.py:35
  71.6 1.4 convolution_convert_fusion.3
  73.0 24.0 %all_to_all.61 = bf16[8,128,768]{2,1,0:T(8,128)(2,1)S(1)} all-to-all(bf16[8,128,768]{2,1,0:T(8,128)(2,1)S(1)} %bitcast.87), channel_id=1, replica_groups=mesh['row'=8,'col'=32] {'row'}, dimensions={0} | all-to-all | bytes 3145728 | tf_op jit(solution)/shard_map/all_to_all | solution.py:42
  97.4 1.3 broadcast_in_dim.15
  98.6 4.3 all-to-all-start.3
  103.7 20.8 %all-to-all-done.3 = bf16[8,128,768]{2,1,0:T(8,128)(2,1)} async-done(((bf16[8,128,768]{2,1,0:T(8,128)(2,1)}), bf16[8,128,768]{2,1,0:T(8,128)(2,1)}, u32[]{:S(2)}, u32[]{:S(2)}) %all-to-all-start.3) | async-done | bytes 1572896 | tf_op jit(solution)/shard_map/all_to_all | solution.py:35
  124.5 3.1 convolution_convert_fusion.2
  127.6 50.8 %all_to_all.62 = bf16[32,32,768]{2,1,0:T(8,128)(2,1)S(1)} all-to-all(bf16[32,32,768]{2,1,0:T(8,128)(2,1)S(1)} %bitcast.88), channel_id=1, replica_groups=mesh['row'=8,'col'=32] {'col'}, dimensions={0} | all-to-all | bytes 3145728 | tf_op jit(solution)/shard_map/all_to_all | solution.py:42
  178.4 0.9 convert_reduce_fusion.2
  179.3 12.0 %all-gather.4.cloned.1.call-done = bf16[32,5,6144]{2,1,0:T(8,128)(2,1)} async-done(((bf16[1,5,6144]{2,1,0:T(8,128)(2,1)}), bf16[32,5,6144]{2,1,0:T(8,128)(2,1)}) %all-gather.4.cloned.1.call-update) | async-done | bytes 1966096 | tf_op jit(solution)/shard_map/all_gather | solution.py:102
  191.3 1.5 add_convert_fusion.3
  192.8 1.4 reshape_transpose_reshape_broadcast_in_dim.7
  194.3 8.8 %all_to_all.63 = bf16[8,4,768]{2,1,0:T(4,128)(2,1)S(1)} all-to-all(bf16[8,4,768]{2,1,0:T(4,128)(2,1)} %reshape_transpose_reshape_broadcast_in_dim.7), channel_id=1, replica_groups=mesh['row'=8,'col'=32] {'row'}, dimensions={0} | all-to-all | bytes 98304 | tf_op jit(solution)/shard_map/all_to_all | solution.py:63
  203.0 1.9 broadcast_in_dim.18
  204.9 7.4 %all-to-all-start.6 = ((bf16[32,4,6144]{2,1,0:T(4,128)(2,1)}), bf16[32,4,6144]{2,1,0:T(4,128)(2,1)}, u32[]{:S(2)}, u32[]{:S(2)}) async-start(bf16[32,4,6144]{2,1,0:T(4,128)(2,1)} %broadcast_in_dim.18), calls=%async_computation.6 | async-start | bytes 3145728 | tf_op jit(solution)/shard_map/all_to_all | solution.py:120
  212.5 0.9 slice.16
  214.1 3.7 slice.17
  217.9 33.6 %all-to-all-done.6 = bf16[32,4,6144]{2,1,0:T(4,128)(2,1)} async-done(((bf16[32,4,6144]{2,1,0:T(4,128)(2,1)}), bf16[32,4,6144]{2,1,0:T(4,128)(2,1)}, u32[]{:S(2)}, u32[]{:S(2)}) %all-to-all-start.6) | async-done | bytes 1572896 | tf_op jit(solution)/shard_map/all_to_all | solution.py:120
  251.4 3.4 multiply_convert_fusion.8
  255.5 4.1 fusion.4
  259.7 0.9 copy.69
  260.6 4.0 fusion.15
  265.2 1.0 fusion.31
  266.2 1.1 fusion
  267.3 1.8 copy.64
  269.1 6.9 %all-to-all-start.7 = ((bf16[256,8,768]{2,1,0:T(8,128)(2,1)}), bf16[256,8,768]{2,1,0:T(8,128)(2,1)S(1)}, u32[]{:S(2)}, u32[]{:S(2)}) async-start(bf16[256,8,768]{2,1,0:T(8,128)(2,1)} %bitcast.20), calls=%async_computation.7 | async-start | bytes 6291456 | tf_op jit(solution)/shard_map/all_to_all | solution.py:146
  276.1 5.5 %fusion.2 = f32[6144,256]{1,0:T(8,128)} fusion(bf16[32,4,256]{2,0,1:T(8,128)(2,1)} %copy-done.15, bf16[32,4,6144]{2,1,0:T(4,128)(2,1)} %all-to-all-done.6), kind=kOutput, calls=%fused_computation.5 | convolution fusion | flops 405798912 | bytes 7929856 | tf_op jit(solution)/shard_map/dot_general | solution.py:140
  282.9 0.8 reshape.142
  284.3 67.2 %all-to-all-done.7 = bf16[256,8,768]{2,1,0:T(8,128)(2,1)S(1)} async-done(((bf16[256,8,768]{2,1,0:T(8,128)(2,1)}), bf16[256,8,768]{2,1,0:T(8,128)(2,1)S(1)}, u32[]{:S(2)}, u32[]{:S(2)}) %all-to-all-start.7) | async-done | bytes 3145760 | tf_op jit(solution)/shard_map/all_to_all | solution.py:146
  352.4 2.3 slice_reduce_fusion
  355.5 44.9 %all_to_all.64 = bf16[32,32,768]{2,1,0:T(8,128)(2,1)S(1)} all-to-all(bf16[32,32,768]{2,1,0:T(8,128)(2,1)S(1)} %broadcast_in_dim.19), channel_id=1, replica_groups=mesh['row'=8,'col'=32] {'col'}, dimensions={0} | all-to-all | bytes 3145728 | tf_op jit(solution)/shard_map/all_to_all | solution.py:35
  400.5 1.4 convolution_convert_fusion.1
  401.9 24.4 %all_to_all.65 = bf16[8,128,768]{2,1,0:T(8,128)(2,1)S(1)} all-to-all(bf16[8,128,768]{2,1,0:T(8,128)(2,1)S(1)} %bitcast.89), channel_id=1, replica_groups=mesh['row'=8,'col'=32] {'row'}, dimensions={0} | all-to-all | bytes 3145728 | tf_op jit(solution)/shard_map/all_to_all | solution.py:42
  427.0 24.2 %all_to_all.66 = bf16[8,128,768]{2,1,0:T(8,128)(2,1)S(1)} all-to-all(bf16[8,128,768]{2,1,0:T(8,128)(2,1)S(1)} %broadcast_in_dim.20), channel_id=1, replica_groups=mesh['row'=8,'col'=32] {'row'}, dimensions={0} | all-to-all | bytes 3145728 | tf_op jit(solution)/shard_map/all_to_all | solution.py:35
  451.1 2.6 convolution_convert_fusion
  453.7 5.1 %all-to-all-start.11 = ((bf16[32,32,768]{2,1,0:T(8,128)(2,1)}), bf16[32,32,768]{2,1,0:T(8,128)(2,1)}, u32[]{:S(2)}, u32[]{:S(2)}) async-start(bf16[32,32,768]{2,1,0:T(8,128)(2,1)} %bitcast.26), calls=%async_computation.11 | async-start | bytes 3145728 | tf_op jit(solution)/shard_map/all_to_all | solution.py:42
  459.5 4.0 convolution_convert_fusion.4
  463.5 2.5 convolution_convert_fusion.5
  466.0 2.1 convert_element_type.172
  468.1 1.9 convert_element_type.169
  470.0 27.9 %all-to-all-done.11 = bf16[32,32,768]{2,1,0:T(8,128)(2,1)} async-done(((bf16[32,32,768]{2,1,0:T(8,128)(2,1)}), bf16[32,32,768]{2,1,0:T(8,128)(2,1)}, u32[]{:S(2)}, u32[]{:S(2)}) %all-to-all-start.11) | async-done | bytes 1572896 | tf_op jit(solution)/shard_map/all_to_all | solution.py:42
  497.9 1.6 convert_reduce_fusion
  (75 shorter events, 9.7 us)
Async XLA Ops:
  7.2 244.3 %copy-start = (bf16[6144,256]{1,0:T(8,128)(2,1)S(1)}, bf16[6144,256]{1,0:T(8,128)(2,1)}, u32[]{:S(2)}) copy-start(bf16[6144,256]{1,0:T(8,128)(2,1)} %param.11) | copy-start | bytes 9437188
  8.8 9.8 %all-to-all-start = ((bf16[8,4,768]{2,1,0:T(4,128)(2,1)}), bf16[8,4,768]{2,1,0:T(4,128)(2,1)S(1)}, u32[]{:S(2)}, u32[]{:S(2)}) async-start(bf16[8,4,768]{2,1,0:T(4,128)(2,1)} %reshape_transpose_reshape_broadcast_in_dim.6), calls=%async_computation | async-start | bytes 98304 | tf_op jit(solution)/shard_map/all_to_all | solution.py:63
  20.3 51.3 %copy-start.20 = (bf16[768,768]{1,0:T(8,128)(2,1)S(1)}, bf16[768,768]{1,0:T(8,128)(2,1)}, u32[]{:S(2)}) copy-start(bf16[768,768]{1,0:T(8,128)(2,1)} %param.9) | copy-start | bytes 3538948
  71.6 1.4 copy-start.4
  98.6 25.9 %all-to-all-start.3 = ((bf16[8,128,768]{2,1,0:T(8,128)(2,1)}), bf16[8,128,768]{2,1,0:T(8,128)(2,1)}, u32[]{:S(2)}, u32[]{:S(2)}) async-start(bf16[8,128,768]{2,1,0:T(8,128)(2,1)} %broadcast_in_dim.15), calls=%async_computation.3 | async-start | bytes 3145728 | tf_op jit(solution)/shard_map/all_to_all | solution.py:35
  102.9 88.4 %all-gather.4.cloned.1.call-start = ((), (), s32[]{:S(2)}) async-start(), calls=%async_computation.16 | async-start | bytes 3244032 | tf_op jit(solution)/shard_map/all_gather | solution.py:102
  204.9 46.5 %all-to-all-start.6 = ((bf16[32,4,6144]{2,1,0:T(4,128)(2,1)}), bf16[32,4,6144]{2,1,0:T(4,128)(2,1)}, u32[]{:S(2)}, u32[]{:S(2)}) async-start(bf16[32,4,6144]{2,1,0:T(4,128)(2,1)} %broadcast_in_dim.18), calls=%async_computation.6 | async-start | bytes 3145728 | tf_op jit(solution)/shard_map/all_to_all | solution.py:120
  212.3 253.7 %reduce-scatter.5.cloned.1.call-start = ((), (), s32[]{:S(2)}) async-start(), calls=%async_computation.15 | async-start | bytes 7077888 | tf_op jit(solution)/shard_map/reduce_scatter | solution.py:171
  214.1 3.7 copy-start.16
  251.4 4.1 copy-start.2
  254.9 0.6 copy-start.13
  260.6 4.6 copy-start.3
  264.6 0.6 copy-start.15
  269.1 82.3 %all-to-all-start.7 = ((bf16[256,8,768]{2,1,0:T(8,128)(2,1)}), bf16[256,8,768]{2,1,0:T(8,128)(2,1)S(1)}, u32[]{:S(2)}, u32[]{:S(2)}) async-start(bf16[256,8,768]{2,1,0:T(8,128)(2,1)} %bitcast.20), calls=%async_computation.7 | async-start | bytes 6291456 | tf_op jit(solution)/shard_map/all_to_all | solution.py:146
  276.1 192.0 %reduce-scatter.3.cloned.1.call-start = ((), (), s32[]{:S(2)}) async-start(), calls=%async_computation.14 | async-start | bytes 7077888 | tf_op jit(solution)/shard_map/reduce_scatter | solution.py:168
  281.6 0.7 copy-start.18
  281.6 0.7 copy-start.17
  351.5 0.9 copy-start.8
  352.4 2.3 copy-start.14
  354.7 0.6 copy-start.9
  355.5 45.0 %copy-start.19 = (bf16[768,768]{1,0:T(8,128)(2,1)S(1)}, bf16[768,768]{1,0:T(8,128)(2,1)}, u32[]{:S(2)}) copy-start(bf16[768,768]{1,0:T(8,128)(2,1)} %param.10) | copy-start | bytes 3538948
  426.9 24.2 %copy-start.21 = (bf16[768,768]{1,0:T(8,128)(2,1)S(1)}, bf16[768,768]{1,0:T(8,128)(2,1)}, u32[]{:S(2)}) copy-start(bf16[768,768]{1,0:T(8,128)(2,1)} %param.9) | copy-start | bytes 3538948
  451.1 2.6 copy-start.6
  453.7 5.1 %copy-start.12 = (f32[8,4,768]{2,1,0:T(4,128)S(1)}, f32[8,4,768]{2,1,0:T(4,128)}, u32[]{:S(2)}) copy-start(f32[8,4,768]{2,1,0:T(4,128)} %get-tuple-element.13) | copy-start | bytes 294916
  453.7 5.2 %copy-start.11 = (bf16[32,768]{1,0:T(8,128)(2,1)S(1)}, bf16[32,768]{1,0:T(8,128)(2,1)}, u32[]{:S(2)}) copy-start(bf16[32,768]{1,0:T(8,128)(2,1)} %add_convert_fusion.3) | copy-start | bytes 147460
  453.7 44.2 %all-to-all-start.11 = ((bf16[32,32,768]{2,1,0:T(8,128)(2,1)}), bf16[32,32,768]{2,1,0:T(8,128)(2,1)}, u32[]{:S(2)}, u32[]{:S(2)}) async-start(bf16[32,32,768]{2,1,0:T(8,128)(2,1)} %bitcast.26), calls=%async_computation.11 | async-start | bytes 3145728 | tf_op jit(solution)/shard_map/all_to_all | solution.py:42
  459.5 4.0 copy-start.5
  459.5 4.0 copy-start.7
  466.0 34.2 %copy-start.1 = (bf16[6144,256]{1,0:T(8,128)(2,1)S(1)}, bf16[6144,256]{1,0:T(8,128)(2,1)}, u32[]{:S(2)}) copy-start(bf16[6144,256]{1,0:T(8,128)(2,1)} %param.11) | copy-start | bytes 9437188
  468.1 31.5 %copy-start.10 = (bf16[32,768]{1,0:T(8,128)(2,1)S(1)}, bf16[32,768]{1,0:T(8,128)(2,1)}, u32[]{:S(2)}) copy-start(bf16[32,768]{1,0:T(8,128)(2,1)} %copy-done.9) | copy-start | bytes 147460
Sparse Core Ops, SparseCore 0:
  106.9 84.3 all-gather.3
  259.8 62.4 reduce-scatter.4
  324.8 50.1 reduce-scatter.2

commit v12 on v5

--- a/solution.py
+++ b/solution.py
@@ -83,7 +83,6 @@
     slot_cap = max(2, 3 * block_len // 4)
     model_width = expert_out.shape[1]
     my_row = lax.axis_index("row")
-    tok_panel = gather_rows(tokens, "col")
     own_grad = swap_blocks(out_grad[None], row_count)[0]
     ids_own = lax.dynamic_slice_in_dim(expert_ids, my_row * block_len, block_len, 0)
     weights_own = lax.dynamic_slice_in_dim(route_weights, my_row * block_len, block_len, 0)
@@ -98,7 +97,8 @@
         ((0, 0), (0, model_width - EXPERTS * block_len)),
     )
     grad_pack = jnp.concatenate([own_grad, table_row], axis=0)
-    tok_panel, grad_pack = lax.optimization_barrier((tok_panel, grad_pack))
+    tokens_ready, grad_pack = lax.optimization_barrier((tokens, grad_pack))
+    tok_panel = gather_rows(tokens_ready, "col")
     pack_all = lax.all_gather(grad_pack, "col", axis=0, tiled=False)
     my_expert = lax.axis_index("col") // group_len
     weights_recv = lax.dynamic_slice_in_dim(
@@ -111,7 +111,10 @@
     preact = scatter_sum(up_terms, "row")
     hidden_full = gather_rows(gelu_tanh(preact).astype(jnp.bfloat16), "row")
     rows_in = hidden_full
-    dense_term = scatter_sum(jnp.dot(rows_in, w_down, preferred_element_type=jnp.float32), "col")
+    down_terms, pack_all = lax.optimization_barrier(
+        (jnp.dot(rows_in, w_down, preferred_element_type=jnp.float32), pack_all)
+    )
+    dense_term = scatter_sum(down_terms, "col")
     mixed_act = (tokens.astype(jnp.float32) + dense_term).astype(jnp.bfloat16)
     own_rows = swap_blocks(mixed_act[None], row_count)[0]
     scaled_flat = grad_rows_in.reshape(col_count * block_len, model_width)

time: 505 us -> 497 us (0.984)
  waiting for transfers between devices: 216 us -> 171 us
  blocking collectives: 172 us -> 208 us
    all_to_all x2 -> x3, blocking collectives: 48 us -> 93.5 us  [scatter_sum(): got = lax.all_to_all(blocks, axis_name, 0, 0, tiled=True)]
    all_to_all x2 -> x1, waiting for transfers between devices: 69.5 us -> 28.1 us  [scatter_sum(): got = lax.all_to_all(blocks, axis_name, 0, 0, tiled=True)]
    all_gather x1, waiting for transfers between devices: 40.8 us -> 0.01 us  [on_device(): pack_all = lax.all_gather(grad_pack, 'col', axis=0, tiled=False)]
    all_to_all x1, waiting for transfers between devices: 2.26 us -> 33.5 us  [on_device(): got = lax.all_to_all(payload, 'col', 0, 0, tiled=True)]
    all_to_all x2 -> x1, blocking collectives: 18.4 us -> 8.78 us  [swap_blocks(): lax.all_to_all(parts.reshape(count, arrays * block, width), 'row', 0, 0,...]
    all_to_all x2 -> x1, starting transfers between devices: 10.8 us -> 5.02 us  [scatter_sum(): got = lax.all_to_all(blocks, axis_name, 0, 0, tiled=True)]
  transfers between devices with their start and end apart: 8 -> 8, of which waited for: 6 -> 5; matrix products, arithmetic and copies ran while one was open for 9% -> 9% of each run, Pallas kernels for 0% -> 0%
where the time goes in v12:
time: 497 us; the launch traced here: 495 us
  blocking collectives  208 us (42%)
  waiting for transfers between devices  171 us (34%)
  matrix products  36.7 us (7%)
  starting transfers between devices  31.8 us (6%)
  local copies, waits for them, and re-layouts  21.5 us (4%)
  between operations  14.1 us (3%)
  other arithmetic  11.7 us (2%)
    all_to_all x3, blocking collectives, gather_rows(): got = lax.all_to_all(spread, axis_name, 0, 0, tiled=True)  98 us
    all_to_all x3, blocking collectives, scatter_sum(): got = lax.all_to_all(blocks, axis_name, 0, 0, tiled=True)  93.5 us
    all_to_all x1, waiting for transfers between devices, on_device(): lax.all_to_all(back_flat.astype(jnp.bfloat16).reshape(col_count, 2 * bloc...  63.5 us
    all_to_all x1, waiting for transfers between devices, gather_rows(): got = lax.all_to_all(spread, axis_name, 0, 0, tiled=True)  41.8 us
    all_to_all x1, waiting for transfers between devices, on_device(): got = lax.all_to_all(payload, 'col', 0, 0, tiled=True)  33.5 us
    all_to_all x1, waiting for transfers between devices, scatter_sum(): got = lax.all_to_all(blocks, axis_name, 0, 0, tiled=True)  28.1 us
    all_to_all x1, starting transfers between devices, gather_rows(): got = lax.all_to_all(spread, axis_name, 0, 0, tiled=True)  11.4 us
  transfers between devices with their start and end apart: 8, of which 5 were waited for; matrix products, arithmetic and copies ran while one was open for 9% of the time, Pallas kernels for 0%

profile of v12, /device:TPU:32, one launch (start us, length us, event | category | flops | bytes accessed | tf_op | source)
XLA Modules:
  0.0 495.2 jit_solution(3218137721329204802)
XLA Ops:
  7.2 1.6 reshape_transpose_reshape_broadcast_in_dim.6
  8.8 4.3 all-to-all-start
  13.1 0.7 constant_dynamic-slice_fusion.2
  13.8 0.7 fusion.34
  15.2 3.4 all-to-all-done
  18.6 0.7 fusion.33
  19.3 2.1 broadcast_in_dim.14
  21.4 11.4 %all-to-all-start.1 = ((bf16[32,32,768]{2,1,0:T(8,128)(2,1)}), bf16[32,32,768]{2,1,0:T(8,128)(2,1)}, u32[]{:S(2)}, u32[]{:S(2)}) async-start(bf16[32,32,768]{2,1,0:T(8,128)(2,1)} %broadcast_in_dim.14), calls=%async_computation.1 | async-start | bytes 3145728 | tf_op jit(solution)/shard_map/all_to_all | solution.py:35
  32.9 0.7 all-gather.4.cloned.1.call-update
  33.6 41.8 %all-to-all-done.1 = bf16[32,32,768]{2,1,0:T(8,128)(2,1)} async-done(((bf16[32,32,768]{2,1,0:T(8,128)(2,1)}), bf16[32,32,768]{2,1,0:T(8,128)(2,1)}, u32[]{:S(2)}, u32[]{:S(2)}) %all-to-all-start.1) | async-done | bytes 1572896 | tf_op jit(solution)/shard_map/all_to_all | solution.py:35
  75.4 3.1 convolution_convert_fusion.2
  78.5 24.0 %all_to_all.65 = bf16[8,128,768]{2,1,0:T(8,128)(2,1)S(1)} all-to-all(bf16[8,128,768]{2,1,0:T(8,128)(2,1)S(1)} %bitcast.89), channel_id=1, replica_groups=mesh['row'=8,'col'=32] {'row'}, dimensions={0} | all-to-all | bytes 3145728 | tf_op jit(solution)/shard_map/all_to_all | solution.py:42
  103.0 24.2 %all_to_all.66 = bf16[8,128,768]{2,1,0:T(8,128)(2,1)S(1)} all-to-all(bf16[8,128,768]{2,1,0:T(8,128)(2,1)S(1)} %broadcast_in_dim.15), channel_id=1, replica_groups=mesh['row'=8,'col'=32] {'row'}, dimensions={0} | all-to-all | bytes 3145728 | tf_op jit(solution)/shard_map/all_to_all | solution.py:35
  127.2 1.2 copy-done.4
  128.4 2.6 fusion.38
  130.9 45.4 %all_to_all.67 = bf16[32,32,768]{2,1,0:T(8,128)(2,1)S(1)} all-to-all(bf16[32,32,768]{2,1,0:T(8,128)(2,1)} %bitcast.88), channel_id=1, replica_groups=mesh['row'=8,'col'=32] {'col'}, dimensions={0} | all-to-all | bytes 3145728 | tf_op jit(solution)/shard_map/all_to_all | solution.py:42
  177.8 1.4 reshape_transpose_reshape_broadcast_in_dim.7
  179.2 8.8 %all_to_all.68 = bf16[8,4,768]{2,1,0:T(4,128)(2,1)S(1)} all-to-all(bf16[8,4,768]{2,1,0:T(4,128)(2,1)} %reshape_transpose_reshape_broadcast_in_dim.7), channel_id=1, replica_groups=mesh['row'=8,'col'=32] {'row'}, dimensions={0} | all-to-all | bytes 98304 | tf_op jit(solution)/shard_map/all_to_all | solution.py:63
  188.6 1.9 broadcast_in_dim.18
  190.5 4.9 all-to-all-start.6
  195.6 0.9 slice.26
  197.2 3.7 slice.27
  201.0 33.5 %all-to-all-done.6 = bf16[32,4,6144]{2,1,0:T(4,128)(2,1)} async-done(((bf16[32,4,6144]{2,1,0:T(4,128)(2,1)}), bf16[32,4,6144]{2,1,0:T(4,128)(2,1)}, u32[]{:S(2)}, u32[]{:S(2)}) %all-to-all-start.6) | async-done | bytes 1572896 | tf_op jit(solution)/shard_map/all_to_all | solution.py:122
  234.5 3.4 multiply_convert_fusion.8
  238.6 4.2 fusion.4
  242.8 0.9 copy.93
  243.7 4.0 fusion.16
  248.4 1.0 fusion.32
  249.4 2.7 fusion.5
  252.1 5.8 %all-to-all-start.7 = ((bf16[32,8,6144]{2,1,0:T(8,128)(2,1)}), bf16[32,8,6144]{2,1,0:T(8,128)(2,1)S(1)}, u32[]{:S(2)}, u32[]{:S(2)}) async-start(bf16[32,8,6144]{2,1,0:T(8,128)(2,1)} %fusion.5), calls=%async_computation.7 | async-start | bytes 6291456 | tf_op jit(solution)/shard_map/all_to_all | solution.py:148
  258.0 5.4 %fusion.2 = f32[6144,256]{1,0:T(8,128)} fusion(bf16[32,4,256]{2,0,1:T(8,128)(2,1)} %copy-done.17, bf16[32,4,6144]{2,1,0:T(4,128)(2,1)} %all-to-all-done.6), kind=kOutput, calls=%fused_computation.5 | convolution fusion | flops 405798912 | bytes 7929856 | tf_op jit(solution)/shard_map/dot_general | solution.py:142
  263.4 0.7 broadcast_bitcast_fusion
  264.1 63.5 %all-to-all-done.7 = bf16[32,8,6144]{2,1,0:T(8,128)(2,1)S(1)} async-done(((bf16[32,8,6144]{2,1,0:T(8,128)(2,1)}), bf16[32,8,6144]{2,1,0:T(8,128)(2,1)S(1)}, u32[]{:S(2)}, u32[]{:S(2)}) %all-to-all-start.7) | async-done | bytes 3145760 | tf_op jit(solution)/shard_map/all_to_all | solution.py:148
  327.6 0.7 convert_element_type.160
  328.4 1.5 fusion.6
  330.0 8.2 %all_to_all.69 = bf16[8,8,768]{2,1,0:T(8,128)(2,1)S(1)} all-to-all(bf16[8,8,768]{2,1,0:T(8,128)(2,1)S(1)} %copy.83), channel_id=1, replica_groups=mesh['row'=8,'col'=32] {'row'}, dimensions={0} | all-to-all | bytes 196608 | tf_op jit(solution)/shard_map/all_to_all | solution.py:72
  339.7 49.6 %all_to_all.70 = bf16[32,32,768]{2,1,0:T(8,128)(2,1)S(1)} all-to-all(bf16[32,32,768]{2,1,0:T(8,128)(2,1)S(1)} %broadcast_in_dim.19), channel_id=1, replica_groups=mesh['row'=8,'col'=32] {'col'}, dimensions={0} | all-to-all | bytes 3145728 | tf_op jit(solution)/shard_map/all_to_all | solution.py:35
  389.4 1.4 convolution_convert_fusion.1
  390.8 24.0 %all_to_all.71 = bf16[8,128,768]{2,1,0:T(8,128)(2,1)S(1)} all-to-all(bf16[8,128,768]{2,1,0:T(8,128)(2,1)S(1)} %bitcast.90), channel_id=1, replica_groups=mesh['row'=8,'col'=32] {'row'}, dimensions={0} | all-to-all | bytes 3145728 | tf_op jit(solution)/shard_map/all_to_all | solution.py:42
  415.4 24.2 %all_to_all.72 = bf16[8,128,768]{2,1,0:T(8,128)(2,1)S(1)} all-to-all(bf16[8,128,768]{2,1,0:T(8,128)(2,1)S(1)} %broadcast_in_dim.20), channel_id=1, replica_groups=mesh['row'=8,'col'=32] {'row'}, dimensions={0} | all-to-all | bytes 3145728 | tf_op jit(solution)/shard_map/all_to_all | solution.py:35
  439.6 2.6 convolution_convert_fusion
  442.2 5.0 %all-to-all-start.12 = ((bf16[32,32,768]{2,1,0:T(8,128)(2,1)}), bf16[32,32,768]{2,1,0:T(8,128)(2,1)}, u32[]{:S(2)}, u32[]{:S(2)}) async-start(bf16[32,32,768]{2,1,0:T(8,128)(2,1)} %bitcast.30), calls=%async_computation.12 | async-start | bytes 3145728 | tf_op jit(solution)/shard_map/all_to_all | solution.py:42
  447.9 2.5 convolution_convert_fusion.3
  450.4 3.9 convolution_convert_fusion.4
  454.2 2.1 convert_element_type.178
  456.3 1.9 convert_element_type.175
  458.2 28.1 %all-to-all-done.12 = bf16[32,32,768]{2,1,0:T(8,128)(2,1)} async-done(((bf16[32,32,768]{2,1,0:T(8,128)(2,1)}), bf16[32,32,768]{2,1,0:T(8,128)(2,1)}, u32[]{:S(2)}, u32[]{:S(2)}) %all-to-all-start.12) | async-done | bytes 1572896 | tf_op jit(solution)/shard_map/all_to_all | solution.py:42
  486.3 1.6 convert_reduce_fusion
  (80 shorter events, 9.1 us)
Async XLA Ops:
  7.2 227.3 %copy-start = (bf16[6144,256]{1,0:T(8,128)(2,1)S(1)}, bf16[6144,256]{1,0:T(8,128)(2,1)}, u32[]{:S(2)}) copy-start(bf16[6144,256]{1,0:T(8,128)(2,1)} %param.11) | copy-start | bytes 9437188
  8.8 9.8 %all-to-all-start = ((bf16[8,4,768]{2,1,0:T(4,128)(2,1)}), bf16[8,4,768]{2,1,0:T(4,128)(2,1)S(1)}, u32[]{:S(2)}, u32[]{:S(2)}) async-start(bf16[8,4,768]{2,1,0:T(4,128)(2,1)} %reshape_transpose_reshape_broadcast_in_dim.6), calls=%async_computation | async-start | bytes 98304 | tf_op jit(solution)/shard_map/all_to_all | solution.py:63
  14.6 0.6 copy-start.18
  18.6 2.8 copy-start.12
  21.4 54.0 %all-to-all-start.1 = ((bf16[32,32,768]{2,1,0:T(8,128)(2,1)}), bf16[32,32,768]{2,1,0:T(8,128)(2,1)}, u32[]{:S(2)}, u32[]{:S(2)}) async-start(bf16[32,32,768]{2,1,0:T(8,128)(2,1)} %broadcast_in_dim.14), calls=%async_computation.1 | async-start | bytes 3145728 | tf_op jit(solution)/shard_map/all_to_all | solution.py:35
  32.8 98.1 %all-gather.4.cloned.1.call-start = ((), (), s32[]{:S(2)}) async-start(), calls=%async_computation.17 | async-start | bytes 3244032 | tf_op jit(solution)/shard_map/all_gather | solution.py:102
  103.0 25.3 %copy-start.20 = (bf16[768,768]{1,0:T(8,128)(2,1)S(1)}, bf16[768,768]{1,0:T(8,128)(2,1)}, u32[]{:S(2)}) copy-start(bf16[768,768]{1,0:T(8,128)(2,1)} %param.10) | copy-start | bytes 3538948
  127.2 1.2 copy-start.4
  176.3 0.8 copy-start.15
  188.0 0.6 copy-start.8
  190.5 44.0 %all-to-all-start.6 = ((bf16[32,4,6144]{2,1,0:T(4,128)(2,1)}), bf16[32,4,6144]{2,1,0:T(4,128)(2,1)}, u32[]{:S(2)}, u32[]{:S(2)}) async-start(bf16[32,4,6144]{2,1,0:T(4,128)(2,1)} %broadcast_in_dim.18), calls=%async_computation.6 | async-start | bytes 3145728 | tf_op jit(solution)/shard_map/all_to_all | solution.py:122
  195.4 258.8 %reduce-scatter.5.cloned.1.call-start = ((), (), s32[]{:S(2)}) async-start(), calls=%async_computation.16 | async-start | bytes 7077888 | tf_op jit(solution)/shard_map/reduce_scatter | solution.py:165
  197.2 3.7 copy-start.19
  234.5 4.1 copy-start.2
  238.0 0.6 copy-start.14
  243.7 4.7 copy-start.3
  247.7 0.6 copy-start.17
  252.1 75.5 %all-to-all-start.7 = ((bf16[32,8,6144]{2,1,0:T(8,128)(2,1)}), bf16[32,8,6144]{2,1,0:T(8,128)(2,1)S(1)}, u32[]{:S(2)}, u32[]{:S(2)}) async-start(bf16[32,8,6144]{2,1,0:T(8,128)(2,1)} %fusion.5), calls=%async_computation.7 | async-start | bytes 6291456 | tf_op jit(solution)/shard_map/all_to_all | solution.py:148
  257.9 198.4 %reduce-scatter.3.cloned.1.call-start = ((), (), s32[]{:S(2)}) async-start(), calls=%async_computation.15 | async-start | bytes 7077888 | tf_op jit(solution)/shard_map/reduce_scatter | solution.py:162
  328.3 1.5 copy-start.9
  328.3 1.5 copy-start.13
  338.9 0.6 copy-start.10
  339.7 49.7 %copy-start.21 = (bf16[768,768]{1,0:T(8,128)(2,1)S(1)}, bf16[768,768]{1,0:T(8,128)(2,1)}, u32[]{:S(2)}) copy-start(bf16[768,768]{1,0:T(8,128)(2,1)} %param.10) | copy-start | bytes 3538948
  415.4 24.2 %copy-start.22 = (bf16[768,768]{1,0:T(8,128)(2,1)S(1)}, bf16[768,768]{1,0:T(8,128)(2,1)}, u32[]{:S(2)}) copy-start(bf16[768,768]{1,0:T(8,128)(2,1)} %param.9) | copy-start | bytes 3538948
  439.6 2.6 copy-start.6
  442.2 5.0 %copy-start.16 = (bf16[1,8,4,768]{3,1,2,0:T(8,128)(2,1)S(1)}, bf16[1,8,4,768]{3,1,2,0:T(8,128)(2,1)}, u32[]{:S(2)}) copy-start(bf16[1,8,4,768]{3,1,2,0:T(8,128)(2,1)} %get-tuple-element.15) | copy-start | bytes 147460
  442.2 5.7 %copy-start.5 = (bf16[8,128,768]{2,1,0:T(8,128)(2,1)S(1)}, bf16[8,128,768]{2,1,0:T(8,128)(2,1)}, u32[]{:S(2)}) copy-start(bf16[8,128,768]{2,1,0:T(8,128)(2,1)} %copy-done.4) | copy-start | bytes 4718596
  442.2 44.2 %all-to-all-start.12 = ((bf16[32,32,768]{2,1,0:T(8,128)(2,1)}), bf16[32,32,768]{2,1,0:T(8,128)(2,1)}, u32[]{:S(2)}, u32[]{:S(2)}) async-start(bf16[32,32,768]{2,1,0:T(8,128)(2,1)} %bitcast.30), calls=%async_computation.12 | async-start | bytes 3145728 | tf_op jit(solution)/shard_map/all_to_all | solution.py:42
  447.9 2.5 copy-start.7
  454.2 34.4 %copy-start.1 = (bf16[6144,256]{1,0:T(8,128)(2,1)S(1)}, bf16[6144,256]{1,0:T(8,128)(2,1)}, u32[]{:S(2)}) copy-start(bf16[6144,256]{1,0:T(8,128)(2,1)} %param.11) | copy-start | bytes 9437188
  456.3 31.7 %copy-start.11 = (bf16[32,768]{1,0:T(8,128)(2,1)S(1)}, bf16[32,768]{1,0:T(8,128)(2,1)}, u32[]{:S(2)}) copy-start(bf16[32,768]{1,0:T(8,128)(2,1)} %copy-done.10) | copy-start | bytes 147460
Sparse Core Ops, SparseCore 0:
  36.8 79.9 all-gather.3
  242.9 40.5 reduce-scatter.4
  286.1 45.7 reduce-scatter.2

commit v13 on v10

--- a/solution.py
+++ b/solution.py
@@ -168,10 +168,10 @@
     layer_out = (mixed_act.astype(jnp.float32) + moe_sum.reshape(tok_col, -1)).astype(jnp.bfloat16)
     mixed_grad = (out_grad.astype(jnp.float32) + grad_sum.reshape(tok_col, -1)).astype(jnp.bfloat16)
     expert_in_grad = lax.psum_scatter(
-        grad_in.astype(jnp.bfloat16).astype(jnp.float32), "row", scatter_dimension=0, tiled=True
+        grad_in.astype(jnp.bfloat16), "row", scatter_dimension=0, tiled=True
     ).astype(jnp.bfloat16)
     expert_out_grad = lax.psum_scatter(
-        grad_out.astype(jnp.bfloat16).astype(jnp.float32), "row", scatter_dimension=1, tiled=True
+        grad_out.astype(jnp.bfloat16), "row", scatter_dimension=1, tiled=True
     ).astype(jnp.bfloat16)
     cot_panel = gather_rows(mixed_grad, "col")
     hgrad_terms = jnp.dot(cot_panel, w_down.T, preferred_element_type=jnp.float32)

time: 491 us -> 493 us (level)
  waiting for transfers between devices: 175 us -> 200 us
  blocking collectives: 196 us -> 178 us
    all_to_all x3 -> x2, blocking collectives: 93.9 us -> 69.4 us  [scatter_sum(): got = lax.all_to_all(blocks, axis_name, 0, 0, tiled=True)]
    all_to_all x1 -> x2, waiting for transfers between devices: 28.1 us -> 52 us  [scatter_sum(): got = lax.all_to_all(blocks, axis_name, 0, 0, tiled=True)]
    all_to_all x3, blocking collectives: 93.3 us -> 99.4 us  [gather_rows(): got = lax.all_to_all(spread, axis_name, 0, 0, tiled=True)]
  transfers between devices with their start and end apart: 8 -> 9, of which waited for: 5 -> 6; matrix products, arithmetic and copies ran while one was open for 10% -> 9% of each run, Pallas kernels for 0% -> 0%
where the time goes in v13:
time: 493 us; the launch traced here: 492 us
  waiting for transfers between devices  200 us (41%)
  blocking collectives  178 us (36%)
  starting transfers between devices  36.3 us (7%)
  matrix products  32.8 us (7%)
  local copies, waits for them, and re-layouts  21.1 us (4%)
  between operations  14.1 us (3%)
  other arithmetic  9.4 us (2%)
    all_to_all x3, blocking collectives, gather_rows(): got = lax.all_to_all(spread, axis_name, 0, 0, tiled=True)  99.4 us
    all_to_all x2, blocking collectives, scatter_sum(): got = lax.all_to_all(blocks, axis_name, 0, 0, tiled=True)  69.4 us
    all_to_all x1, waiting for transfers between devices, on_device(): lax.all_to_all(back_flat.astype(jnp.bfloat16).reshape(col_count, 2 * bloc...  68 us
    all_to_all x2, waiting for transfers between devices, scatter_sum(): got = lax.all_to_all(blocks, axis_name, 0, 0, tiled=True)  52 us
    all_to_all x1, waiting for transfers between devices, gather_rows(): got = lax.all_to_all(spread, axis_name, 0, 0, tiled=True)  41.8 us
    all_to_all x1, waiting for transfers between devices, on_device(): got = lax.all_to_all(payload, 'col', 0, 0, tiled=True)  33.7 us
    all_to_all x1, starting transfers between devices, gather_rows(): got = lax.all_to_all(spread, axis_name, 0, 0, tiled=True)  11.4 us
  transfers between devices with their start and end apart: 9, of which 6 were waited for; matrix products, arithmetic and copies ran while one was open for 9% of the time, Pallas kernels for 0%

profile of v13, /device:TPU:32, one launch (start us, length us, event | category | flops | bytes accessed | tf_op | source)
XLA Modules:
  0.0 491.6 jit_solution(7662647761833861725)
XLA Ops:
  7.2 1.6 reshape_transpose_reshape_broadcast_in_dim.6
  8.8 4.3 all-to-all-start
  13.1 0.7 constant_dynamic-slice_fusion.2
  13.8 0.7 fusion.31
  14.7 4.0 all-to-all-done
  18.6 0.7 fusion.30
  19.3 2.1 broadcast_in_dim.14
  21.4 11.4 %all-to-all-start.1 = ((bf16[32,32,768]{2,1,0:T(8,128)(2,1)}), bf16[32,32,768]{2,1,0:T(8,128)(2,1)}, u32[]{:S(2)}, u32[]{:S(2)}) async-start(bf16[32,32,768]{2,1,0:T(8,128)(2,1)} %broadcast_in_dim.14), calls=%async_computation.1 | async-start | bytes 3145728 | tf_op jit(solution)/shard_map/all_to_all | solution.py:35
  32.9 0.7 all-gather.4.cloned.1.call-update
  33.6 41.8 %all-to-all-done.1 = bf16[32,32,768]{2,1,0:T(8,128)(2,1)} async-done(((bf16[32,32,768]{2,1,0:T(8,128)(2,1)}), bf16[32,32,768]{2,1,0:T(8,128)(2,1)}, u32[]{:S(2)}, u32[]{:S(2)}) %all-to-all-start.1) | async-done | bytes 1572896 | tf_op jit(solution)/shard_map/all_to_all | solution.py:35
  75.4 3.1 convolution_convert_fusion.2
  78.5 24.0 %all_to_all.60 = bf16[8,128,768]{2,1,0:T(8,128)(2,1)S(1)} all-to-all(bf16[8,128,768]{2,1,0:T(8,128)(2,1)S(1)} %bitcast.86), channel_id=1, replica_groups=mesh['row'=8,'col'=32] {'row'}, dimensions={0} | all-to-all | bytes 3145728 | tf_op jit(solution)/shard_map/all_to_all | solution.py:42
  103.0 24.2 %all_to_all.61 = bf16[8,128,768]{2,1,0:T(8,128)(2,1)S(1)} all-to-all(bf16[8,128,768]{2,1,0:T(8,128)(2,1)S(1)} %broadcast_in_dim.15), channel_id=1, replica_groups=mesh['row'=8,'col'=32] {'row'}, dimensions={0} | all-to-all | bytes 3145728 | tf_op jit(solution)/shard_map/all_to_all | solution.py:35
  127.2 1.2 copy-done.3
  128.4 2.6 fusion.34
  131.0 45.4 %all_to_all.62 = bf16[32,32,768]{2,1,0:T(8,128)(2,1)S(1)} all-to-all(bf16[32,32,768]{2,1,0:T(8,128)(2,1)} %bitcast.85), channel_id=1, replica_groups=mesh['row'=8,'col'=32] {'col'}, dimensions={0} | all-to-all | bytes 3145728 | tf_op jit(solution)/shard_map/all_to_all | solution.py:42
  177.8 1.4 reshape_transpose_reshape_broadcast_in_dim.7
  179.3 8.8 %all_to_all.63 = bf16[8,4,768]{2,1,0:T(4,128)(2,1)S(1)} all-to-all(bf16[8,4,768]{2,1,0:T(4,128)(2,1)} %reshape_transpose_reshape_broadcast_in_dim.7), channel_id=1, replica_groups=mesh['row'=8,'col'=32] {'row'}, dimensions={0} | all-to-all | bytes 98304 | tf_op jit(solution)/shard_map/all_to_all | solution.py:63
  188.1 1.9 broadcast_in_dim.18
  189.9 4.9 all-to-all-start.6
  194.8 0.9 slice.16
  195.8 0.7 copy.67
  196.5 3.8 slice.17
  200.2 33.7 %all-to-all-done.6 = bf16[32,4,6144]{2,1,0:T(4,128)(2,1)} async-done(((bf16[32,4,6144]{2,1,0:T(4,128)(2,1)}), bf16[32,4,6144]{2,1,0:T(4,128)(2,1)}, u32[]{:S(2)}, u32[]{:S(2)}) %all-to-all-start.6) | async-done | bytes 1572896 | tf_op jit(solution)/shard_map/all_to_all | solution.py:122
  234.0 2.8 multiply_convert_fusion.8
  236.8 1.5 fusion.13
  238.9 1.0 fusion.29
  239.9 1.1 fusion
  241.0 1.9 copy.64
  242.9 7.0 %all-to-all-start.7 = ((bf16[256,8,768]{2,1,0:T(8,128)(2,1)}), bf16[256,8,768]{2,1,0:T(8,128)(2,1)S(1)}, u32[]{:S(2)}, u32[]{:S(2)}) async-start(bf16[256,8,768]{2,1,0:T(8,128)(2,1)} %bitcast.20), calls=%async_computation.7 | async-start | bytes 6291456 | tf_op jit(solution)/shard_map/all_to_all | solution.py:148
  250.0 4.6 fusion.2
  255.9 0.8 reshape.142
  256.6 0.7 broadcast_bitcast_fusion
  257.3 68.0 %all-to-all-done.7 = bf16[256,8,768]{2,1,0:T(8,128)(2,1)S(1)} async-done(((bf16[256,8,768]{2,1,0:T(8,128)(2,1)}), bf16[256,8,768]{2,1,0:T(8,128)(2,1)S(1)}, u32[]{:S(2)}, u32[]{:S(2)}) %all-to-all-start.7) | async-done | bytes 3145760 | tf_op jit(solution)/shard_map/all_to_all | solution.py:148
  326.2 2.3 slice_reduce_fusion
  329.4 45.0 %all_to_all.64 = bf16[32,32,768]{2,1,0:T(8,128)(2,1)S(1)} all-to-all(bf16[32,32,768]{2,1,0:T(8,128)(2,1)S(1)} %broadcast_in_dim.19), channel_id=1, replica_groups=mesh['row'=8,'col'=32] {'col'}, dimensions={0} | all-to-all | bytes 3145728 | tf_op jit(solution)/shard_map/all_to_all | solution.py:35
  374.3 2.6 convolution_convert_fusion.1
  376.9 3.6 all-to-all-start.9
  380.6 4.5 fusion.1
  385.1 20.1 %all-to-all-done.9 = bf16[8,128,768]{2,1,0:T(8,128)(2,1)S(1)} async-done(((bf16[8,128,768]{2,1,0:T(8,128)(2,1)}), bf16[8,128,768]{2,1,0:T(8,128)(2,1)S(1)}, u32[]{:S(2)}, u32[]{:S(2)}) %all-to-all-start.9) | async-done | bytes 1572896 | tf_op jit(solution)/shard_map/all_to_all | solution.py:42
  405.8 30.3 %all_to_all.65 = bf16[8,128,768]{2,1,0:T(8,128)(2,1)S(1)} all-to-all(bf16[8,128,768]{2,1,0:T(8,128)(2,1)S(1)} %broadcast_in_dim.20), channel_id=1, replica_groups=mesh['row'=8,'col'=32] {'row'}, dimensions={0} | all-to-all | bytes 3145728 | tf_op jit(solution)/shard_map/all_to_all | solution.py:35
  436.1 2.6 convolution_convert_fusion
  438.8 4.9 %all-to-all-start.11 = ((bf16[32,32,768]{2,1,0:T(8,128)(2,1)}), bf16[32,32,768]{2,1,0:T(8,128)(2,1)}, u32[]{:S(2)}, u32[]{:S(2)}) async-start(bf16[32,32,768]{2,1,0:T(8,128)(2,1)} %bitcast.84), calls=%async_computation.11 | async-start | bytes 3145728 | tf_op jit(solution)/shard_map/all_to_all | solution.py:42
  443.8 0.6 add_convert_fusion.2
  444.4 2.5 convolution_convert_fusion.3
  446.9 4.0 convolution_convert_fusion.4
  450.9 31.9 %all-to-all-done.11 = bf16[32,32,768]{2,1,0:T(8,128)(2,1)} async-done(((bf16[32,32,768]{2,1,0:T(8,128)(2,1)}), bf16[32,32,768]{2,1,0:T(8,128)(2,1)}, u32[]{:S(2)}, u32[]{:S(2)}) %all-to-all-start.11) | async-done | bytes 1572896 | tf_op jit(solution)/shard_map/all_to_all | solution.py:42
  482.8 1.6 convert_reduce_fusion
  (76 shorter events, 7.1 us)
Async XLA Ops:
  7.2 226.8 %copy-start = (bf16[6144,256]{1,0:T(8,128)(2,1)S(1)}, bf16[6144,256]{1,0:T(8,128)(2,1)}, u32[]{:S(2)}) copy-start(bf16[6144,256]{1,0:T(8,128)(2,1)} %param.11) | copy-start | bytes 9437188
  8.8 9.8 %all-to-all-start = ((bf16[8,4,768]{2,1,0:T(4,128)(2,1)}), bf16[8,4,768]{2,1,0:T(4,128)(2,1)S(1)}, u32[]{:S(2)}, u32[]{:S(2)}) async-start(bf16[8,4,768]{2,1,0:T(4,128)(2,1)} %reshape_transpose_reshape_broadcast_in_dim.6), calls=%async_computation | async-start | bytes 98304 | tf_op jit(solution)/shard_map/all_to_all | solution.py:63
  21.4 54.0 %all-to-all-start.1 = ((bf16[32,32,768]{2,1,0:T(8,128)(2,1)}), bf16[32,32,768]{2,1,0:T(8,128)(2,1)}, u32[]{:S(2)}, u32[]{:S(2)}) async-start(bf16[32,32,768]{2,1,0:T(8,128)(2,1)} %broadcast_in_dim.14), calls=%async_computation.1 | async-start | bytes 3145728 | tf_op jit(solution)/shard_map/all_to_all | solution.py:35
  32.8 98.2 %all-gather.4.cloned.1.call-start = ((), (), s32[]{:S(2)}) async-start(), calls=%async_computation.16 | async-start | bytes 3244032 | tf_op jit(solution)/shard_map/all_gather | solution.py:102
  103.0 25.4 %copy-start.20 = (bf16[768,768]{1,0:T(8,128)(2,1)S(1)}, bf16[768,768]{1,0:T(8,128)(2,1)}, u32[]{:S(2)}) copy-start(bf16[768,768]{1,0:T(8,128)(2,1)} %param.10) | copy-start | bytes 3538948
  127.2 1.2 copy-start.3
  176.4 0.8 copy-start.13
  189.9 44.0 %all-to-all-start.6 = ((bf16[32,4,6144]{2,1,0:T(4,128)(2,1)}), bf16[32,4,6144]{2,1,0:T(4,128)(2,1)}, u32[]{:S(2)}, u32[]{:S(2)}) async-start(bf16[32,4,6144]{2,1,0:T(4,128)(2,1)} %broadcast_in_dim.18), calls=%async_computation.6 | async-start | bytes 3145728 | tf_op jit(solution)/shard_map/all_to_all | solution.py:122
  196.5 3.8 copy-start.17
  233.9 2.9 copy-start.2
  234.0 2.9 copy-start.5
  236.8 1.6 copy-start.16
  238.3 0.6 copy-start.15
  242.9 82.4 %all-to-all-start.7 = ((bf16[256,8,768]{2,1,0:T(8,128)(2,1)}), bf16[256,8,768]{2,1,0:T(8,128)(2,1)S(1)}, u32[]{:S(2)}, u32[]{:S(2)}) async-start(bf16[256,8,768]{2,1,0:T(8,128)(2,1)} %bitcast.20), calls=%async_computation.7 | async-start | bytes 6291456 | tf_op jit(solution)/shard_map/all_to_all | solution.py:148
  249.9 235.1 %reduce-scatter.5.cloned.1.call-start = ((), (), s32[]{:S(2)}) async-start(), calls=%async_computation.15 | async-start | bytes 3538944 | tf_op jit(solution)/shard_map/reduce_scatter | solution.py:173
  254.6 0.7 copy-start.19
  254.6 0.7 copy-start.18
  325.3 0.9 copy-start.8
  326.2 2.3 copy-start.14
  328.6 0.6 copy-start.9
  329.4 45.0 %copy-start.21 = (bf16[768,768]{1,0:T(8,128)(2,1)S(1)}, bf16[768,768]{1,0:T(8,128)(2,1)}, u32[]{:S(2)}) copy-start(bf16[768,768]{1,0:T(8,128)(2,1)} %param.10) | copy-start | bytes 3538948
  376.9 28.2 %all-to-all-start.9 = ((bf16[8,128,768]{2,1,0:T(8,128)(2,1)}), bf16[8,128,768]{2,1,0:T(8,128)(2,1)S(1)}, u32[]{:S(2)}, u32[]{:S(2)}) async-start(bf16[8,128,768]{2,1,0:T(8,128)(2,1)} %bitcast.81), calls=%async_computation.9 | async-start | bytes 3145728 | tf_op jit(solution)/shard_map/all_to_all | solution.py:42
  380.5 104.5 %reduce-scatter.3.cloned.1.call-start = ((), (), s32[]{:S(2)}) async-start(), calls=%async_computation.14 | async-start | bytes 3538944 | tf_op jit(solution)/shard_map/reduce_scatter | solution.py:170
  405.8 30.4 %copy-start.22 = (bf16[768,768]{1,0:T(8,128)(2,1)S(1)}, bf16[768,768]{1,0:T(8,128)(2,1)}, u32[]{:S(2)}) copy-start(bf16[768,768]{1,0:T(8,128)(2,1)} %param.9) | copy-start | bytes 3538948
  436.1 2.6 copy-start.6
  438.7 5.0 %copy-start.12 = (f32[8,4,768]{2,1,0:T(4,128)S(1)}, f32[8,4,768]{2,1,0:T(4,128)}, u32[]{:S(2)}) copy-start(f32[8,4,768]{2,1,0:T(4,128)} %get-tuple-element.13) | copy-start | bytes 294916
  438.7 5.0 %copy-start.11 = (bf16[32,768]{1,0:T(8,128)(2,1)S(1)}, bf16[32,768]{1,0:T(8,128)(2,1)}, u32[]{:S(2)}) copy-start(bf16[32,768]{1,0:T(8,128)(2,1)} %add_convert_fusion.3) | copy-start | bytes 147460
  438.7 5.7 %copy-start.4 = (bf16[8,128,768]{2,1,0:T(8,128)(2,1)S(1)}, bf16[8,128,768]{2,1,0:T(8,128)(2,1)}, u32[]{:S(2)}) copy-start(bf16[8,128,768]{2,1,0:T(8,128)(2,1)} %copy-done.3) | copy-start | bytes 4718596
  438.8 44.0 %all-to-all-start.11 = ((bf16[32,32,768]{2,1,0:T(8,128)(2,1)}), bf16[32,32,768]{2,1,0:T(8,128)(2,1)}, u32[]{:S(2)}, u32[]{:S(2)}) async-start(bf16[32,32,768]{2,1,0:T(8,128)(2,1)} %bitcast.84), calls=%async_computation.11 | async-start | bytes 3145728 | tf_op jit(solution)/shard_map/all_to_all | solution.py:42
  444.4 2.5 copy-start.7
  446.9 38.2 %copy-start.1 = (bf16[6144,256]{1,0:T(8,128)(2,1)S(1)}, bf16[6144,256]{1,0:T(8,128)(2,1)}, u32[]{:S(2)}) copy-start(bf16[6144,256]{1,0:T(8,128)(2,1)} %param.11) | copy-start | bytes 9437188
  450.9 33.5 %copy-start.10 = (bf16[32,768]{1,0:T(8,128)(2,1)S(1)}, bf16[32,768]{1,0:T(8,128)(2,1)}, u32[]{:S(2)}) copy-start(bf16[32,768]{1,0:T(8,128)(2,1)} %copy-done.9) | copy-start | bytes 147460
Sparse Core Ops, SparseCore 0:
  36.8 79.9 all-gather.3
  254.7 46.5 reduce-scatter.4
  385.2 50.9 reduce-scatter.2
